TPU v7x, 512 devices: a whole 4x8x8 slice. The times are simulated.
512 devices in a mesh: seq: 64 (over z_hi, y, core), ch: 8 (over x, z_lo).
Axes of the slice: x: 4, y: 8, z: 8 (z_hi: 4, z_lo: 2; z = z_hi * 2 + z_lo), core: 2. Of those that a mesh axis runs over, the one named last changes fastest.
Arguments:
- inputs: bfloat16 [262144, 2048], P('seq', 'ch'), may hold values from -6 to 6
- first_factor: bfloat16 [512, 512], P('ch'), may hold values from -0.25 to 0.25
- twiddle: float32 [512, 512], P('seq'), may hold values from -4 to 4
- second_factor: bfloat16 [512, 512], P('ch'), may hold values from -0.25 to 0.25
- block_first: bfloat16 [64, 32, 32], P('ch'), may hold values from -1 to 1
- block_second: bfloat16 [32, 64, 64], P('ch'), may hold values from -0.75 to 0.75
Outputs:
- mixed_out: bfloat16 [262144, 2048], P('seq', 'ch')
All inputs are finite; a program needn't handle non-finite values.
Results may differ from a plain program's by a relative error of at most 0.007.
Values may be sent and summed in bfloat16 or wider, within the bound.
No kernel may reach another device: no remote copies, remote signals or barrier semaphores. Data moves between devices by JAX's collectives and lax.ppermute only.
A program may use at most 128 MiB of HBM per device.

v0:
```python
import jax
import jax.numpy as jnp
from jax import lax
from jax.sharding import PartitionSpec as P

BLOCK = 512


def local(inputs, first_factor, twiddle, second_factor, block_first, block_second):
    tok_rows, channels = inputs.shape
    outer_rows = tok_rows // BLOCK
    token_grid = inputs.reshape(outer_rows, BLOCK, channels)
    contract = (((1,), (1,)), ((), ()))
    first = lax.dot_general(
        lax.all_gather(first_factor, "ch", axis=0, tiled=True),
        token_grid,
        contract,
        preferred_element_type=jnp.float32,
    )
    full_second = lax.all_gather(second_factor, "ch", axis=0, tiled=True)
    twisted = (first * jnp.transpose(twiddle)[:, :, None]).astype(jnp.bfloat16)
    mixed = lax.dot_general(
        full_second,
        lax.all_to_all(twisted, "seq", split_axis=0, concat_axis=1, tiled=True),
        contract,
        preferred_element_type=jnp.float32,
    )
    second = mixed.astype(jnp.bfloat16)
    returned = lax.all_to_all(second, "seq", split_axis=0, concat_axis=1, tiled=True)
    gated = (token_grid.astype(jnp.float32) * returned.astype(jnp.float32)).astype(jnp.bfloat16)
    grouped = gated.reshape(tok_rows, block_first.shape[0], block_first.shape[2])
    block_mix = jnp.einsum(
        "amb,tab->mat", block_first, grouped, preferred_element_type=jnp.float32
    ).astype(jnp.bfloat16)
    result_rows = jnp.einsum(
        "mpa,mat->tmp",
        block_second,
        lax.all_to_all(block_mix, "ch", split_axis=0, concat_axis=1, tiled=True),
        preferred_element_type=jnp.float32,
    )
    return result_rows.reshape(tok_rows, channels).astype(jnp.bfloat16)


def solution(mesh):
    placed = (
        P("seq", "ch"),
        P("ch", None),
        P("seq", None),
        P("ch", None),
        P("ch", None, None),
        P("ch", None, None),
    )
    return jax.shard_map(
        local, mesh=mesh, in_specs=placed, out_specs=P("seq", "ch"), check_vma=False
    )
```

profile of v0, /device:TPU:41, one launch (start us, length us, event | category | flops | bytes accessed | tf_op | source)
XLA Modules:
  0.0 266.0 jit_solution(8618646083847221918)
XLA Ops:
  0.0 0.0 copy-start
  0.0 25.3 %all_gather.6 = bf16[512,512]{1,0:T(8,128)(2,1)S(1)} all-gather(bf16[64,512]{1,0:T(8,128)(2,1)} %param.7), channel_id=1, replica_groups=mesh['seq'=64,'ch'=8] {'ch'}, dimensions={0}, use_global_device_ids=true | all-gather | bytes 589824 | tf_op jit(solution)/shard_map/all_gather | solution.py:15
  25.3 3.1 %multiply_convert_fusion = bf16[512,8,256]{2,0,1:T(8,128)(2,1)S(1)} fusion(bf16[8,512,256]{2,1,0:T(8,128)(2,1)} %bitcast.44, f32[512,8]{0,1:T(8,128)} %bitcast.46, bf16[512,512]{1,0:T(8,128)(2,1)S(1)} %all_gather.6), kind=kOutput, calls=%fused_computation.6 | convolution fusion | flops 1075838976 | bytes 4734976 | tf_op jit(solution)/shard_map/dot_general | solution.py:14
  28.4 2.5 copy.30
  30.9 0.0 copy-start.3
  30.9 21.6 %all-to-all-start = ((bf16[512,8,256]{2,1,0:T(8,128)(2,1)}), bf16[512,8,256]{2,1,0:T(8,128)(2,1)S(1)}, u32[]{:S(2)}, u32[]{:S(2)}) async-start(bf16[512,8,256]{2,1,0:T(8,128)(2,1)} %copy.30), calls=%async_computation | async-start | bytes 4194304 | tf_op jit(solution)/shard_map/all_to_all | solution.py:24
  52.5 0.0 copy-done.3
  52.5 64.1 %all_gather.7 = bf16[512,512]{1,0:T(8,128)(2,1)S(1)} all-gather(bf16[64,512]{1,0:T(8,128)(2,1)S(1)} %copy-done.3), channel_id=1, replica_groups=mesh['seq'=64,'ch'=8] {'ch'}, dimensions={0}, use_global_device_ids=true | all-gather | bytes 589824 | tf_op jit(solution)/shard_map/all_gather | solution.py:20
  116.6 0.0 all-to-all-done
  116.6 2.6 convert_bitcast_fusion.1
  119.2 4.5 %copy.33 = bf16[512,8,256]{2,1,0:T(8,128)(2,1)} copy(bf16[512,8,256]{0,2,1:T(8,128)(2,1)} %convert_bitcast_fusion.1) | data formatting | bytes 4194304 | tf_op jit(solution)/shard_map/convert_element_type | solution.py:28
  123.7 22.9 %all-to-all-start.1 = ((bf16[512,8,256]{2,1,0:T(8,128)(2,1)}), bf16[512,8,256]{2,1,0:T(8,128)(2,1)S(1)}, u32[]{:S(2)}, u32[]{:S(2)}) async-start(bf16[512,8,256]{2,1,0:T(8,128)(2,1)} %copy.33), calls=%async_computation.1 | async-start | bytes 4194304 | tf_op jit(solution)/shard_map/all_to_all | solution.py:29
  146.6 4.1 %copy.29 = bf16[4096,256]{0,1:T(8,128)(2,1)} copy(bf16[4096,256]{1,0:T(8,128)(2,1)} %param.6) | data formatting | bytes 4194304 | tf_op args[0]
  150.7 50.4 %all-to-all-done.1 = bf16[512,8,256]{2,1,0:T(8,128)(2,1)S(1)} async-done(((bf16[512,8,256]{2,1,0:T(8,128)(2,1)}), bf16[512,8,256]{2,1,0:T(8,128)(2,1)S(1)}, u32[]{:S(2)}, u32[]{:S(2)}) %all-to-all-start.1) | async-done | bytes 2097184 | tf_op jit(solution)/shard_map/all_to_all | solution.py:29
  201.1 0.5 convert_bitcast_fusion
  201.6 2.3 copy.34
  204.0 10.9 %reshape.17 = f32[4096,8,32]{2,1,0:T(8,128)} reshape(f32[8,64,8,256]{3,2,1,0:T(8,128)} %copy.34) | data formatting | bytes 8388608 | tf_op jit(solution)/shard_map/convert_element_type | solution.py:30
  214.9 0.0 copy-start.1
  214.9 11.6 %copy.35 = f32[4096,8,32]{0,2,1:T(8,128)} copy(f32[4096,8,32]{2,1,0:T(8,128)} %reshape.17) | data formatting | bytes 8388608 | tf_op jit(solution)/shard_map/convert_element_type | solution.py:30
  226.4 0.0 copy-done
  226.4 0.0 copy-done.1
  226.4 2.9 %fusion = bf16[32,8,4096]{2,0,1:T(8,128)(2,1)S(1)} fusion(bf16[8,32,32]{2,1,0:T(8,128)(2,1)S(1)} %copy-done, f32[4096,8,32]{0,2,1:T(8,128)} %copy.35, bf16[4096,8,32]{0,2,1:T(8,128)(2,1)S(1)} %bitcast.43), kind=kOutput, calls=%fused_computation.2 | convolution fusion | flops 71303168 | bytes 8404992 | tf_op jit(solution)/shard_map/amb,tab->mat/dot_general | solution.py:32
  229.3 1.2 copy.36
  230.5 0.0 copy-start.2
  230.5 32.3 %all_to_all.45 = bf16[32,8,4096]{2,1,0:T(8,128)(2,1)S(1)} all-to-all(bf16[32,8,4096]{2,1,0:T(8,128)(2,1)S(1)} %copy.36), channel_id=1, replica_groups=mesh['seq'=64,'ch'=8] {'ch'}, dimensions={0} | all-to-all | bytes 4194304 | tf_op jit(solution)/shard_map/all_to_all | solution.py:38
  262.8 0.0 copy-done.2
  262.8 0.7 convolution_convert_fusion
  263.5 2.5 copy.38
Async XLA Ops:
  0.0 226.4 %copy-start = (bf16[8,32,32]{2,1,0:T(8,128)(2,1)S(1)}, bf16[8,32,32]{2,1,0:T(8,128)(2,1)}, u32[]{:S(2)}) copy-start(bf16[8,32,32]{2,1,0:T(8,128)(2,1)} %param.10) | copy-start | bytes 49156
  30.9 21.6 %copy-start.3 = (bf16[64,512]{1,0:T(8,128)(2,1)S(1)}, bf16[64,512]{1,0:T(8,128)(2,1)}, u32[]{:S(2)}) copy-start(bf16[64,512]{1,0:T(8,128)(2,1)} %param.9) | copy-start | bytes 196612
  30.9 85.7 %all-to-all-start = ((bf16[512,8,256]{2,1,0:T(8,128)(2,1)}), bf16[512,8,256]{2,1,0:T(8,128)(2,1)S(1)}, u32[]{:S(2)}, u32[]{:S(2)}) async-start(bf16[512,8,256]{2,1,0:T(8,128)(2,1)} %copy.30), calls=%async_computation | async-start | bytes 4194304 | tf_op jit(solution)/shard_map/all_to_all | solution.py:24
  123.7 77.4 %all-to-all-start.1 = ((bf16[512,8,256]{2,1,0:T(8,128)(2,1)}), bf16[512,8,256]{2,1,0:T(8,128)(2,1)S(1)}, u32[]{:S(2)}, u32[]{:S(2)}) async-start(bf16[512,8,256]{2,1,0:T(8,128)(2,1)} %copy.33), calls=%async_computation.1 | async-start | bytes 4194304 | tf_op jit(solution)/shard_map/all_to_all | solution.py:29
  214.9 11.6 %copy-start.1 = (bf16[4096,256]{0,1:T(8,128)(2,1)S(1)}, bf16[4096,256]{0,1:T(8,128)(2,1)}, u32[]{:S(2)}) copy-start(bf16[4096,256]{0,1:T(8,128)(2,1)} %copy.29) | copy-start | bytes 6291460
  230.5 32.4 %copy-start.2 = (bf16[4,64,64]{2,1,0:T(8,128)(2,1)S(1)}, bf16[4,64,64]{2,1,0:T(8,128)(2,1)}, u32[]{:S(2)}) copy-start(bf16[4,64,64]{2,1,0:T(8,128)(2,1)} %param.11) | copy-start | bytes 98308
where the time goes:
time: 267 us; the launch traced here: 266 us
  blocking collectives  122 us (46%)
  waiting for transfers between devices  50.4 us (19%)
  starting transfers between devices  44.5 us (17%)
  local copies, waits for them, and re-layouts  39.5 us (15%)
  matrix products  9.27 us (3%)
    all_gather x1, blocking collectives, local(): full_second = lax.all_gather(second_factor, 'ch', axis=0, tiled=True)  64.1 us
    all_to_all x1, waiting for transfers between devices, local(): lax.all_to_all(second, 'seq', split_axis=0, concat_axis=1, tiled=True)  50.4 us
    all_to_all x1, blocking collectives, local(): lax.all_to_all(block_mix, 'ch', split_axis=0, concat_axis=1, tiled=True)  32.3 us
    all_gather x1, blocking collectives, local(): lax.all_gather(first_factor, 'ch', axis=0, tiled=True)  25.3 us
    convert_element_type x3, local copies, waits for them, and re-layouts, local(): returned.astype(jnp.float32)  24.8 us
    all_to_all x1, starting transfers between devices, local(): lax.all_to_all(second, 'seq', split_axis=0, concat_axis=1, tiled=True)  22.9 us
    all_to_all x1, starting transfers between devices, local(): lax.all_to_all(twisted, 'seq', split_axis=0, concat_axis=1, tiled=True)  21.6 us
  transfers between devices with their start and end apart: 2, of which 1 were waited for; matrix products, arithmetic and copies ran while one was open for 2% of the time, Pallas kernels for 0%

commit v1 on v0

v1 whole, which is shorter than its diff:
```python
import jax
import jax.numpy as jnp
from jax import lax
from jax.sharding import PartitionSpec as P

BLOCK = 512
CHUNKS = 2


def channel_weights(block_first, block_second, n_ch):
    n_a, n_m, n_b = block_first.shape
    m_l = n_m // n_ch
    bf = jnp.transpose(block_first, (1, 0, 2))
    bf = bf.reshape(n_ch, m_l, n_a, 1, n_b)
    eye_a = jnp.eye(n_a, dtype=jnp.bool_).reshape(1, 1, n_a, n_a, 1)
    w1t = jnp.where(eye_a, bf, jnp.zeros((), bf.dtype))
    w1t = w1t.reshape(n_ch * m_l * n_a, n_a * n_b)
    n_m2, n_p, n_a2 = block_second.shape
    a_l = n_a2 // n_ch
    bs = block_second.reshape(n_m2, n_p, n_ch, a_l)
    bs = jnp.transpose(bs, (2, 0, 3, 1))
    bs = bs.reshape(n_ch, n_m2, a_l, 1, n_p)
    eye_m = jnp.eye(n_m2, dtype=jnp.bool_).reshape(1, n_m2, 1, n_m2, 1)
    w2 = jnp.where(eye_m, bs, jnp.zeros((), bs.dtype))
    w2 = w2.reshape(n_ch * n_m2 * a_l, n_m2 * n_p)
    return w1t, w2


def make_local(n_seq, n_ch):
    def local(inputs, first_factor, twiddle, second_factor, block_first, block_second):
        tok_rows, channels = inputs.shape
        outer_rows = tok_rows // BLOCK
        token_grid = inputs.reshape(outer_rows, BLOCK, channels)
        rows = first_factor.shape[0]
        both = lax.all_gather(
            jnp.concatenate([first_factor, second_factor], axis=0), "ch", axis=0, tiled=True
        ).reshape(n_ch, 2, rows, BLOCK)
        full_first = both[:, 0].reshape(BLOCK, BLOCK)
        full_second = both[:, 1].reshape(BLOCK, BLOCK)
        twiddle_t = jnp.transpose(twiddle)
        w1t, w2 = channel_weights(block_first, block_second, n_ch)
        contract = (((1,), (1,)), ((), ()))
        width = BLOCK // CHUNKS
        outs = []
        for q in range(CHUNKS):
            lo = q * width
            first = lax.dot_general(
                full_first[lo:lo + width],
                token_grid,
                contract,
                preferred_element_type=jnp.float32,
            )
            twisted = (first * twiddle_t[lo:lo + width, :, None]).astype(jnp.bfloat16)
            gathered = lax.all_to_all(twisted, "seq", split_axis=0, concat_axis=1, tiled=True)
            mixed = lax.dot_general(
                full_second, gathered, contract, preferred_element_type=jnp.float32
            ).astype(jnp.bfloat16)
            returned = lax.all_to_all(mixed, "seq", split_axis=0, concat_axis=1, tiled=True)
            gated = (
                token_grid[:, lo:lo + width].astype(jnp.float32) * returned.astype(jnp.float32)
            ).astype(jnp.bfloat16)
            gated = gated.reshape(outer_rows * width, channels)
            middle_t = lax.dot_general(
                w1t, gated, contract, preferred_element_type=jnp.float32
            ).astype(jnp.bfloat16)
            middle_t = middle_t.reshape(n_ch, channels // n_ch, outer_rows * width)
            recv = lax.all_to_all(middle_t, "ch", split_axis=0, concat_axis=0, tiled=True)
            recv = recv.reshape(channels, outer_rows * width)
            result = lax.dot_general(
                recv, w2, (((0,), (0,)), ((), ())), preferred_element_type=jnp.float32
            ).astype(jnp.bfloat16)
            outs.append(result.reshape(outer_rows, width, channels))
        out = jnp.concatenate(outs, axis=1)
        return out.reshape(tok_rows, channels)

    return local


def solution(mesh):
    placed = (
        P("seq", "ch"),
        P("ch", None),
        P("seq", None),
        P("ch", None),
        P("ch", None, None),
        P("ch", None, None),
    )
    return jax.shard_map(
        make_local(mesh.shape["seq"], mesh.shape["ch"]),
        mesh=mesh,
        in_specs=placed,
        out_specs=P("seq", "ch"),
        check_vma=False,
    )
```

time: 267 us -> 276 us (1.034)
  the two profiles are of different devices: /device:TPU:41 before, /device:TPU:24 now
where the time goes in v1:
time: 276 us; the launch traced here: 275 us
  waiting for transfers between devices  183 us (66%)
  starting transfers between devices  47.9 us (17%)
  local copies, waits for them, and re-layouts  14.3 us (5%)
  between operations  13.7 us (5%)
  matrix products  8.32 us (3%)
  other arithmetic  7.35 us (3%)
    all_gather x1, waiting for transfers between devices, local(): lax.all_gather(jnp.concatenate([first_factor, second_factor], axis=0), 'c...  51.1 us
    all_to_all x2, waiting for transfers between devices, local(): lax.all_to_all(mixed, 'seq', split_axis=0, concat_axis=1, tiled=True)  51 us
    all_to_all x2, waiting for transfers between devices, local(): lax.all_to_all(twisted, 'seq', split_axis=0, concat_axis=1, tiled=True)  50.8 us
    all_to_all x2, waiting for transfers between devices, local(): lax.all_to_all(middle_t, 'ch', split_axis=0, concat_axis=0, tiled=True)  30.6 us
    all_to_all x2, starting transfers between devices, local(): lax.all_to_all(twisted, 'seq', split_axis=0, concat_axis=1, tiled=True)  20.9 us
    all_to_all x2, starting transfers between devices, local(): lax.all_to_all(mixed, 'seq', split_axis=0, concat_axis=1, tiled=True)  18.2 us
    all_to_all x2, starting transfers between devices, local(): lax.all_to_all(middle_t, 'ch', split_axis=0, concat_axis=0, tiled=True)  8.74 us
  transfers between devices with their start and end apart: 7, of which 7 were waited for; matrix products, arithmetic and copies ran while one was open for 5% of the time, Pallas kernels for 0%

profile of v1, /device:TPU:24, one launch (start us, length us, event | category | flops | bytes accessed | tf_op | source)
XLA Modules:
  0.0 274.9 jit_solution(7449750613190882592)
XLA Ops:
  6.5 0.0 all-gather.2.cloned.1.call-start
  6.5 1.5 pad_maximum_fusion.1
  8.1 0.0 all-gather.2.cloned.1.call-update
  8.1 0.7 fusion.5
  8.8 51.1 %all-gather.2.cloned.1.call-done = bf16[1024,512]{1,0:T(8,128)(2,1)} async-done(((bf16[128,512]{1,0:T(8,128)(2,1)}), bf16[1024,512]{1,0:T(8,128)(2,1)}) %all-gather.2.cloned.1.call-update) | async-done | bytes 1048592 | tf_op jit(solution)/shard_map/all_gather | solution.py:35
  59.9 1.1 fusion.4
  61.0 2.3 multiply_convert_fusion.3
  63.3 0.0 copy-start
  63.3 1.6 copy.29
  64.9 12.4 %all-to-all-start = ((bf16[256,8,256]{2,1,0:T(8,128)(2,1)}), bf16[256,8,256]{2,1,0:T(8,128)(2,1)S(1)}, u32[]{:S(2)}, u32[]{:S(2)}) async-start(bf16[256,8,256]{2,1,0:T(8,128)(2,1)} %copy.29), calls=%async_computation | async-start | bytes 2097152 | tf_op jit(solution)/shard_map/all_to_all | solution.py:54
  77.3 0.0 copy-done
  77.3 0.7 multiply_convert_fusion.1
  78.0 1.6 copy.36
  79.6 25.8 %all-to-all-done = bf16[256,8,256]{2,1,0:T(8,128)(2,1)S(1)} async-done(((bf16[256,8,256]{2,1,0:T(8,128)(2,1)}), bf16[256,8,256]{2,1,0:T(8,128)(2,1)S(1)}, u32[]{:S(2)}, u32[]{:S(2)}) %all-to-all-start) | async-done | bytes 1048608 | tf_op jit(solution)/shard_map/all_to_all | solution.py:54
  105.4 8.5 %all-to-all-start.3 = ((bf16[256,8,256]{2,1,0:T(8,128)(2,1)}), bf16[256,8,256]{2,1,0:T(8,128)(2,1)S(1)}, u32[]{:S(2)}, u32[]{:S(2)}) async-start(bf16[256,8,256]{2,1,0:T(8,128)(2,1)} %copy.36), calls=%async_computation.3 | async-start | bytes 2097152 | tf_op jit(solution)/shard_map/all_to_all | solution.py:54
  113.9 0.8 copy-done.2
  114.7 0.7 convolution_convert_fusion.5
  115.5 1.8 copy.31
  117.2 25.0 %all-to-all-done.3 = bf16[256,8,256]{2,1,0:T(8,128)(2,1)S(1)} async-done(((bf16[256,8,256]{2,1,0:T(8,128)(2,1)}), bf16[256,8,256]{2,1,0:T(8,128)(2,1)S(1)}, u32[]{:S(2)}, u32[]{:S(2)}) %all-to-all-start.3) | async-done | bytes 1048608 | tf_op jit(solution)/shard_map/all_to_all | solution.py:54
  142.2 9.0 %all-to-all-start.1 = ((bf16[512,4,256]{2,1,0:T(4,128)(2,1)}), bf16[512,4,256]{2,1,0:T(4,128)(2,1)S(1)}, u32[]{:S(2)}, u32[]{:S(2)}) async-start(bf16[512,4,256]{2,1,0:T(4,128)(2,1)} %copy.31), calls=%async_computation.1 | async-start | bytes 2097152 | tf_op jit(solution)/shard_map/all_to_all | solution.py:58
  151.2 0.7 convolution_convert_fusion.4
  151.9 0.0 copy-start.4
  151.9 1.8 copy.38
  153.8 25.7 %all-to-all-done.1 = bf16[512,4,256]{2,1,0:T(4,128)(2,1)S(1)} async-done(((bf16[512,4,256]{2,1,0:T(4,128)(2,1)}), bf16[512,4,256]{2,1,0:T(4,128)(2,1)S(1)}, u32[]{:S(2)}, u32[]{:S(2)}) %all-to-all-start.1) | async-done | bytes 1048608 | tf_op jit(solution)/shard_map/all_to_all | solution.py:58
  179.5 9.3 %all-to-all-start.4 = ((bf16[512,4,256]{2,1,0:T(4,128)(2,1)}), bf16[512,4,256]{2,1,0:T(4,128)(2,1)S(1)}, u32[]{:S(2)}, u32[]{:S(2)}) async-start(bf16[512,4,256]{2,1,0:T(4,128)(2,1)} %copy.38), calls=%async_computation.4 | async-start | bytes 2097152 | tf_op jit(solution)/shard_map/all_to_all | solution.py:58
  188.8 0.1 broadcast_select_fusion
  188.9 0.4 select_n.37
  189.3 0.3 convert_bitcast_fusion.1
  189.6 0.4 copy.32
  190.0 1.7 reshape.114
  191.7 25.3 %all-to-all-done.4 = bf16[512,4,256]{2,1,0:T(4,128)(2,1)S(1)} async-done(((bf16[512,4,256]{2,1,0:T(4,128)(2,1)}), bf16[512,4,256]{2,1,0:T(4,128)(2,1)S(1)}, u32[]{:S(2)}, u32[]{:S(2)}) %all-to-all-start.4) | async-done | bytes 1048608 | tf_op jit(solution)/shard_map/all_to_all | solution.py:58
  217.0 0.3 convert_bitcast_fusion
  217.3 0.4 copy.39
  217.7 1.7 reshape.115
  219.4 3.4 %multiply_convert_fusion.2 = (bf16[8,256,256]{2,1,0:T(8,128)(2,1)S(1)}, bf16[8,256,256]{2,1,0:T(8,128)(2,1)S(1)}) fusion(f32[8,256,256]{2,1,0:T(8,128)} %reshape.114, bf16[8,512,256]{2,1,0:T(8,128)(2,1)} %bitcast.81, f32[8,256,256]{2,1,0:T(8,128)} %reshape.115), kind=kLoop, calls=%fused_computation.9 | loop fusion | flops 3145728 | bytes 8388608 | tf_op jit(solution)/shard_map/convert_element_type | solution.py:61
  222.8 1.5 convolution_convert_fusion.3
  224.3 5.2 %all-to-all-start.2 = ((bf16[8,32,2048]{2,1,0:T(8,128)(2,1)}), bf16[8,32,2048]{2,1,0:T(8,128)(2,1)S(1)}, u32[]{:S(2)}, u32[]{:S(2)}) async-start(bf16[8,32,2048]{2,1,0:T(8,128)(2,1)} %bitcast.15), calls=%async_computation.2 | async-start | bytes 2097152 | tf_op jit(solution)/shard_map/all_to_all | solution.py:67
  229.5 1.4 convolution_convert_fusion.1
  230.9 15.0 %all-to-all-done.2 = bf16[8,32,2048]{2,1,0:T(8,128)(2,1)S(1)} async-done(((bf16[8,32,2048]{2,1,0:T(8,128)(2,1)}), bf16[8,32,2048]{2,1,0:T(8,128)(2,1)S(1)}, u32[]{:S(2)}, u32[]{:S(2)}) %all-to-all-start.2) | async-done | bytes 1048608 | tf_op jit(solution)/shard_map/all_to_all | solution.py:67
  245.9 3.6 %all-to-all-start.5 = ((bf16[8,32,2048]{2,1,0:T(8,128)(2,1)}), bf16[8,32,2048]{2,1,0:T(8,128)(2,1)S(1)}, u32[]{:S(2)}, u32[]{:S(2)}) async-start(bf16[8,32,2048]{2,1,0:T(8,128)(2,1)} %bitcast.29), calls=%async_computation.5 | async-start | bytes 2097152 | tf_op jit(solution)/shard_map/all_to_all | solution.py:67
  249.5 0.0 copy-done.5
  249.5 0.1 copy.33
  249.6 0.2 broadcast_select_fusion.1
  249.8 0.2 select_n.39
  250.0 0.5 convolution_convert_fusion.2
  250.5 15.6 %all-to-all-done.5 = bf16[8,32,2048]{2,1,0:T(8,128)(2,1)S(1)} async-done(((bf16[8,32,2048]{2,1,0:T(8,128)(2,1)}), bf16[8,32,2048]{2,1,0:T(8,128)(2,1)S(1)}, u32[]{:S(2)}, u32[]{:S(2)}) %all-to-all-start.5) | async-done | bytes 1048608 | tf_op jit(solution)/shard_map/all_to_all | solution.py:67
  266.1 0.5 convolution_convert_fusion
  266.6 1.5 pad_maximum_fusion
  (11 shorter events, 0.1 us)
Async XLA Ops:
  6.5 53.4 %all-gather.2.cloned.1.call-start = ((), (), s32[]{:S(2)}) async-start(), calls=%async_computation.6 | async-start | bytes 1179648 | tf_op jit(solution)/shard_map/all_gather | solution.py:35
  63.3 14.0 %copy-start = (bf16[4096,256]{1,0:T(8,128)(2,1)S(1)}, bf16[4096,256]{1,0:T(8,128)(2,1)}, u32[]{:S(2)}) copy-start(bf16[4096,256]{1,0:T(8,128)(2,1)} %param.6) | copy-start | bytes 6291460
  64.9 40.5 %all-to-all-start = ((bf16[256,8,256]{2,1,0:T(8,128)(2,1)}), bf16[256,8,256]{2,1,0:T(8,128)(2,1)S(1)}, u32[]{:S(2)}, u32[]{:S(2)}) async-start(bf16[256,8,256]{2,1,0:T(8,128)(2,1)} %copy.29), calls=%async_computation | async-start | bytes 2097152 | tf_op jit(solution)/shard_map/all_to_all | solution.py:54
  78.0 35.8 %copy-start.1 = (bf16[1024,512]{1,0:T(8,128)(2,1)S(1)}, bf16[1024,512]{1,0:T(8,128)(2,1)}, u32[]{:S(2)}) copy-start(bf16[1024,512]{1,0:T(8,128)(2,1)} %all-gather.2.cloned.1.call-done) | copy-start | bytes 3145732
  105.4 36.8 %all-to-all-start.3 = ((bf16[256,8,256]{2,1,0:T(8,128)(2,1)}), bf16[256,8,256]{2,1,0:T(8,128)(2,1)S(1)}, u32[]{:S(2)}, u32[]{:S(2)}) async-start(bf16[256,8,256]{2,1,0:T(8,128)(2,1)} %copy.36), calls=%async_computation.3 | async-start | bytes 2097152 | tf_op jit(solution)/shard_map/all_to_all | solution.py:54
  113.9 0.8 copy-start.2
  115.4 35.8 %copy-start.3 = (bf16[8,1,64,512]{3,2,1,0:T(8,128)(2,1)S(1)}, bf16[8,1,64,512]{3,2,1,0:T(8,128)(2,1)}, u32[]{:S(2)}) copy-start(bf16[8,1,64,512]{3,2,1,0:T(8,128)(2,1)} %copy-done.2) | copy-start | bytes 1572868
  142.2 37.2 %all-to-all-start.1 = ((bf16[512,4,256]{2,1,0:T(4,128)(2,1)}), bf16[512,4,256]{2,1,0:T(4,128)(2,1)S(1)}, u32[]{:S(2)}, u32[]{:S(2)}) async-start(bf16[512,4,256]{2,1,0:T(4,128)(2,1)} %copy.31), calls=%async_computation.1 | async-start | bytes 2097152 | tf_op jit(solution)/shard_map/all_to_all | solution.py:58
  151.9 36.8 %copy-start.4 = (bf16[8,32,32]{2,1,0:T(8,128)(2,1)S(1)}, bf16[8,32,32]{2,1,0:T(8,128)(2,1)}, u32[]{:S(2)}) copy-start(bf16[8,32,32]{2,1,0:T(8,128)(2,1)} %param.10) | copy-start | bytes 49156
  179.5 37.5 %all-to-all-start.4 = ((bf16[512,4,256]{2,1,0:T(4,128)(2,1)}), bf16[512,4,256]{2,1,0:T(4,128)(2,1)S(1)}, u32[]{:S(2)}, u32[]{:S(2)}) async-start(bf16[512,4,256]{2,1,0:T(4,128)(2,1)} %copy.38), calls=%async_computation.4 | async-start | bytes 2097152 | tf_op jit(solution)/shard_map/all_to_all | solution.py:58
  224.3 21.6 %all-to-all-start.2 = ((bf16[8,32,2048]{2,1,0:T(8,128)(2,1)}), bf16[8,32,2048]{2,1,0:T(8,128)(2,1)S(1)}, u32[]{:S(2)}, u32[]{:S(2)}) async-start(bf16[8,32,2048]{2,1,0:T(8,128)(2,1)} %bitcast.15), calls=%async_computation.2 | async-start | bytes 2097152 | tf_op jit(solution)/shard_map/all_to_all | solution.py:67
  229.5 20.0 %copy-start.5 = (bf16[4,64,64]{2,1,0:T(8,128)(2,1)S(1)}, bf16[4,64,64]{2,1,0:T(8,128)(2,1)}, u32[]{:S(2)}) copy-start(bf16[4,64,64]{2,1,0:T(8,128)(2,1)} %param.11) | copy-start | bytes 98308
  245.9 20.2 %all-to-all-start.5 = ((bf16[8,32,2048]{2,1,0:T(8,128)(2,1)}), bf16[8,32,2048]{2,1,0:T(8,128)(2,1)S(1)}, u32[]{:S(2)}, u32[]{:S(2)}) async-start(bf16[8,32,2048]{2,1,0:T(8,128)(2,1)} %bitcast.29), calls=%async_computation.5 | async-start | bytes 2097152 | tf_op jit(solution)/shard_map/all_to_all | solution.py:67
Sparse Core Ops, SparseCore 0:
  9.4 50.4 all-gather.1

commit v2 on v1

--- a/solution.py
+++ b/solution.py
@@ -32,13 +32,26 @@
         outer_rows = tok_rows // BLOCK
         token_grid = inputs.reshape(outer_rows, BLOCK, channels)
         rows = first_factor.shape[0]
-        both = lax.all_gather(
-            jnp.concatenate([first_factor, second_factor], axis=0), "ch", axis=0, tiled=True
-        ).reshape(n_ch, 2, rows, BLOCK)
+        me = lax.axis_index("ch")
+        pair = jnp.concatenate([first_factor, second_factor], axis=0)
+        blocks = [pair]
+        for q in range(1, n_ch):
+            blocks.append(
+                lax.ppermute(pair, "ch", perm=[(j, (j + q) % n_ch) for j in range(n_ch)])
+            )
+        stacked = jnp.stack(blocks)
+        order = (me - jnp.arange(n_ch)) % n_ch
+        both = jnp.take(stacked, order, axis=0).reshape(n_ch, 2, rows, BLOCK)
         full_first = both[:, 0].reshape(BLOCK, BLOCK)
         full_second = both[:, 1].reshape(BLOCK, BLOCK)
         twiddle_t = jnp.transpose(twiddle)
         w1t, w2 = channel_weights(block_first, block_second, n_ch)
+        w1t = jnp.take(
+            w1t.reshape(n_ch, -1, channels), (me + jnp.arange(n_ch)) % n_ch, axis=0
+        ).reshape(channels, channels)
+        w2 = jnp.take(
+            w2.reshape(n_ch, -1, channels), (me - jnp.arange(n_ch)) % n_ch, axis=0
+        ).reshape(channels, channels)
         contract = (((1,), (1,)), ((), ()))
         width = BLOCK // CHUNKS
         outs = []
@@ -64,8 +77,14 @@
                 w1t, gated, contract, preferred_element_type=jnp.float32
             ).astype(jnp.bfloat16)
             middle_t = middle_t.reshape(n_ch, channels // n_ch, outer_rows * width)
-            recv = lax.all_to_all(middle_t, "ch", split_axis=0, concat_axis=0, tiled=True)
-            recv = recv.reshape(channels, outer_rows * width)
+            pieces = [middle_t[0]]
+            for s_ in range(1, n_ch):
+                pieces.append(
+                    lax.ppermute(
+                        middle_t[s_], "ch", perm=[(j, (j + s_) % n_ch) for j in range(n_ch)]
+                    )
+                )
+            recv = jnp.stack(pieces).reshape(channels, outer_rows * width)
             result = lax.dot_general(
                 recv, w2, (((0,), (0,)), ((), ())), preferred_element_type=jnp.float32
             ).astype(jnp.bfloat16)

time: 276 us -> 259 us (0.938)
  the two profiles are of different devices: /device:TPU:24 before, /device:TPU:4 now
where the time goes in v2:
time: 259 us; the launch traced here: 257 us
  starting transfers between devices  113 us (44%)
  waiting for transfers between devices  110 us (42%)
  local copies, waits for them, and re-layouts  19 us (7%)
  matrix products  8.51 us (3%)
  other arithmetic  5.84 us (2%)
    all_to_all x2, waiting for transfers between devices, local(): lax.all_to_all(twisted, 'seq', split_axis=0, concat_axis=1, tiled=True)  52.2 us
    all_to_all x2, waiting for transfers between devices, local(): lax.all_to_all(mixed, 'seq', split_axis=0, concat_axis=1, tiled=True)  51.7 us
    ppermute x14, starting transfers between devices, local(): lax.ppermute(middle_t[s_], 'ch', perm=[(j, (j + s_) % n_ch) for j in rang...  48.4 us
    ppermute x7, starting transfers between devices, local(): lax.ppermute(pair, 'ch', perm=[(j, (j + q) % n_ch) for j in range(n_ch)])  28.9 us
    all_to_all x2, starting transfers between devices, local(): lax.all_to_all(twisted, 'seq', split_axis=0, concat_axis=1, tiled=True)  20.4 us
    all_to_all x2, starting transfers between devices, local(): lax.all_to_all(mixed, 'seq', split_axis=0, concat_axis=1, tiled=True)  15.6 us
  transfers between devices with their start and end apart: 25, of which 7 were waited for; matrix products, arithmetic and copies ran while one was open for 7% of the time, Pallas kernels for 0%

profile of v2, /device:TPU:4, one launch (start us, length us, event | category | flops | bytes accessed | tf_op | source)
XLA Modules:
  0.0 257.3 jit_solution(6241435916504055776)
XLA Ops:
  0.0 0.8 constant_dynamic-update-slice_fusion.1
  0.8 0.8 constant_dynamic-update-slice_fusion
  1.7 4.3 %collective-permute-start = (bf16[128,512]{1,0:T(8,128)(2,1)S(1)}, bf16[128,512]{1,0:T(8,128)(2,1)S(1)}, u32[]{:S(2)}, u32[]{:S(2)}) collective-permute-start(bf16[128,512]{1,0:T(8,128)(2,1)S(1)} %constant_dynamic-update-slice_fusion), channel_id=1, source_target_pairs={{0,1},{1,2},{2,3},{3,4},{4,5},{5,6},{6,7},{7,0},{8,9},{9,10},{10,1... | collective-permute-start | bytes 393224 | tf_op jit(solution)/shard_map/ppermute | solution.py:40
  6.0 3.1 %collective-permute-start.1 = (bf16[128,512]{1,0:T(8,128)(2,1)S(1)}, bf16[128,512]{1,0:T(8,128)(2,1)S(1)}, u32[]{:S(2)}, u32[]{:S(2)}) collective-permute-start(bf16[128,512]{1,0:T(8,128)(2,1)S(1)} %constant_dynamic-update-slice_fusion), channel_id=1, source_target_pairs={{0,2},{1,3},{2,4},{3,5},{4,6},{5,7},{6,0},{7,1},{8,10},{9,11},{10,... | collective-permute-start | bytes 393224 | tf_op jit(solution)/shard_map/ppermute | solution.py:40
  9.1 6.3 %collective-permute-start.2 = (bf16[128,512]{1,0:T(8,128)(2,1)S(1)}, bf16[128,512]{1,0:T(8,128)(2,1)S(1)}, u32[]{:S(2)}, u32[]{:S(2)}) collective-permute-start(bf16[128,512]{1,0:T(8,128)(2,1)S(1)} %constant_dynamic-update-slice_fusion), channel_id=1, source_target_pairs={{0,3},{1,4},{2,5},{3,6},{4,7},{5,0},{6,1},{7,2},{8,11},{9,12},{10,... | collective-permute-start | bytes 393224 | tf_op jit(solution)/shard_map/ppermute | solution.py:40
  15.4 1.9 collective-permute-start.3
  17.3 5.4 %collective-permute-start.4 = (bf16[128,512]{1,0:T(8,128)(2,1)S(1)}, bf16[128,512]{1,0:T(8,128)(2,1)S(1)}, u32[]{:S(2)}, u32[]{:S(2)}) collective-permute-start(bf16[128,512]{1,0:T(8,128)(2,1)S(1)} %constant_dynamic-update-slice_fusion), channel_id=1, source_target_pairs={{0,5},{1,6},{2,7},{3,0},{4,1},{5,2},{6,3},{7,4},{8,13},{9,14},{10,... | collective-permute-start | bytes 393224 | tf_op jit(solution)/shard_map/ppermute | solution.py:40
  22.8 0.7 fusion.17
  23.5 3.4 %collective-permute-start.5 = (bf16[128,512]{1,0:T(8,128)(2,1)S(1)}, bf16[128,512]{1,0:T(8,128)(2,1)S(1)}, u32[]{:S(2)}, u32[]{:S(2)}) collective-permute-start(bf16[128,512]{1,0:T(8,128)(2,1)S(1)} %constant_dynamic-update-slice_fusion), channel_id=1, source_target_pairs={{0,6},{1,7},{2,0},{3,1},{4,2},{5,3},{6,4},{7,5},{8,14},{9,15},{10,... | collective-permute-start | bytes 393224 | tf_op jit(solution)/shard_map/ppermute | solution.py:40
  26.9 4.5 %collective-permute-start.6 = (bf16[128,512]{1,0:T(8,128)(2,1)S(1)}, bf16[128,512]{1,0:T(8,128)(2,1)S(1)}, u32[]{:S(2)}, u32[]{:S(2)}) collective-permute-start(bf16[128,512]{1,0:T(8,128)(2,1)S(1)} %constant_dynamic-update-slice_fusion), channel_id=1, source_target_pairs={{0,7},{1,0},{2,1},{3,2},{4,3},{5,4},{6,5},{7,6},{8,15},{9,8},{10,9... | collective-permute-start | bytes 393224 | tf_op jit(solution)/shard_map/ppermute | solution.py:40
  31.6 2.4 collective-permute-done.6
  34.8 1.4 copy-done
  36.2 0.7 multiply_convert_fusion.1
  36.9 1.6 copy.30
  38.5 12.5 %all-to-all-start.2 = ((bf16[256,8,256]{2,1,0:T(8,128)(2,1)}), bf16[256,8,256]{2,1,0:T(8,128)(2,1)S(1)}, u32[]{:S(2)}, u32[]{:S(2)}) async-start(bf16[256,8,256]{2,1,0:T(8,128)(2,1)} %copy.30), calls=%async_computation.2 | async-start | bytes 2097152 | tf_op jit(solution)/shard_map/all_to_all | solution.py:67
  51.0 2.3 multiply_convert_fusion.3
  53.3 1.6 copy.24
  54.9 26.4 %all-to-all-done.2 = bf16[256,8,256]{2,1,0:T(8,128)(2,1)S(1)} async-done(((bf16[256,8,256]{2,1,0:T(8,128)(2,1)}), bf16[256,8,256]{2,1,0:T(8,128)(2,1)S(1)}, u32[]{:S(2)}, u32[]{:S(2)}) %all-to-all-start.2) | async-done | bytes 1048608 | tf_op jit(solution)/shard_map/all_to_all | solution.py:67
  81.3 7.8 %all-to-all-start = ((bf16[256,8,256]{2,1,0:T(8,128)(2,1)}), bf16[256,8,256]{2,1,0:T(8,128)(2,1)S(1)}, u32[]{:S(2)}, u32[]{:S(2)}) async-start(bf16[256,8,256]{2,1,0:T(8,128)(2,1)} %copy.24), calls=%async_computation | async-start | bytes 2097152 | tf_op jit(solution)/shard_map/all_to_all | solution.py:67
  89.1 0.9 slice.132
  90.0 1.8 convolution_convert_fusion.2
  91.7 1.8 copy.32
  93.5 25.9 %all-to-all-done = bf16[256,8,256]{2,1,0:T(8,128)(2,1)S(1)} async-done(((bf16[256,8,256]{2,1,0:T(8,128)(2,1)}), bf16[256,8,256]{2,1,0:T(8,128)(2,1)S(1)}, u32[]{:S(2)}, u32[]{:S(2)}) %all-to-all-start) | async-done | bytes 1048608 | tf_op jit(solution)/shard_map/all_to_all | solution.py:67
  119.4 7.8 %all-to-all-start.3 = ((bf16[512,4,256]{2,1,0:T(4,128)(2,1)}), bf16[512,4,256]{2,1,0:T(4,128)(2,1)S(1)}, u32[]{:S(2)}, u32[]{:S(2)}) async-start(bf16[512,4,256]{2,1,0:T(4,128)(2,1)} %copy.32), calls=%async_computation.3 | async-start | bytes 2097152 | tf_op jit(solution)/shard_map/all_to_all | solution.py:71
  127.1 1.8 convolution_convert_fusion.3
  128.9 1.8 copy.26
  130.7 26.7 %all-to-all-done.3 = bf16[512,4,256]{2,1,0:T(4,128)(2,1)S(1)} async-done(((bf16[512,4,256]{2,1,0:T(4,128)(2,1)}), bf16[512,4,256]{2,1,0:T(4,128)(2,1)S(1)}, u32[]{:S(2)}, u32[]{:S(2)}) %all-to-all-start.3) | async-done | bytes 1048608 | tf_op jit(solution)/shard_map/all_to_all | solution.py:71
  157.4 7.9 %all-to-all-start.1 = ((bf16[512,4,256]{2,1,0:T(4,128)(2,1)}), bf16[512,4,256]{2,1,0:T(4,128)(2,1)S(1)}, u32[]{:S(2)}, u32[]{:S(2)}) async-start(bf16[512,4,256]{2,1,0:T(4,128)(2,1)} %copy.26), calls=%async_computation.1 | async-start | bytes 2097152 | tf_op jit(solution)/shard_map/all_to_all | solution.py:71
  168.7 1.7 reshape.165
  170.5 25.0 %all-to-all-done.1 = bf16[512,4,256]{2,1,0:T(4,128)(2,1)S(1)} async-done(((bf16[512,4,256]{2,1,0:T(4,128)(2,1)}), bf16[512,4,256]{2,1,0:T(4,128)(2,1)S(1)}, u32[]{:S(2)}, u32[]{:S(2)}) %all-to-all-start.1) | async-done | bytes 1048608 | tf_op jit(solution)/shard_map/all_to_all | solution.py:71
  196.1 1.7 reshape.164
  197.9 3.4 %multiply_convert_fusion.2 = (bf16[8,256,256]{2,1,0:T(8,128)(2,1)S(1)}, bf16[8,256,256]{2,1,0:T(8,128)(2,1)S(1)}) fusion(f32[8,256,256]{2,1,0:T(8,128)} %reshape.164, bf16[8,512,256]{2,1,0:T(8,128)(2,1)} %bitcast.128, f32[8,256,256]{2,1,0:T(8,128)} %reshape.165), kind=kLoop, calls=%fused_computation.14 | loop fusion | flops 3145728 | bytes 8388608 | tf_op jit(solution)/shard_map/convert_element_type | solution.py:74
  201.9 3.1 %collective-permute-start.7 = (bf16[32,2048]{1,0:T(8,128)(2,1)S(1)}, bf16[32,2048]{1,0:T(8,128)(2,1)S(1)}, u32[]{:S(2)}, u32[]{:S(2)}) collective-permute-start(bf16[32,2048]{1,0:T(8,128)(2,1)S(1)} %get-tuple-element.14), channel_id=1, source_target_pairs={{0,1},{1,2},{2,3},{3,4},{4,5},{5,6},{6,7},{7,0},{8,9},{9,10},{10,1... | collective-permute-start | bytes 393224 | tf_op jit(solution)/shard_map/ppermute | solution.py:83
  205.5 3.6 %collective-permute-start.8 = (bf16[32,2048]{1,0:T(8,128)(2,1)S(1)}, bf16[32,2048]{1,0:T(8,128)(2,1)S(1)}, u32[]{:S(2)}, u32[]{:S(2)}) collective-permute-start(bf16[32,2048]{1,0:T(8,128)(2,1)S(1)} %get-tuple-element.13), channel_id=1, source_target_pairs={{0,2},{1,3},{2,4},{3,5},{4,6},{5,7},{6,0},{7,1},{8,10},{9,11},{10,... | collective-permute-start | bytes 393224 | tf_op jit(solution)/shard_map/ppermute | solution.py:83
  209.2 3.5 %collective-permute-start.9 = (bf16[32,2048]{1,0:T(8,128)(2,1)S(1)}, bf16[32,2048]{1,0:T(8,128)(2,1)S(1)}, u32[]{:S(2)}, u32[]{:S(2)}) collective-permute-start(bf16[32,2048]{1,0:T(8,128)(2,1)S(1)} %get-tuple-element.12), channel_id=1, source_target_pairs={{0,3},{1,4},{2,5},{3,6},{4,7},{5,0},{6,1},{7,2},{8,11},{9,12},{10,... | collective-permute-start | bytes 393224 | tf_op jit(solution)/shard_map/ppermute | solution.py:83
  212.7 3.5 %collective-permute-start.10 = (bf16[32,2048]{1,0:T(8,128)(2,1)S(1)}, bf16[32,2048]{1,0:T(8,128)(2,1)S(1)}, u32[]{:S(2)}, u32[]{:S(2)}) collective-permute-start(bf16[32,2048]{1,0:T(8,128)(2,1)S(1)} %get-tuple-element.11), channel_id=1, source_target_pairs={{0,4},{1,5},{2,6},{3,7},{4,0},{5,1},{6,2},{7,3},{8,12},{9,13},{10,... | collective-permute-start | bytes 393224 | tf_op jit(solution)/shard_map/ppermute | solution.py:83
  216.2 3.4 %collective-permute-start.11 = (bf16[32,2048]{1,0:T(8,128)(2,1)S(1)}, bf16[32,2048]{1,0:T(8,128)(2,1)S(1)}, u32[]{:S(2)}, u32[]{:S(2)}) collective-permute-start(bf16[32,2048]{1,0:T(8,128)(2,1)S(1)} %get-tuple-element.10), channel_id=1, source_target_pairs={{0,5},{1,6},{2,7},{3,0},{4,1},{5,2},{6,3},{7,4},{8,13},{9,14},{10,... | collective-permute-start | bytes 393224 | tf_op jit(solution)/shard_map/ppermute | solution.py:83
  219.7 3.3 %collective-permute-start.12 = (bf16[32,2048]{1,0:T(8,128)(2,1)S(1)}, bf16[32,2048]{1,0:T(8,128)(2,1)S(1)}, u32[]{:S(2)}, u32[]{:S(2)}) collective-permute-start(bf16[32,2048]{1,0:T(8,128)(2,1)S(1)} %get-tuple-element.9), channel_id=1, source_target_pairs={{0,6},{1,7},{2,0},{3,1},{4,2},{5,3},{6,4},{7,5},{8,14},{9,15},{10,... | collective-permute-start | bytes 393224 | tf_op jit(solution)/shard_map/ppermute | solution.py:83
  223.1 3.8 %collective-permute-start.13 = (bf16[32,2048]{1,0:T(8,128)(2,1)S(1)}, bf16[32,2048]{1,0:T(8,128)(2,1)S(1)}, u32[]{:S(2)}, u32[]{:S(2)}) collective-permute-start(bf16[32,2048]{1,0:T(8,128)(2,1)S(1)} %get-tuple-element.8), channel_id=1, source_target_pairs={{0,7},{1,0},{2,1},{3,2},{4,3},{5,4},{6,5},{7,6},{8,15},{9,8},{10,9... | collective-permute-start | bytes 393224 | tf_op jit(solution)/shard_map/ppermute | solution.py:83
  226.9 2.1 collective-permute-start.14
  229.0 2.5 collective-permute-start.15
  231.5 5.4 %collective-permute-start.16 = (bf16[32,2048]{1,0:T(8,128)(2,1)S(1)}, bf16[32,2048]{1,0:T(8,128)(2,1)S(1)}, u32[]{:S(2)}, u32[]{:S(2)}) collective-permute-start(bf16[32,2048]{1,0:T(8,128)(2,1)S(1)} %get-tuple-element.21), channel_id=1, source_target_pairs={{0,3},{1,4},{2,5},{3,6},{4,7},{5,0},{6,1},{7,2},{8,11},{9,12},{10,... | collective-permute-start | bytes 393224 | tf_op jit(solution)/shard_map/ppermute | solution.py:83
  237.0 2.6 %collective-permute-start.17 = (bf16[32,2048]{1,0:T(8,128)(2,1)S(1)}, bf16[32,2048]{1,0:T(8,128)(2,1)S(1)}, u32[]{:S(2)}, u32[]{:S(2)}) collective-permute-start(bf16[32,2048]{1,0:T(8,128)(2,1)S(1)} %get-tuple-element.20), channel_id=1, source_target_pairs={{0,4},{1,5},{2,6},{3,7},{4,0},{5,1},{6,2},{7,3},{8,12},{9,13},{10,... | collective-permute-start | bytes 393224 | tf_op jit(solution)/shard_map/ppermute | solution.py:83
  239.6 5.3 %collective-permute-start.18 = (bf16[32,2048]{1,0:T(8,128)(2,1)S(1)}, bf16[32,2048]{1,0:T(8,128)(2,1)S(1)}, u32[]{:S(2)}, u32[]{:S(2)}) collective-permute-start(bf16[32,2048]{1,0:T(8,128)(2,1)S(1)} %get-tuple-element.19), channel_id=1, source_target_pairs={{0,5},{1,6},{2,7},{3,0},{4,1},{5,2},{6,3},{7,4},{8,13},{9,14},{10,... | collective-permute-start | bytes 393224 | tf_op jit(solution)/shard_map/ppermute | solution.py:83
  245.0 3.4 %collective-permute-start.19 = (bf16[32,2048]{1,0:T(8,128)(2,1)S(1)}, bf16[32,2048]{1,0:T(8,128)(2,1)S(1)}, u32[]{:S(2)}, u32[]{:S(2)}) collective-permute-start(bf16[32,2048]{1,0:T(8,128)(2,1)S(1)} %get-tuple-element.18), channel_id=1, source_target_pairs={{0,6},{1,7},{2,0},{3,1},{4,2},{5,3},{6,4},{7,5},{8,14},{9,15},{10,... | collective-permute-start | bytes 393224 | tf_op jit(solution)/shard_map/ppermute | solution.py:83
  248.4 2.8 %collective-permute-start.20 = (bf16[32,2048]{1,0:T(8,128)(2,1)S(1)}, bf16[32,2048]{1,0:T(8,128)(2,1)S(1)}, u32[]{:S(2)}, u32[]{:S(2)}) collective-permute-start(bf16[32,2048]{1,0:T(8,128)(2,1)S(1)} %get-tuple-element.17), channel_id=1, source_target_pairs={{0,7},{1,0},{2,1},{3,2},{4,3},{5,4},{6,5},{7,6},{8,15},{9,8},{10,9... | collective-permute-start | bytes 393224 | tf_op jit(solution)/shard_map/ppermute | solution.py:83
  252.4 2.9 %collective-permute-done.20 = bf16[32,2048]{1,0:T(8,128)(2,1)S(1)} collective-permute-done((bf16[32,2048]{1,0:T(8,128)(2,1)S(1)}, bf16[32,2048]{1,0:T(8,128)(2,1)S(1)}, u32[]{:S(2)}, u32[]{:S(2)}) %collective-permute-start.20) | collective-permute-done | bytes 131104 | tf_op jit(solution)/shard_map/ppermute | solution.py:83
  255.8 1.5 pad_maximum_fusion
  (85 shorter events, 7.7 us)
Async XLA Ops:
  1.7 21.8 %collective-permute-start = (bf16[128,512]{1,0:T(8,128)(2,1)S(1)}, bf16[128,512]{1,0:T(8,128)(2,1)S(1)}, u32[]{:S(2)}, u32[]{:S(2)}) collective-permute-start(bf16[128,512]{1,0:T(8,128)(2,1)S(1)} %constant_dynamic-update-slice_fusion), channel_id=1, source_target_pairs={{0,1},{1,2},{2,3},{3,4},{4,5},{5,6},{6,7},{7,0},{8,9},{9,10},{10,1... | collective-permute-start | bytes 393224 | tf_op jit(solution)/shard_map/ppermute | solution.py:40
  6.0 21.0 %collective-permute-start.1 = (bf16[128,512]{1,0:T(8,128)(2,1)S(1)}, bf16[128,512]{1,0:T(8,128)(2,1)S(1)}, u32[]{:S(2)}, u32[]{:S(2)}) collective-permute-start(bf16[128,512]{1,0:T(8,128)(2,1)S(1)} %constant_dynamic-update-slice_fusion), channel_id=1, source_target_pairs={{0,2},{1,3},{2,4},{3,5},{4,6},{5,7},{6,0},{7,1},{8,10},{9,11},{10,... | collective-permute-start | bytes 393224 | tf_op jit(solution)/shard_map/ppermute | solution.py:40
  9.1 22.4 %collective-permute-start.2 = (bf16[128,512]{1,0:T(8,128)(2,1)S(1)}, bf16[128,512]{1,0:T(8,128)(2,1)S(1)}, u32[]{:S(2)}, u32[]{:S(2)}) collective-permute-start(bf16[128,512]{1,0:T(8,128)(2,1)S(1)} %constant_dynamic-update-slice_fusion), channel_id=1, source_target_pairs={{0,3},{1,4},{2,5},{3,6},{4,7},{5,0},{6,1},{7,2},{8,11},{9,12},{10,... | collective-permute-start | bytes 393224 | tf_op jit(solution)/shard_map/ppermute | solution.py:40
  15.4 16.2 %collective-permute-start.3 = (bf16[128,512]{1,0:T(8,128)(2,1)S(1)}, bf16[128,512]{1,0:T(8,128)(2,1)S(1)}, u32[]{:S(2)}, u32[]{:S(2)}) collective-permute-start(bf16[128,512]{1,0:T(8,128)(2,1)S(1)} %constant_dynamic-update-slice_fusion), channel_id=1, source_target_pairs={{0,4},{1,5},{2,6},{3,7},{4,0},{5,1},{6,2},{7,3},{8,12},{9,13},{10,... | collective-permute-start | bytes 393224 | tf_op jit(solution)/shard_map/ppermute | solution.py:40
  17.3 14.3 %collective-permute-start.4 = (bf16[128,512]{1,0:T(8,128)(2,1)S(1)}, bf16[128,512]{1,0:T(8,128)(2,1)S(1)}, u32[]{:S(2)}, u32[]{:S(2)}) collective-permute-start(bf16[128,512]{1,0:T(8,128)(2,1)S(1)} %constant_dynamic-update-slice_fusion), channel_id=1, source_target_pairs={{0,5},{1,6},{2,7},{3,0},{4,1},{5,2},{6,3},{7,4},{8,13},{9,14},{10,... | collective-permute-start | bytes 393224 | tf_op jit(solution)/shard_map/ppermute | solution.py:40
  23.5 8.1 %collective-permute-start.5 = (bf16[128,512]{1,0:T(8,128)(2,1)S(1)}, bf16[128,512]{1,0:T(8,128)(2,1)S(1)}, u32[]{:S(2)}, u32[]{:S(2)}) collective-permute-start(bf16[128,512]{1,0:T(8,128)(2,1)S(1)} %constant_dynamic-update-slice_fusion), channel_id=1, source_target_pairs={{0,6},{1,7},{2,0},{3,1},{4,2},{5,3},{6,4},{7,5},{8,14},{9,15},{10,... | collective-permute-start | bytes 393224 | tf_op jit(solution)/shard_map/ppermute | solution.py:40
  26.9 7.0 %collective-permute-start.6 = (bf16[128,512]{1,0:T(8,128)(2,1)S(1)}, bf16[128,512]{1,0:T(8,128)(2,1)S(1)}, u32[]{:S(2)}, u32[]{:S(2)}) collective-permute-start(bf16[128,512]{1,0:T(8,128)(2,1)S(1)} %constant_dynamic-update-slice_fusion), channel_id=1, source_target_pairs={{0,7},{1,0},{2,1},{3,2},{4,3},{5,4},{6,5},{7,6},{8,15},{9,8},{10,9... | collective-permute-start | bytes 393224 | tf_op jit(solution)/shard_map/ppermute | solution.py:40
  34.6 1.6 copy-start
  38.5 42.8 %all-to-all-start.2 = ((bf16[256,8,256]{2,1,0:T(8,128)(2,1)}), bf16[256,8,256]{2,1,0:T(8,128)(2,1)S(1)}, u32[]{:S(2)}, u32[]{:S(2)}) async-start(bf16[256,8,256]{2,1,0:T(8,128)(2,1)} %copy.30), calls=%async_computation.2 | async-start | bytes 2097152 | tf_op jit(solution)/shard_map/all_to_all | solution.py:67
  81.3 38.1 %all-to-all-start = ((bf16[256,8,256]{2,1,0:T(8,128)(2,1)}), bf16[256,8,256]{2,1,0:T(8,128)(2,1)S(1)}, u32[]{:S(2)}, u32[]{:S(2)}) async-start(bf16[256,8,256]{2,1,0:T(8,128)(2,1)} %copy.24), calls=%async_computation | async-start | bytes 2097152 | tf_op jit(solution)/shard_map/all_to_all | solution.py:67
  119.4 38.0 %all-to-all-start.3 = ((bf16[512,4,256]{2,1,0:T(4,128)(2,1)}), bf16[512,4,256]{2,1,0:T(4,128)(2,1)S(1)}, u32[]{:S(2)}, u32[]{:S(2)}) async-start(bf16[512,4,256]{2,1,0:T(4,128)(2,1)} %copy.32), calls=%async_computation.3 | async-start | bytes 2097152 | tf_op jit(solution)/shard_map/all_to_all | solution.py:71
  128.9 36.4 %copy-start.1 = (bf16[8,32,32]{2,1,0:T(8,128)(2,1)S(1)}, bf16[8,32,32]{2,1,0:T(8,128)(2,1)}, u32[]{:S(2)}) copy-start(bf16[8,32,32]{2,1,0:T(8,128)(2,1)} %param.12) | copy-start | bytes 49156
  130.7 35.4 %copy-start.2 = (bf16[4,64,64]{2,1,0:T(8,128)(2,1)S(1)}, bf16[4,64,64]{2,1,0:T(8,128)(2,1)}, u32[]{:S(2)}) copy-start(bf16[4,64,64]{2,1,0:T(8,128)(2,1)} %param.13) | copy-start | bytes 98308
  157.4 38.0 %all-to-all-start.1 = ((bf16[512,4,256]{2,1,0:T(4,128)(2,1)}), bf16[512,4,256]{2,1,0:T(4,128)(2,1)S(1)}, u32[]{:S(2)}, u32[]{:S(2)}) async-start(bf16[512,4,256]{2,1,0:T(4,128)(2,1)} %copy.26), calls=%async_computation.1 | async-start | bytes 2097152 | tf_op jit(solution)/shard_map/all_to_all | solution.py:71
  201.9 17.8 %collective-permute-start.7 = (bf16[32,2048]{1,0:T(8,128)(2,1)S(1)}, bf16[32,2048]{1,0:T(8,128)(2,1)S(1)}, u32[]{:S(2)}, u32[]{:S(2)}) collective-permute-start(bf16[32,2048]{1,0:T(8,128)(2,1)S(1)} %get-tuple-element.14), channel_id=1, source_target_pairs={{0,1},{1,2},{2,3},{3,4},{4,5},{5,6},{6,7},{7,0},{8,9},{9,10},{10,1... | collective-permute-start | bytes 393224 | tf_op jit(solution)/shard_map/ppermute | solution.py:83
  205.5 17.5 %collective-permute-start.8 = (bf16[32,2048]{1,0:T(8,128)(2,1)S(1)}, bf16[32,2048]{1,0:T(8,128)(2,1)S(1)}, u32[]{:S(2)}, u32[]{:S(2)}) collective-permute-start(bf16[32,2048]{1,0:T(8,128)(2,1)S(1)} %get-tuple-element.13), channel_id=1, source_target_pairs={{0,2},{1,3},{2,4},{3,5},{4,6},{5,7},{6,0},{7,1},{8,10},{9,11},{10,... | collective-permute-start | bytes 393224 | tf_op jit(solution)/shard_map/ppermute | solution.py:83
  209.2 17.7 %collective-permute-start.9 = (bf16[32,2048]{1,0:T(8,128)(2,1)S(1)}, bf16[32,2048]{1,0:T(8,128)(2,1)S(1)}, u32[]{:S(2)}, u32[]{:S(2)}) collective-permute-start(bf16[32,2048]{1,0:T(8,128)(2,1)S(1)} %get-tuple-element.12), channel_id=1, source_target_pairs={{0,3},{1,4},{2,5},{3,6},{4,7},{5,0},{6,1},{7,2},{8,11},{9,12},{10,... | collective-permute-start | bytes 393224 | tf_op jit(solution)/shard_map/ppermute | solution.py:83
  212.7 16.3 %collective-permute-start.10 = (bf16[32,2048]{1,0:T(8,128)(2,1)S(1)}, bf16[32,2048]{1,0:T(8,128)(2,1)S(1)}, u32[]{:S(2)}, u32[]{:S(2)}) collective-permute-start(bf16[32,2048]{1,0:T(8,128)(2,1)S(1)} %get-tuple-element.11), channel_id=1, source_target_pairs={{0,4},{1,5},{2,6},{3,7},{4,0},{5,1},{6,2},{7,3},{8,12},{9,13},{10,... | collective-permute-start | bytes 393224 | tf_op jit(solution)/shard_map/ppermute | solution.py:83
  216.2 15.3 %collective-permute-start.11 = (bf16[32,2048]{1,0:T(8,128)(2,1)S(1)}, bf16[32,2048]{1,0:T(8,128)(2,1)S(1)}, u32[]{:S(2)}, u32[]{:S(2)}) collective-permute-start(bf16[32,2048]{1,0:T(8,128)(2,1)S(1)} %get-tuple-element.10), channel_id=1, source_target_pairs={{0,5},{1,6},{2,7},{3,0},{4,1},{5,2},{6,3},{7,4},{8,13},{9,14},{10,... | collective-permute-start | bytes 393224 | tf_op jit(solution)/shard_map/ppermute | solution.py:83
  219.7 17.3 %collective-permute-start.12 = (bf16[32,2048]{1,0:T(8,128)(2,1)S(1)}, bf16[32,2048]{1,0:T(8,128)(2,1)S(1)}, u32[]{:S(2)}, u32[]{:S(2)}) collective-permute-start(bf16[32,2048]{1,0:T(8,128)(2,1)S(1)} %get-tuple-element.9), channel_id=1, source_target_pairs={{0,6},{1,7},{2,0},{3,1},{4,2},{5,3},{6,4},{7,5},{8,14},{9,15},{10,... | collective-permute-start | bytes 393224 | tf_op jit(solution)/shard_map/ppermute | solution.py:83
  223.1 16.5 %collective-permute-start.13 = (bf16[32,2048]{1,0:T(8,128)(2,1)S(1)}, bf16[32,2048]{1,0:T(8,128)(2,1)S(1)}, u32[]{:S(2)}, u32[]{:S(2)}) collective-permute-start(bf16[32,2048]{1,0:T(8,128)(2,1)S(1)} %get-tuple-element.8), channel_id=1, source_target_pairs={{0,7},{1,0},{2,1},{3,2},{4,3},{5,4},{6,5},{7,6},{8,15},{9,8},{10,9... | collective-permute-start | bytes 393224 | tf_op jit(solution)/shard_map/ppermute | solution.py:83
  226.9 18.1 %collective-permute-start.14 = (bf16[32,2048]{1,0:T(8,128)(2,1)S(1)}, bf16[32,2048]{1,0:T(8,128)(2,1)S(1)}, u32[]{:S(2)}, u32[]{:S(2)}) collective-permute-start(bf16[32,2048]{1,0:T(8,128)(2,1)S(1)} %get-tuple-element.23), channel_id=1, source_target_pairs={{0,1},{1,2},{2,3},{3,4},{4,5},{5,6},{6,7},{7,0},{8,9},{9,10},{10,1... | collective-permute-start | bytes 393224 | tf_op jit(solution)/shard_map/ppermute | solution.py:83
  229.0 19.5 %collective-permute-start.15 = (bf16[32,2048]{1,0:T(8,128)(2,1)S(1)}, bf16[32,2048]{1,0:T(8,128)(2,1)S(1)}, u32[]{:S(2)}, u32[]{:S(2)}) collective-permute-start(bf16[32,2048]{1,0:T(8,128)(2,1)S(1)} %get-tuple-element.22), channel_id=1, source_target_pairs={{0,2},{1,3},{2,4},{3,5},{4,6},{5,7},{6,0},{7,1},{8,10},{9,11},{10,... | collective-permute-start | bytes 393224 | tf_op jit(solution)/shard_map/ppermute | solution.py:83
  231.5 19.7 %collective-permute-start.16 = (bf16[32,2048]{1,0:T(8,128)(2,1)S(1)}, bf16[32,2048]{1,0:T(8,128)(2,1)S(1)}, u32[]{:S(2)}, u32[]{:S(2)}) collective-permute-start(bf16[32,2048]{1,0:T(8,128)(2,1)S(1)} %get-tuple-element.21), channel_id=1, source_target_pairs={{0,3},{1,4},{2,5},{3,6},{4,7},{5,0},{6,1},{7,2},{8,11},{9,12},{10,... | collective-permute-start | bytes 393224 | tf_op jit(solution)/shard_map/ppermute | solution.py:83
  237.0 14.3 %collective-permute-start.17 = (bf16[32,2048]{1,0:T(8,128)(2,1)S(1)}, bf16[32,2048]{1,0:T(8,128)(2,1)S(1)}, u32[]{:S(2)}, u32[]{:S(2)}) collective-permute-start(bf16[32,2048]{1,0:T(8,128)(2,1)S(1)} %get-tuple-element.20), channel_id=1, source_target_pairs={{0,4},{1,5},{2,6},{3,7},{4,0},{5,1},{6,2},{7,3},{8,12},{9,13},{10,... | collective-permute-start | bytes 393224 | tf_op jit(solution)/shard_map/ppermute | solution.py:83
  239.6 11.7 %collective-permute-start.18 = (bf16[32,2048]{1,0:T(8,128)(2,1)S(1)}, bf16[32,2048]{1,0:T(8,128)(2,1)S(1)}, u32[]{:S(2)}, u32[]{:S(2)}) collective-permute-start(bf16[32,2048]{1,0:T(8,128)(2,1)S(1)} %get-tuple-element.19), channel_id=1, source_target_pairs={{0,5},{1,6},{2,7},{3,0},{4,1},{5,2},{6,3},{7,4},{8,13},{9,14},{10,... | collective-permute-start | bytes 393224 | tf_op jit(solution)/shard_map/ppermute | solution.py:83
  245.0 6.9 %collective-permute-start.19 = (bf16[32,2048]{1,0:T(8,128)(2,1)S(1)}, bf16[32,2048]{1,0:T(8,128)(2,1)S(1)}, u32[]{:S(2)}, u32[]{:S(2)}) collective-permute-start(bf16[32,2048]{1,0:T(8,128)(2,1)S(1)} %get-tuple-element.18), channel_id=1, source_target_pairs={{0,6},{1,7},{2,0},{3,1},{4,2},{5,3},{6,4},{7,5},{8,14},{9,15},{10,... | collective-permute-start | bytes 393224 | tf_op jit(solution)/shard_map/ppermute | solution.py:83
  248.4 6.9 %collective-permute-start.20 = (bf16[32,2048]{1,0:T(8,128)(2,1)S(1)}, bf16[32,2048]{1,0:T(8,128)(2,1)S(1)}, u32[]{:S(2)}, u32[]{:S(2)}) collective-permute-start(bf16[32,2048]{1,0:T(8,128)(2,1)S(1)} %get-tuple-element.17), channel_id=1, source_target_pairs={{0,7},{1,0},{2,1},{3,2},{4,3},{5,4},{6,5},{7,6},{8,15},{9,8},{10,9... | collective-permute-start | bytes 393224 | tf_op jit(solution)/shard_map/ppermute | solution.py:83

commit v3 on v1

--- a/solution.py
+++ b/solution.py
@@ -32,9 +32,10 @@
         outer_rows = tok_rows // BLOCK
         token_grid = inputs.reshape(outer_rows, BLOCK, channels)
         rows = first_factor.shape[0]
-        both = lax.all_gather(
-            jnp.concatenate([first_factor, second_factor], axis=0), "ch", axis=0, tiled=True
-        ).reshape(n_ch, 2, rows, BLOCK)
+        pair = jnp.concatenate([first_factor, second_factor], axis=0)
+        spread = jnp.broadcast_to(pair[None], (n_ch,) + pair.shape)
+        both = lax.all_to_all(spread, "ch", split_axis=0, concat_axis=0, tiled=True)
+        both = both.reshape(n_ch, 2, rows, BLOCK)
         full_first = both[:, 0].reshape(BLOCK, BLOCK)
         full_second = both[:, 1].reshape(BLOCK, BLOCK)
         twiddle_t = jnp.transpose(twiddle)

time: 276 us -> 233 us (0.84)
  waiting for transfers between devices: 183 us -> 148 us
  between operations: 13.7 us -> 0.26 us
  starting transfers between devices: 47.9 us -> 57.3 us
    all_gather x1 -> x0, waiting for transfers between devices: 51.1 us -> none  [local(): lax.all_gather(jnp.concatenate([first_factor, second_factor], axis=0), 'c...]
    all_to_all x0 -> x1, waiting for transfers between devices: none -> 15.7 us  [local(): both = lax.all_to_all(spread, 'ch', split_axis=0, concat_axis=0, tiled=True)]
    all_to_all x0 -> x1, starting transfers between devices: none -> 6.11 us  [local(): both = lax.all_to_all(spread, 'ch', split_axis=0, concat_axis=0, tiled=True)]
    all_to_all x2, starting transfers between devices: 20.9 us -> 25.1 us  [local(): lax.all_to_all(twisted, 'seq', split_axis=0, concat_axis=1, tiled=True)]
  transfers between devices with their start and end apart: 7 -> 7, of which waited for: 7 -> 7; matrix products, arithmetic and copies ran while one was open for 5% -> 6% of each run, Pallas kernels for 0% -> 0%
where the time goes in v3:
time: 233 us
  waiting for transfers between devices  148 us (64%)
  starting transfers between devices  57.3 us (25%)
  local copies, waits for them, and re-layouts  12.8 us (5%)
  matrix products  7.94 us (3%)
  other arithmetic  6.71 us (3%)
    all_to_all x2, waiting for transfers between devices, local(): lax.all_to_all(mixed, 'seq', split_axis=0, concat_axis=1, tiled=True)  51.2 us
    all_to_all x2, waiting for transfers between devices, local(): lax.all_to_all(twisted, 'seq', split_axis=0, concat_axis=1, tiled=True)  50.4 us
    all_to_all x2, waiting for transfers between devices, local(): lax.all_to_all(middle_t, 'ch', split_axis=0, concat_axis=0, tiled=True)  30.5 us
    all_to_all x2, starting transfers between devices, local(): lax.all_to_all(twisted, 'seq', split_axis=0, concat_axis=1, tiled=True)  25.1 us
    all_to_all x2, starting transfers between devices, local(): lax.all_to_all(mixed, 'seq', split_axis=0, concat_axis=1, tiled=True)  19 us
    all_to_all x1, waiting for transfers between devices, local(): both = lax.all_to_all(spread, 'ch', split_axis=0, concat_axis=0, tiled=True)  15.7 us
    all_to_all x2, starting transfers between devices, local(): lax.all_to_all(middle_t, 'ch', split_axis=0, concat_axis=0, tiled=True)  7.12 us
    all_to_all x1, starting transfers between devices, local(): both = lax.all_to_all(spread, 'ch', split_axis=0, concat_axis=0, tiled=True)  6.11 us
  transfers between devices with their start and end apart: 7, of which 7 were waited for; matrix products, arithmetic and copies ran while one was open for 6% of the time, Pallas kernels for 0%

profile of v3, /device:TPU:24, one launch (start us, length us, event | category | flops | bytes accessed | tf_op | source)
XLA Modules:
  0.0 232.8 jit_solution(8422021919565129018)
XLA Ops:
  0.0 0.9 pad_maximum_fusion.1
  0.9 0.0 copy-start
  0.9 1.1 broadcast_in_dim.54
  2.0 6.1 %all-to-all-start = ((bf16[8,128,512]{2,1,0:T(8,128)(2,1)}), bf16[8,128,512]{2,1,0:T(8,128)(2,1)S(1)}, u32[]{:S(2)}, u32[]{:S(2)}) async-start(bf16[8,128,512]{2,1,0:T(8,128)(2,1)} %broadcast_in_dim.54), calls=%async_computation | async-start | bytes 2097152 | tf_op jit(solution)/shard_map/all_to_all | solution.py:37
  8.1 0.0 copy-done.3
  8.1 15.7 %all-to-all-done = bf16[8,128,512]{2,1,0:T(8,128)(2,1)S(1)} async-done(((bf16[8,128,512]{2,1,0:T(8,128)(2,1)}), bf16[8,128,512]{2,1,0:T(8,128)(2,1)S(1)}, u32[]{:S(2)}, u32[]{:S(2)}) %all-to-all-start) | async-done | bytes 1048608 | tf_op jit(solution)/shard_map/all_to_all | solution.py:37
  23.8 0.0 copy-done
  23.8 0.7 multiply_convert_fusion.1
  24.6 1.6 copy.27
  26.1 15.6 %all-to-all-start.4 = ((bf16[256,8,256]{2,1,0:T(8,128)(2,1)}), bf16[256,8,256]{2,1,0:T(8,128)(2,1)}, u32[]{:S(2)}, u32[]{:S(2)}) async-start(bf16[256,8,256]{2,1,0:T(8,128)(2,1)} %copy.27), calls=%async_computation.4 | async-start | bytes 2097152 | tf_op jit(solution)/shard_map/all_to_all | solution.py:55
  41.8 0.7 multiply_convert_fusion.3
  42.5 1.6 copy.21
  44.0 25.9 %all-to-all-done.4 = bf16[256,8,256]{2,1,0:T(8,128)(2,1)} async-done(((bf16[256,8,256]{2,1,0:T(8,128)(2,1)}), bf16[256,8,256]{2,1,0:T(8,128)(2,1)}, u32[]{:S(2)}, u32[]{:S(2)}) %all-to-all-start.4) | async-done | bytes 1048608 | tf_op jit(solution)/shard_map/all_to_all | solution.py:55
  70.0 9.5 %all-to-all-start.1 = ((bf16[256,8,256]{2,1,0:T(8,128)(2,1)}), bf16[256,8,256]{2,1,0:T(8,128)(2,1)S(1)}, u32[]{:S(2)}, u32[]{:S(2)}) async-start(bf16[256,8,256]{2,1,0:T(8,128)(2,1)} %copy.21), calls=%async_computation.1 | async-start | bytes 2097152 | tf_op jit(solution)/shard_map/all_to_all | solution.py:55
  79.5 1.9 convolution_convert_fusion.4
  81.4 1.8 copy.29
  83.2 24.5 %all-to-all-done.1 = bf16[256,8,256]{2,1,0:T(8,128)(2,1)S(1)} async-done(((bf16[256,8,256]{2,1,0:T(8,128)(2,1)}), bf16[256,8,256]{2,1,0:T(8,128)(2,1)S(1)}, u32[]{:S(2)}, u32[]{:S(2)}) %all-to-all-start.1) | async-done | bytes 1048608 | tf_op jit(solution)/shard_map/all_to_all | solution.py:55
  107.7 9.5 %all-to-all-start.5 = ((bf16[512,4,256]{2,1,0:T(4,128)(2,1)}), bf16[512,4,256]{2,1,0:T(4,128)(2,1)S(1)}, u32[]{:S(2)}, u32[]{:S(2)}) async-start(bf16[512,4,256]{2,1,0:T(4,128)(2,1)} %copy.29), calls=%async_computation.5 | async-start | bytes 2097152 | tf_op jit(solution)/shard_map/all_to_all | solution.py:59
  117.2 0.7 convolution_convert_fusion.5
  117.9 0.0 copy-start.1
  117.9 1.8 copy.23
  119.7 25.8 %all-to-all-done.5 = bf16[512,4,256]{2,1,0:T(4,128)(2,1)S(1)} async-done(((bf16[512,4,256]{2,1,0:T(4,128)(2,1)}), bf16[512,4,256]{2,1,0:T(4,128)(2,1)S(1)}, u32[]{:S(2)}, u32[]{:S(2)}) %all-to-all-start.5) | async-done | bytes 1048608 | tf_op jit(solution)/shard_map/all_to_all | solution.py:59
  145.5 9.5 %all-to-all-start.2 = ((bf16[512,4,256]{2,1,0:T(4,128)(2,1)}), bf16[512,4,256]{2,1,0:T(4,128)(2,1)S(1)}, u32[]{:S(2)}, u32[]{:S(2)}) async-start(bf16[512,4,256]{2,1,0:T(4,128)(2,1)} %copy.23), calls=%async_computation.2 | async-start | bytes 2097152 | tf_op jit(solution)/shard_map/all_to_all | solution.py:59
  155.0 0.0 copy-done.1
  155.0 0.1 broadcast_select_fusion
  155.2 0.4 select_n.37
  155.5 0.3 convert_bitcast_fusion
  155.8 0.4 copy.30
  156.2 1.7 reshape.116
  158.0 25.4 %all-to-all-done.2 = bf16[512,4,256]{2,1,0:T(4,128)(2,1)S(1)} async-done(((bf16[512,4,256]{2,1,0:T(4,128)(2,1)}), bf16[512,4,256]{2,1,0:T(4,128)(2,1)S(1)}, u32[]{:S(2)}, u32[]{:S(2)}) %all-to-all-start.2) | async-done | bytes 1048608 | tf_op jit(solution)/shard_map/all_to_all | solution.py:59
  183.3 0.3 convert_bitcast_fusion.1
  183.7 0.4 copy.24
  184.0 1.7 reshape.115
  185.8 3.4 %multiply_convert_fusion.2 = (bf16[8,256,256]{2,1,0:T(8,128)(2,1)S(1)}, bf16[8,256,256]{2,1,0:T(8,128)(2,1)S(1)}) fusion(f32[8,256,256]{2,1,0:T(8,128)} %reshape.115, bf16[8,512,256]{2,1,0:T(8,128)(2,1)} %bitcast.76, f32[8,256,256]{2,1,0:T(8,128)} %reshape.116), kind=kLoop, calls=%fused_computation.9 | loop fusion | flops 3145728 | bytes 8388608 | tf_op jit(solution)/shard_map/convert_element_type | solution.py:62
  189.2 1.5 convolution_convert_fusion.3
  190.6 3.6 %all-to-all-start.3 = ((bf16[8,32,2048]{2,1,0:T(8,128)(2,1)}), bf16[8,32,2048]{2,1,0:T(8,128)(2,1)S(1)}, u32[]{:S(2)}, u32[]{:S(2)}) async-start(bf16[8,32,2048]{2,1,0:T(8,128)(2,1)} %bitcast.15), calls=%async_computation.3 | async-start | bytes 2097152 | tf_op jit(solution)/shard_map/all_to_all | solution.py:68
  194.2 0.0 copy-start.2
  194.2 1.4 convolution_convert_fusion.1
  195.7 14.8 %all-to-all-done.3 = bf16[8,32,2048]{2,1,0:T(8,128)(2,1)S(1)} async-done(((bf16[8,32,2048]{2,1,0:T(8,128)(2,1)}), bf16[8,32,2048]{2,1,0:T(8,128)(2,1)S(1)}, u32[]{:S(2)}, u32[]{:S(2)}) %all-to-all-start.3) | async-done | bytes 1048608 | tf_op jit(solution)/shard_map/all_to_all | solution.py:68
  210.5 3.6 %all-to-all-start.6 = ((bf16[8,32,2048]{2,1,0:T(8,128)(2,1)}), bf16[8,32,2048]{2,1,0:T(8,128)(2,1)S(1)}, u32[]{:S(2)}, u32[]{:S(2)}) async-start(bf16[8,32,2048]{2,1,0:T(8,128)(2,1)} %bitcast.29), calls=%async_computation.6 | async-start | bytes 2097152 | tf_op jit(solution)/shard_map/all_to_all | solution.py:68
  214.1 0.0 copy-done.2
  214.1 0.1 copy.25
  214.2 0.2 broadcast_select_fusion.1
  214.4 0.2 select_n.39
  214.6 0.5 convolution_convert_fusion.2
  215.1 15.7 %all-to-all-done.6 = bf16[8,32,2048]{2,1,0:T(8,128)(2,1)S(1)} async-done(((bf16[8,32,2048]{2,1,0:T(8,128)(2,1)}), bf16[8,32,2048]{2,1,0:T(8,128)(2,1)S(1)}, u32[]{:S(2)}, u32[]{:S(2)}) %all-to-all-start.6) | async-done | bytes 1048608 | tf_op jit(solution)/shard_map/all_to_all | solution.py:68
  230.8 0.5 convolution_convert_fusion
  231.3 1.5 pad_maximum_fusion
  (7 shorter events, 0.1 us)
Async XLA Ops:
  0.0 8.1 %copy-start.3 = (f32[8,512]{1,0:T(8,128)S(1)}, f32[8,512]{1,0:T(8,128)}, u32[]{:S(2)}) copy-start(f32[8,512]{1,0:T(8,128)} %param.8) | copy-start | bytes 49156
  0.9 22.9 %copy-start = (bf16[4096,256]{1,0:T(8,128)(2,1)S(1)}, bf16[4096,256]{1,0:T(8,128)(2,1)}, u32[]{:S(2)}) copy-start(bf16[4096,256]{1,0:T(8,128)(2,1)} %param.6) | copy-start | bytes 6291460
  2.0 21.8 %all-to-all-start = ((bf16[8,128,512]{2,1,0:T(8,128)(2,1)}), bf16[8,128,512]{2,1,0:T(8,128)(2,1)S(1)}, u32[]{:S(2)}, u32[]{:S(2)}) async-start(bf16[8,128,512]{2,1,0:T(8,128)(2,1)} %broadcast_in_dim.54), calls=%async_computation | async-start | bytes 2097152 | tf_op jit(solution)/shard_map/all_to_all | solution.py:37
  26.1 43.9 %all-to-all-start.4 = ((bf16[256,8,256]{2,1,0:T(8,128)(2,1)}), bf16[256,8,256]{2,1,0:T(8,128)(2,1)}, u32[]{:S(2)}, u32[]{:S(2)}) async-start(bf16[256,8,256]{2,1,0:T(8,128)(2,1)} %copy.27), calls=%async_computation.4 | async-start | bytes 2097152 | tf_op jit(solution)/shard_map/all_to_all | solution.py:55
  70.0 37.7 %all-to-all-start.1 = ((bf16[256,8,256]{2,1,0:T(8,128)(2,1)}), bf16[256,8,256]{2,1,0:T(8,128)(2,1)S(1)}, u32[]{:S(2)}, u32[]{:S(2)}) async-start(bf16[256,8,256]{2,1,0:T(8,128)(2,1)} %copy.21), calls=%async_computation.1 | async-start | bytes 2097152 | tf_op jit(solution)/shard_map/all_to_all | solution.py:55
  107.7 37.8 %all-to-all-start.5 = ((bf16[512,4,256]{2,1,0:T(4,128)(2,1)}), bf16[512,4,256]{2,1,0:T(4,128)(2,1)S(1)}, u32[]{:S(2)}, u32[]{:S(2)}) async-start(bf16[512,4,256]{2,1,0:T(4,128)(2,1)} %copy.29), calls=%async_computation.5 | async-start | bytes 2097152 | tf_op jit(solution)/shard_map/all_to_all | solution.py:59
  117.9 37.1 %copy-start.1 = (bf16[8,32,32]{2,1,0:T(8,128)(2,1)S(1)}, bf16[8,32,32]{2,1,0:T(8,128)(2,1)}, u32[]{:S(2)}) copy-start(bf16[8,32,32]{2,1,0:T(8,128)(2,1)} %param.10) | copy-start | bytes 49156
  145.5 37.9 %all-to-all-start.2 = ((bf16[512,4,256]{2,1,0:T(4,128)(2,1)}), bf16[512,4,256]{2,1,0:T(4,128)(2,1)S(1)}, u32[]{:S(2)}, u32[]{:S(2)}) async-start(bf16[512,4,256]{2,1,0:T(4,128)(2,1)} %copy.23), calls=%async_computation.2 | async-start | bytes 2097152 | tf_op jit(solution)/shard_map/all_to_all | solution.py:59
  190.6 19.9 %all-to-all-start.3 = ((bf16[8,32,2048]{2,1,0:T(8,128)(2,1)}), bf16[8,32,2048]{2,1,0:T(8,128)(2,1)S(1)}, u32[]{:S(2)}, u32[]{:S(2)}) async-start(bf16[8,32,2048]{2,1,0:T(8,128)(2,1)} %bitcast.15), calls=%async_computation.3 | async-start | bytes 2097152 | tf_op jit(solution)/shard_map/all_to_all | solution.py:68
  194.2 19.9 %copy-start.2 = (bf16[4,64,64]{2,1,0:T(8,128)(2,1)S(1)}, bf16[4,64,64]{2,1,0:T(8,128)(2,1)}, u32[]{:S(2)}) copy-start(bf16[4,64,64]{2,1,0:T(8,128)(2,1)} %param.11) | copy-start | bytes 98308
  210.5 20.3 %all-to-all-start.6 = ((bf16[8,32,2048]{2,1,0:T(8,128)(2,1)}), bf16[8,32,2048]{2,1,0:T(8,128)(2,1)S(1)}, u32[]{:S(2)}, u32[]{:S(2)}) async-start(bf16[8,32,2048]{2,1,0:T(8,128)(2,1)} %bitcast.29), calls=%async_computation.6 | async-start | bytes 2097152 | tf_op jit(solution)/shard_map/all_to_all | solution.py:68

commit v4 on v3

--- a/solution.py
+++ b/solution.py
@@ -1,10 +1,12 @@
 import jax
 import jax.numpy as jnp
 from jax import lax
-from jax.sharding import PartitionSpec as P
+from jax.sharding import Mesh, PartitionSpec as P
 
 BLOCK = 512
 CHUNKS = 2
+CH = ("x", "zlo")
+SPREAD = ("seq", "zlo")
 
 
 def channel_weights(block_first, block_second, n_ch):
@@ -26,7 +28,7 @@
     return w1t, w2
 
 
-def make_local(n_seq, n_ch):
+def make_local(n_seq, n_ch, n_zlo):
     def local(inputs, first_factor, twiddle, second_factor, block_first, block_second):
         tok_rows, channels = inputs.shape
         outer_rows = tok_rows // BLOCK
@@ -34,7 +36,7 @@
         rows = first_factor.shape[0]
         pair = jnp.concatenate([first_factor, second_factor], axis=0)
         spread = jnp.broadcast_to(pair[None], (n_ch,) + pair.shape)
-        both = lax.all_to_all(spread, "ch", split_axis=0, concat_axis=0, tiled=True)
+        both = lax.all_to_all(spread, CH, split_axis=0, concat_axis=0, tiled=True)
         both = both.reshape(n_ch, 2, rows, BLOCK)
         full_first = both[:, 0].reshape(BLOCK, BLOCK)
         full_second = both[:, 1].reshape(BLOCK, BLOCK)
@@ -52,11 +54,21 @@
                 preferred_element_type=jnp.float32,
             )
             twisted = (first * twiddle_t[lo:lo + width, :, None]).astype(jnp.bfloat16)
-            gathered = lax.all_to_all(twisted, "seq", split_axis=0, concat_axis=1, tiled=True)
+            owners = n_seq * n_zlo
+            kk = width // owners
+            gathered = lax.all_to_all(
+                twisted.reshape(owners, kk, outer_rows, channels), SPREAD, 0, 0, tiled=True
+            ).reshape(n_seq, n_zlo, kk, outer_rows, channels)
             mixed = lax.dot_general(
-                full_second, gathered, contract, preferred_element_type=jnp.float32
+                full_second.reshape(BLOCK, n_seq, outer_rows),
+                gathered,
+                (((1, 2), (0, 3)), ((), ())),
+                preferred_element_type=jnp.float32,
             ).astype(jnp.bfloat16)
-            returned = lax.all_to_all(mixed, "seq", split_axis=0, concat_axis=1, tiled=True)
+            mixed = mixed.reshape(n_seq, outer_rows, n_zlo, kk, channels)
+            mixed = jnp.transpose(mixed, (0, 2, 1, 3, 4)).reshape(owners, outer_rows, kk, channels)
+            returned = lax.all_to_all(mixed, SPREAD, 0, 0, tiled=True)
+            returned = jnp.transpose(returned, (1, 0, 2, 3)).reshape(outer_rows, width, channels)
             gated = (
                 token_grid[:, lo:lo + width].astype(jnp.float32) * returned.astype(jnp.float32)
             ).astype(jnp.bfloat16)
@@ -65,7 +77,7 @@
                 w1t, gated, contract, preferred_element_type=jnp.float32
             ).astype(jnp.bfloat16)
             middle_t = middle_t.reshape(n_ch, channels // n_ch, outer_rows * width)
-            recv = lax.all_to_all(middle_t, "ch", split_axis=0, concat_axis=0, tiled=True)
+            recv = lax.all_to_all(middle_t, CH, split_axis=0, concat_axis=0, tiled=True)
             recv = recv.reshape(channels, outer_rows * width)
             result = lax.dot_general(
                 recv, w2, (((0,), (0,)), ((), ())), preferred_element_type=jnp.float32
@@ -78,18 +90,21 @@
 
 
 def solution(mesh):
+    n_seq, n_ch = mesh.shape["seq"], mesh.shape["ch"]
+    n_zlo = 2
+    split = Mesh(mesh.devices.reshape(n_seq, n_ch // n_zlo, n_zlo), ("seq",) + CH)
     placed = (
-        P("seq", "ch"),
-        P("ch", None),
+        P("seq", CH),
+        P(CH, None),
         P("seq", None),
-        P("ch", None),
-        P("ch", None, None),
-        P("ch", None, None),
+        P(CH, None),
+        P(CH, None, None),
+        P(CH, None, None),
     )
     return jax.shard_map(
-        make_local(mesh.shape["seq"], mesh.shape["ch"]),
-        mesh=mesh,
+        make_local(n_seq, n_ch, n_zlo),
+        mesh=split,
         in_specs=placed,
-        out_specs=P("seq", "ch"),
+        out_specs=P("seq", CH),
         check_vma=False,
     )

time: 233 us -> 234 us (level)
  the two profiles are of different devices: /device:TPU:24 before, /device:TPU:8 now
where the time goes in v4:
time: 234 us; the launch traced here: 233 us
  waiting for transfers between devices  157 us (67%)
  starting transfers between devices  51.8 us (22%)
  matrix products  9.23 us (4%)
  local copies, waits for them, and re-layouts  8.84 us (4%)
  other arithmetic  6.24 us (3%)
    all_to_all x2, waiting for transfers between devices, local(): returned = lax.all_to_all(mixed, SPREAD, 0, 0, tiled=True)  56.9 us
    all_to_all x2, waiting for transfers between devices, local(): lax.all_to_all(twisted.reshape(owners, kk, outer_rows, channels), SPREAD,...  53.6 us
    all_to_all x2, waiting for transfers between devices, local(): recv = lax.all_to_all(middle_t, CH, split_axis=0, concat_axis=0, tiled=True)  30.4 us
    all_to_all x2, starting transfers between devices, local(): lax.all_to_all(twisted.reshape(owners, kk, outer_rows, channels), SPREAD,...  24.2 us
    all_to_all x1, waiting for transfers between devices, local(): both = lax.all_to_all(spread, CH, split_axis=0, concat_axis=0, tiled=True)  15.7 us
    all_to_all x2, starting transfers between devices, local(): returned = lax.all_to_all(mixed, SPREAD, 0, 0, tiled=True)  14.4 us
    all_to_all x2, starting transfers between devices, local(): recv = lax.all_to_all(middle_t, CH, split_axis=0, concat_axis=0, tiled=True)  7.12 us
    all_to_all x1, starting transfers between devices, local(): both = lax.all_to_all(spread, CH, split_axis=0, concat_axis=0, tiled=True)  6.11 us
  transfers between devices with their start and end apart: 7, of which 7 were waited for; matrix products, arithmetic and copies ran while one was open for 6% of the time, Pallas kernels for 0%

profile of v4, /device:TPU:8, one launch (start us, length us, event | category | flops | bytes accessed | tf_op | source)
XLA Modules:
  0.0 233.0 jit_solution(16721877912791091832)
XLA Ops:
  0.0 0.0 copy-start.4
  0.0 0.9 pad_maximum_fusion.1
  0.9 0.0 copy-start
  0.9 1.1 broadcast_in_dim.54
  2.0 6.1 %all-to-all-start = ((bf16[8,128,512]{2,1,0:T(8,128)(2,1)}), bf16[8,128,512]{2,1,0:T(8,128)(2,1)S(1)}, u32[]{:S(2)}, u32[]{:S(2)}) async-start(bf16[8,128,512]{2,1,0:T(8,128)(2,1)} %broadcast_in_dim.54), calls=%async_computation | async-start | bytes 2097152 | tf_op jit(solution)/shard_map/all_to_all | solution.py:39
  8.1 0.0 copy-done.4
  8.1 15.7 %all-to-all-done = bf16[8,128,512]{2,1,0:T(8,128)(2,1)S(1)} async-done(((bf16[8,128,512]{2,1,0:T(8,128)(2,1)}), bf16[8,128,512]{2,1,0:T(8,128)(2,1)S(1)}, u32[]{:S(2)}, u32[]{:S(2)}) %all-to-all-start) | async-done | bytes 1048608 | tf_op jit(solution)/shard_map/all_to_all | solution.py:39
  23.8 0.0 copy-done
  23.8 0.7 multiply_convert_fusion
  24.6 1.6 copy.33
  26.1 16.9 %all-to-all-start.4 = ((bf16[128,2,8,256]{3,2,1,0:T(8,128)(2,1)}), bf16[128,2,8,256]{3,2,1,0:T(8,128)(2,1)}, u32[]{:S(2)}, u32[]{:S(2)}) async-start(bf16[128,2,8,256]{3,2,1,0:T(8,128)(2,1)} %bitcast.26), calls=%async_computation.4 | async-start | bytes 2097152 | tf_op jit(solution)/shard_map/all_to_all | solution.py:59
  43.1 0.7 multiply_convert_fusion.1
  43.8 1.6 copy.30
  45.3 28.0 %all-to-all-done.4 = bf16[128,2,8,256]{3,2,1,0:T(8,128)(2,1)} async-done(((bf16[128,2,8,256]{3,2,1,0:T(8,128)(2,1)}), bf16[128,2,8,256]{3,2,1,0:T(8,128)(2,1)}, u32[]{:S(2)}, u32[]{:S(2)}) %all-to-all-start.4) | async-done | bytes 1048608 | tf_op jit(solution)/shard_map/all_to_all | solution.py:59
  73.3 7.3 %all-to-all-start.1 = ((bf16[128,2,8,256]{3,2,1,0:T(8,128)(2,1)}), bf16[128,2,8,256]{3,2,1,0:T(8,128)(2,1)}, u32[]{:S(2)}, u32[]{:S(2)}) async-start(bf16[128,2,8,256]{3,2,1,0:T(8,128)(2,1)} %bitcast.8), calls=%async_computation.1 | async-start | bytes 2097152 | tf_op jit(solution)/shard_map/all_to_all | solution.py:59
  80.7 0.8 copy.10
  81.5 0.6 reshape_reshape_squeeze.4
  82.1 2.0 fusion.3
  84.0 1.1 copy.21
  85.2 25.7 %all-to-all-done.1 = bf16[128,2,8,256]{3,2,1,0:T(8,128)(2,1)} async-done(((bf16[128,2,8,256]{3,2,1,0:T(8,128)(2,1)}), bf16[128,2,8,256]{3,2,1,0:T(8,128)(2,1)}, u32[]{:S(2)}, u32[]{:S(2)}) %all-to-all-start.1) | async-done | bytes 1048608 | tf_op jit(solution)/shard_map/all_to_all | solution.py:59
  110.9 6.9 %all-to-all-start.5 = ((bf16[128,8,2,256]{3,1,2,0:T(8,128)(2,1)}), bf16[128,8,2,256]{3,1,2,0:T(8,128)(2,1)S(1)}, u32[]{:S(2)}, u32[]{:S(2)}) async-start(bf16[128,8,2,256]{3,1,2,0:T(8,128)(2,1)} %bitcast.32), calls=%async_computation.5 | async-start | bytes 2097152 | tf_op jit(solution)/shard_map/all_to_all | solution.py:70
  117.7 2.0 fusion.2
  119.7 0.0 copy-start.2
  119.7 1.1 copy.14
  120.8 27.5 %all-to-all-done.5 = bf16[128,8,2,256]{3,1,2,0:T(8,128)(2,1)S(1)} async-done(((bf16[128,8,2,256]{3,1,2,0:T(8,128)(2,1)}), bf16[128,8,2,256]{3,1,2,0:T(8,128)(2,1)S(1)}, u32[]{:S(2)}, u32[]{:S(2)}) %all-to-all-start.5) | async-done | bytes 1048608 | tf_op jit(solution)/shard_map/all_to_all | solution.py:70
  148.3 7.5 %all-to-all-start.2 = ((bf16[128,8,2,256]{3,1,2,0:T(8,128)(2,1)}), bf16[128,8,2,256]{3,1,2,0:T(8,128)(2,1)}, u32[]{:S(2)}, u32[]{:S(2)}) async-start(bf16[128,8,2,256]{3,1,2,0:T(8,128)(2,1)} %bitcast.14), calls=%async_computation.2 | async-start | bytes 2097152 | tf_op jit(solution)/shard_map/all_to_all | solution.py:70
  155.8 0.0 copy-done.2
  155.9 0.1 broadcast_select_fusion
  156.0 0.4 select_n.37
  156.4 0.3 convert_element_type.75
  156.7 29.4 %all-to-all-done.2 = bf16[128,8,2,256]{3,1,2,0:T(8,128)(2,1)} async-done(((bf16[128,8,2,256]{3,1,2,0:T(8,128)(2,1)}), bf16[128,8,2,256]{3,1,2,0:T(8,128)(2,1)}, u32[]{:S(2)}, u32[]{:S(2)}) %all-to-all-start.2) | async-done | bytes 1048608 | tf_op jit(solution)/shard_map/all_to_all | solution.py:70
  186.1 1.7 convert_element_type.74
  187.7 0.2 copy-done.1
  188.0 1.6 fusion.1
  189.6 1.5 convolution_convert_fusion.3
  191.1 3.6 %all-to-all-start.3 = ((bf16[8,32,2048]{2,1,0:T(8,128)(2,1)}), bf16[8,32,2048]{2,1,0:T(8,128)(2,1)S(1)}, u32[]{:S(2)}, u32[]{:S(2)}) async-start(bf16[8,32,2048]{2,1,0:T(8,128)(2,1)} %bitcast.18), calls=%async_computation.3 | async-start | bytes 2097152 | tf_op jit(solution)/shard_map/all_to_all | solution.py:80
  194.6 0.0 copy-start.3
  194.6 1.4 convolution_convert_fusion.1
  196.1 15.4 %all-to-all-done.3 = bf16[8,32,2048]{2,1,0:T(8,128)(2,1)S(1)} async-done(((bf16[8,32,2048]{2,1,0:T(8,128)(2,1)}), bf16[8,32,2048]{2,1,0:T(8,128)(2,1)S(1)}, u32[]{:S(2)}, u32[]{:S(2)}) %all-to-all-start.3) | async-done | bytes 1048608 | tf_op jit(solution)/shard_map/all_to_all | solution.py:80
  211.5 3.6 %all-to-all-start.6 = ((bf16[8,32,2048]{2,1,0:T(8,128)(2,1)}), bf16[8,32,2048]{2,1,0:T(8,128)(2,1)S(1)}, u32[]{:S(2)}, u32[]{:S(2)}) async-start(bf16[8,32,2048]{2,1,0:T(8,128)(2,1)} %bitcast.36), calls=%async_computation.6 | async-start | bytes 2097152 | tf_op jit(solution)/shard_map/all_to_all | solution.py:80
  215.0 0.0 copy-done.3
  215.0 0.1 copy.16
  215.2 0.2 broadcast_select_fusion.1
  215.4 0.2 select_n.39
  215.6 0.5 convolution_convert_fusion.2
  216.1 15.0 %all-to-all-done.6 = bf16[8,32,2048]{2,1,0:T(8,128)(2,1)S(1)} async-done(((bf16[8,32,2048]{2,1,0:T(8,128)(2,1)}), bf16[8,32,2048]{2,1,0:T(8,128)(2,1)S(1)}, u32[]{:S(2)}, u32[]{:S(2)}) %all-to-all-start.6) | async-done | bytes 1048608 | tf_op jit(solution)/shard_map/all_to_all | solution.py:80
  231.0 0.5 convolution_convert_fusion
  231.5 1.5 pad_maximum_fusion
  (7 shorter events, 0.1 us)
Async XLA Ops:
  0.0 8.1 %copy-start.4 = (f32[8,512]{1,0:T(8,128)S(1)}, f32[8,512]{1,0:T(8,128)}, u32[]{:S(2)}) copy-start(f32[8,512]{1,0:T(8,128)} %param.8) | copy-start | bytes 49156
  0.9 22.9 %copy-start = (bf16[4096,256]{1,0:T(8,128)(2,1)S(1)}, bf16[4096,256]{1,0:T(8,128)(2,1)}, u32[]{:S(2)}) copy-start(bf16[4096,256]{1,0:T(8,128)(2,1)} %param.6) | copy-start | bytes 6291460
  2.0 21.8 %all-to-all-start = ((bf16[8,128,512]{2,1,0:T(8,128)(2,1)}), bf16[8,128,512]{2,1,0:T(8,128)(2,1)S(1)}, u32[]{:S(2)}, u32[]{:S(2)}) async-start(bf16[8,128,512]{2,1,0:T(8,128)(2,1)} %broadcast_in_dim.54), calls=%async_computation | async-start | bytes 2097152 | tf_op jit(solution)/shard_map/all_to_all | solution.py:39
  26.1 47.2 %all-to-all-start.4 = ((bf16[128,2,8,256]{3,2,1,0:T(8,128)(2,1)}), bf16[128,2,8,256]{3,2,1,0:T(8,128)(2,1)}, u32[]{:S(2)}, u32[]{:S(2)}) async-start(bf16[128,2,8,256]{3,2,1,0:T(8,128)(2,1)} %bitcast.26), calls=%async_computation.4 | async-start | bytes 2097152 | tf_op jit(solution)/shard_map/all_to_all | solution.py:59
  73.3 37.6 %all-to-all-start.1 = ((bf16[128,2,8,256]{3,2,1,0:T(8,128)(2,1)}), bf16[128,2,8,256]{3,2,1,0:T(8,128)(2,1)}, u32[]{:S(2)}, u32[]{:S(2)}) async-start(bf16[128,2,8,256]{3,2,1,0:T(8,128)(2,1)} %bitcast.8), calls=%async_computation.1 | async-start | bytes 2097152 | tf_op jit(solution)/shard_map/all_to_all | solution.py:59
  110.9 37.5 %all-to-all-start.5 = ((bf16[128,8,2,256]{3,1,2,0:T(8,128)(2,1)}), bf16[128,8,2,256]{3,1,2,0:T(8,128)(2,1)S(1)}, u32[]{:S(2)}, u32[]{:S(2)}) async-start(bf16[128,8,2,256]{3,1,2,0:T(8,128)(2,1)} %bitcast.32), calls=%async_computation.5 | async-start | bytes 2097152 | tf_op jit(solution)/shard_map/all_to_all | solution.py:70
  119.7 36.1 %copy-start.2 = (bf16[8,32,32]{2,1,0:T(8,128)(2,1)S(1)}, bf16[8,32,32]{2,1,0:T(8,128)(2,1)}, u32[]{:S(2)}) copy-start(bf16[8,32,32]{2,1,0:T(8,128)(2,1)} %param.10) | copy-start | bytes 49156
  148.3 37.7 %all-to-all-start.2 = ((bf16[128,8,2,256]{3,1,2,0:T(8,128)(2,1)}), bf16[128,8,2,256]{3,1,2,0:T(8,128)(2,1)}, u32[]{:S(2)}, u32[]{:S(2)}) async-start(bf16[128,8,2,256]{3,1,2,0:T(8,128)(2,1)} %bitcast.14), calls=%async_computation.2 | async-start | bytes 2097152 | tf_op jit(solution)/shard_map/all_to_all | solution.py:70
  186.1 1.9 copy-start.1
  191.1 20.4 %all-to-all-start.3 = ((bf16[8,32,2048]{2,1,0:T(8,128)(2,1)}), bf16[8,32,2048]{2,1,0:T(8,128)(2,1)S(1)}, u32[]{:S(2)}, u32[]{:S(2)}) async-start(bf16[8,32,2048]{2,1,0:T(8,128)(2,1)} %bitcast.18), calls=%async_computation.3 | async-start | bytes 2097152 | tf_op jit(solution)/shard_map/all_to_all | solution.py:80
  194.6 20.4 %copy-start.3 = (bf16[4,64,64]{2,1,0:T(8,128)(2,1)S(1)}, bf16[4,64,64]{2,1,0:T(8,128)(2,1)}, u32[]{:S(2)}) copy-start(bf16[4,64,64]{2,1,0:T(8,128)(2,1)} %param.11) | copy-start | bytes 98308
  211.5 19.6 %all-to-all-start.6 = ((bf16[8,32,2048]{2,1,0:T(8,128)(2,1)}), bf16[8,32,2048]{2,1,0:T(8,128)(2,1)S(1)}, u32[]{:S(2)}, u32[]{:S(2)}) async-start(bf16[8,32,2048]{2,1,0:T(8,128)(2,1)} %bitcast.36), calls=%async_computation.6 | async-start | bytes 2097152 | tf_op jit(solution)/shard_map/all_to_all | solution.py:80

commit v5 on v3

--- a/solution.py
+++ b/solution.py
@@ -4,7 +4,7 @@
 from jax.sharding import PartitionSpec as P
 
 BLOCK = 512
-CHUNKS = 2
+WIDTHS = (320, 192)
 
 
 def channel_weights(block_first, block_second, n_ch):
@@ -41,10 +41,15 @@
         twiddle_t = jnp.transpose(twiddle)
         w1t, w2 = channel_weights(block_first, block_second, n_ch)
         contract = (((1,), (1,)), ((), ()))
-        width = BLOCK // CHUNKS
-        outs = []
-        for q in range(CHUNKS):
-            lo = q * width
+        me = lax.axis_index("ch")
+        w1t_rot = jnp.take(
+            w1t.reshape(n_ch, -1, channels), (me + jnp.arange(n_ch)) % n_ch, axis=0
+        ).reshape(channels, channels)
+        w2_rot = jnp.take(
+            w2.reshape(n_ch, -1, channels), (me - jnp.arange(n_ch)) % n_ch, axis=0
+        ).reshape(channels, channels)
+
+        def seq_front(lo, width):
             first = lax.dot_general(
                 full_first[lo:lo + width],
                 token_grid,
@@ -53,24 +58,46 @@
             )
             twisted = (first * twiddle_t[lo:lo + width, :, None]).astype(jnp.bfloat16)
             gathered = lax.all_to_all(twisted, "seq", split_axis=0, concat_axis=1, tiled=True)
-            mixed = lax.dot_general(
+            return lax.dot_general(
                 full_second, gathered, contract, preferred_element_type=jnp.float32
             ).astype(jnp.bfloat16)
+
+        def seq_back(mixed, lo, width, w1):
             returned = lax.all_to_all(mixed, "seq", split_axis=0, concat_axis=1, tiled=True)
             gated = (
                 token_grid[:, lo:lo + width].astype(jnp.float32) * returned.astype(jnp.float32)
             ).astype(jnp.bfloat16)
             gated = gated.reshape(outer_rows * width, channels)
             middle_t = lax.dot_general(
-                w1t, gated, contract, preferred_element_type=jnp.float32
+                w1, gated, contract, preferred_element_type=jnp.float32
             ).astype(jnp.bfloat16)
-            middle_t = middle_t.reshape(n_ch, channels // n_ch, outer_rows * width)
-            recv = lax.all_to_all(middle_t, "ch", split_axis=0, concat_axis=0, tiled=True)
-            recv = recv.reshape(channels, outer_rows * width)
+            return middle_t.reshape(n_ch, channels // n_ch, outer_rows * width)
+
+        def channel_second(recv, w, width):
             result = lax.dot_general(
-                recv, w2, (((0,), (0,)), ((), ())), preferred_element_type=jnp.float32
+                recv.reshape(channels, outer_rows * width),
+                w,
+                (((0,), (0,)), ((), ())),
+                preferred_element_type=jnp.float32,
             ).astype(jnp.bfloat16)
-            outs.append(result.reshape(outer_rows, width, channels))
+            return result.reshape(outer_rows, width, channels)
+
+        w_a, w_b = WIDTHS
+        mixed_a = seq_front(0, w_a)
+        mixed_b = seq_front(w_a, w_b)
+        middle_a = seq_back(mixed_a, 0, w_a, w1t_rot)
+        middle_a, mixed_b = lax.optimization_barrier((middle_a, mixed_b))
+        pieces = [middle_a[0]]
+        for q in range(1, n_ch):
+            pieces.append(
+                lax.ppermute(middle_a[q], "ch", perm=[(j, (j + q) % n_ch) for j in range(n_ch)])
+            )
+        middle_b = seq_back(mixed_b, w_a, w_b, w1t)
+        recv_b = lax.all_to_all(middle_b, "ch", split_axis=0, concat_axis=0, tiled=True)
+        outs = [
+            channel_second(jnp.stack(pieces), w2_rot, w_a),
+            channel_second(recv_b, w2, w_b),
+        ]
         out = jnp.concatenate(outs, axis=1)
         return out.reshape(tok_rows, channels)
 

time: 233 us -> 256 us (1.099)
  the two profiles are of different devices: /device:TPU:24 before, /device:TPU:8 now
where the time goes in v5:
time: 256 us; the launch traced here: 255 us
  waiting for transfers between devices  130 us (51%)
  starting transfers between devices  81.3 us (32%)
  local copies, waits for them, and re-layouts  23.5 us (9%)
  matrix products  10.4 us (4%)
  other arithmetic  9.52 us (4%)
    all_to_all x2, waiting for transfers between devices, seq_front(): lax.all_to_all(twisted, 'seq', split_axis=0, concat_axis=1, tiled=True)  50.6 us
    all_to_all x2, waiting for transfers between devices, seq_back(): lax.all_to_all(mixed, 'seq', split_axis=0, concat_axis=1, tiled=True)  42.1 us
    all_to_all x2, starting transfers between devices, seq_front(): lax.all_to_all(twisted, 'seq', split_axis=0, concat_axis=1, tiled=True)  25.8 us
    ppermute x7, starting transfers between devices, local(): lax.ppermute(middle_a[q], 'ch', perm=[(j, (j + q) % n_ch) for j in range(...  22.5 us
    all_to_all x2, starting transfers between devices, seq_back(): lax.all_to_all(mixed, 'seq', split_axis=0, concat_axis=1, tiled=True)  22.1 us
    all_to_all x1, waiting for transfers between devices, local(): both = lax.all_to_all(spread, 'ch', split_axis=0, concat_axis=0, tiled=True)  15.7 us
    ppermute x7, waiting for transfers between devices, local(): lax.ppermute(middle_a[q], 'ch', perm=[(j, (j + q) % n_ch) for j in range(...  14 us
    all_to_all x1, waiting for transfers between devices, local(): lax.all_to_all(middle_b, 'ch', split_axis=0, concat_axis=0, tiled=True)  7.77 us
  transfers between devices with their start and end apart: 13, of which 7 were waited for; matrix products, arithmetic and copies ran while one was open for 12% of the time, Pallas kernels for 0%

profile of v5, /device:TPU:8, one launch (start us, length us, event | category | flops | bytes accessed | tf_op | source)
XLA Modules:
  0.0 255.3 jit_solution(12060353835933464839)
XLA Ops:
  0.0 0.9 pad_maximum_fusion.1
  0.9 1.1 broadcast_in_dim.84
  2.0 6.2 %all-to-all-start = ((bf16[8,128,512]{2,1,0:T(8,128)(2,1)}), bf16[8,128,512]{2,1,0:T(8,128)(2,1)S(1)}, u32[]{:S(2)}, u32[]{:S(2)}) async-start(bf16[8,128,512]{2,1,0:T(8,128)(2,1)} %broadcast_in_dim.84), calls=%async_computation | async-start | bytes 2097152 | tf_op jit(solution)/shard_map/all_to_all | solution.py:37
  8.2 15.7 %all-to-all-done = bf16[8,128,512]{2,1,0:T(8,128)(2,1)S(1)} async-done(((bf16[8,128,512]{2,1,0:T(8,128)(2,1)}), bf16[8,128,512]{2,1,0:T(8,128)(2,1)S(1)}, u32[]{:S(2)}, u32[]{:S(2)}) %all-to-all-start) | async-done | bytes 1048608 | tf_op jit(solution)/shard_map/all_to_all | solution.py:37
  23.9 0.9 multiply_convert_fusion
  24.8 1.8 copy.47
  26.6 15.8 %all-to-all-start.1 = ((bf16[320,8,256]{2,1,0:T(8,128)(2,1)}), bf16[320,8,256]{2,1,0:T(8,128)(2,1)}, u32[]{:S(2)}, u32[]{:S(2)}) async-start(bf16[320,8,256]{2,1,0:T(8,128)(2,1)} %copy.47), calls=%async_computation.1 | async-start | bytes 2621440 | tf_op jit(solution)/shard_map/all_to_all | solution.py:60
  43.1 1.3 copy.53
  44.4 32.2 %all-to-all-done.1 = bf16[320,8,256]{2,1,0:T(8,128)(2,1)} async-done(((bf16[320,8,256]{2,1,0:T(8,128)(2,1)}), bf16[320,8,256]{2,1,0:T(8,128)(2,1)}, u32[]{:S(2)}, u32[]{:S(2)}) %all-to-all-start.1) | async-done | bytes 1310752 | tf_op jit(solution)/shard_map/all_to_all | solution.py:60
  76.7 10.0 %all-to-all-start.3 = ((bf16[192,8,256]{2,1,0:T(8,128)(2,1)}), bf16[192,8,256]{2,1,0:T(8,128)(2,1)}, u32[]{:S(2)}, u32[]{:S(2)}) async-start(bf16[192,8,256]{2,1,0:T(8,128)(2,1)} %copy.53), calls=%async_computation.3 | async-start | bytes 1572864 | tf_op jit(solution)/shard_map/all_to_all | solution.py:60
  86.7 0.8 copy-done.2
  87.5 2.2 convolution_convert_fusion.3
  89.7 2.1 copy.49
  91.9 18.3 %all-to-all-done.3 = bf16[192,8,256]{2,1,0:T(8,128)(2,1)} async-done(((bf16[192,8,256]{2,1,0:T(8,128)(2,1)}), bf16[192,8,256]{2,1,0:T(8,128)(2,1)}, u32[]{:S(2)}, u32[]{:S(2)}) %all-to-all-start.3) | async-done | bytes 786464 | tf_op jit(solution)/shard_map/all_to_all | solution.py:60
  110.2 8.5 %all-to-all-start.2 = ((bf16[512,5,256]{2,1,0:T(8,128)(2,1)}), bf16[512,5,256]{2,1,0:T(8,128)(2,1)}, u32[]{:S(2)}, u32[]{:S(2)}) async-start(bf16[512,5,256]{2,1,0:T(8,128)(2,1)} %copy.49), calls=%async_computation.2 | async-start | bytes 4194304 | tf_op jit(solution)/shard_map/all_to_all | solution.py:66
  121.8 0.7 broadcast_select_fusion.2
  123.2 0.8 broadcast_select_fusion.1
  123.9 0.8 broadcast_select_fusion
  124.7 2.6 %convolution_convert_fusion.4 = bf16[512,3,256]{2,0,1:T(8,128)(2,1)} fusion(bf16[512,512,1]{1,0,2:T(8,128)(2,1)S(1)} %bitcast.123, bf16[3,64,8,256]{3,2,0,1:T(8,128)(2,1)} %bitcast.22), kind=kOutput, calls=%fused_computation.17 | convolution fusion | flops 403046400 | bytes 2097152 | tf_op jit(solution)/shard_map/dot_general | solution.py:61
  127.3 42.1 %all-to-all-done.2 = bf16[512,5,256]{2,1,0:T(8,128)(2,1)} async-done(((bf16[512,5,256]{2,1,0:T(8,128)(2,1)}), bf16[512,5,256]{2,1,0:T(8,128)(2,1)}, u32[]{:S(2)}, u32[]{:S(2)}) %all-to-all-start.2) | async-done | bytes 1310752 | tf_op jit(solution)/shard_map/all_to_all | solution.py:66
  169.4 1.9 convert_bitcast_fusion
  171.5 1.0 fusion.1
  173.0 1.1 slice_bitcast_fusion
  174.1 2.8 %collective-permute-start = (bf16[32,2560]{1,0:T(8,128)(2,1)}, bf16[32,2560]{1,0:T(8,128)(2,1)}, u32[]{:S(2)}, u32[]{:S(2)}) collective-permute-start(bf16[32,2560]{1,0:T(8,128)(2,1)} %get-tuple-element.16), channel_id=1, source_target_pairs={{0,1},{1,2},{2,3},{3,4},{4,5},{5,6},{6,7},{7,0},{8,9},{9,10},{10,1... | collective-permute-start | bytes 491528 | tf_op jit(solution)/shard_map/ppermute | solution.py:93
  176.9 0.9 select_n.59
  177.8 1.0 select_n.57
  178.8 1.2 gather_fusion.1
  180.0 1.6 copy.57
  181.6 13.6 %all-to-all-start.4 = ((bf16[512,3,256]{2,1,0:T(4,128)(2,1)}), bf16[512,3,256]{2,1,0:T(4,128)(2,1)S(1)}, u32[]{:S(2)}, u32[]{:S(2)}) async-start(bf16[512,3,256]{2,1,0:T(4,128)(2,1)} %copy.57), calls=%async_computation.4 | async-start | bytes 2097152 | tf_op jit(solution)/shard_map/all_to_all | solution.py:66
  195.3 4.3 %collective-permute-start.6 = (bf16[32,2560]{1,0:T(8,128)(2,1)S(1)}, bf16[32,2560]{1,0:T(8,128)(2,1)}, u32[]{:S(2)}, u32[]{:S(2)}) collective-permute-start(bf16[32,2560]{1,0:T(8,128)(2,1)S(1)} %copy-done.8), channel_id=1, source_target_pairs={{0,7},{1,0},{2,1},{3,2},{4,3},{5,4},{6,5},{7,6},{8,15},{9,8},{10,9... | collective-permute-start | bytes 491528 | tf_op jit(solution)/shard_map/ppermute | solution.py:93
  199.6 2.4 collective-permute-start.5
  202.0 3.3 %collective-permute-start.4 = (bf16[32,2560]{1,0:T(8,128)(2,1)}, bf16[32,2560]{1,0:T(8,128)(2,1)S(1)}, u32[]{:S(2)}, u32[]{:S(2)}) collective-permute-start(bf16[32,2560]{1,0:T(8,128)(2,1)} %get-tuple-element.12), channel_id=1, source_target_pairs={{0,5},{1,6},{2,7},{3,0},{4,1},{5,2},{6,3},{7,4},{8,13},{9,14},{10,... | collective-permute-start | bytes 491528 | tf_op jit(solution)/shard_map/ppermute | solution.py:93
  205.3 4.0 %collective-permute-start.3 = (bf16[32,2560]{1,0:T(8,128)(2,1)}, bf16[32,2560]{1,0:T(8,128)(2,1)S(1)}, u32[]{:S(2)}, u32[]{:S(2)}) collective-permute-start(bf16[32,2560]{1,0:T(8,128)(2,1)} %get-tuple-element.13), channel_id=1, source_target_pairs={{0,4},{1,5},{2,6},{3,7},{4,0},{5,1},{6,2},{7,3},{8,12},{9,13},{10,... | collective-permute-start | bytes 491528 | tf_op jit(solution)/shard_map/ppermute | solution.py:93
  209.3 2.6 %collective-permute-start.1 = (bf16[32,2560]{1,0:T(8,128)(2,1)}, bf16[32,2560]{1,0:T(8,128)(2,1)S(1)}, u32[]{:S(2)}, u32[]{:S(2)}) collective-permute-start(bf16[32,2560]{1,0:T(8,128)(2,1)} %get-tuple-element.15), channel_id=1, source_target_pairs={{0,2},{1,3},{2,4},{3,5},{4,6},{5,7},{6,0},{7,1},{8,10},{9,11},{10,... | collective-permute-start | bytes 491528 | tf_op jit(solution)/shard_map/ppermute | solution.py:93
  211.9 1.6 bitcast_dynamic-update-slice_fusion.6
  213.5 4.7 %collective-permute-done.1 = bf16[32,2560]{1,0:T(8,128)(2,1)S(1)} collective-permute-done((bf16[32,2560]{1,0:T(8,128)(2,1)}, bf16[32,2560]{1,0:T(8,128)(2,1)S(1)}, u32[]{:S(2)}, u32[]{:S(2)}) %collective-permute-start.1) | collective-permute-done | bytes 163872 | tf_op jit(solution)/shard_map/ppermute | solution.py:93
  218.1 3.2 %collective-permute-start.2 = (bf16[32,2560]{1,0:T(8,128)(2,1)}, bf16[32,2560]{1,0:T(8,128)(2,1)S(1)}, u32[]{:S(2)}, u32[]{:S(2)}) collective-permute-start(bf16[32,2560]{1,0:T(8,128)(2,1)} %get-tuple-element.14), channel_id=1, source_target_pairs={{0,3},{1,4},{2,5},{3,6},{4,7},{5,0},{6,1},{7,2},{8,11},{9,12},{10,... | collective-permute-start | bytes 491528 | tf_op jit(solution)/shard_map/ppermute | solution.py:93
  221.3 0.7 bitcast_dynamic-update-slice_fusion.5
  222.0 9.3 %collective-permute-done.2 = bf16[32,2560]{1,0:T(8,128)(2,1)S(1)} collective-permute-done((bf16[32,2560]{1,0:T(8,128)(2,1)}, bf16[32,2560]{1,0:T(8,128)(2,1)S(1)}, u32[]{:S(2)}, u32[]{:S(2)}) %collective-permute-start.2) | collective-permute-done | bytes 163872 | tf_op jit(solution)/shard_map/ppermute | solution.py:93
  232.0 0.7 bitcast_dynamic-update-slice_fusion.3
  232.6 0.7 bitcast_dynamic-update-slice_fusion.2
  234.5 1.3 convolution_convert_fusion.2
  235.8 4.7 %all-to-all-start.5 = ((bf16[8,32,1536]{2,1,0:T(8,128)(2,1)}), bf16[8,32,1536]{2,1,0:T(8,128)(2,1)S(1)}, u32[]{:S(2)}, u32[]{:S(2)}) async-start(bf16[8,32,1536]{2,1,0:T(8,128)(2,1)} %bitcast.46), calls=%async_computation.5 | async-start | bytes 1572864 | tf_op jit(solution)/shard_map/all_to_all | solution.py:96
  240.5 1.6 bitcast_dynamic-update-slice_fusion.1
  242.1 1.6 bitcast_dynamic-update-slice_fusion
  243.7 1.9 fusion
  245.6 7.8 %all-to-all-done.5 = bf16[8,32,1536]{2,1,0:T(8,128)(2,1)S(1)} async-done(((bf16[8,32,1536]{2,1,0:T(8,128)(2,1)}), bf16[8,32,1536]{2,1,0:T(8,128)(2,1)S(1)}, u32[]{:S(2)}, u32[]{:S(2)}) %all-to-all-start.5) | async-done | bytes 786464 | tf_op jit(solution)/shard_map/all_to_all | solution.py:96
  253.8 1.5 pad_maximum_fusion
  (73 shorter events, 7.4 us)
Async XLA Ops:
  0.9 7.3 %copy-start.13 = (f32[8,512]{1,0:T(8,128)S(1)}, f32[8,512]{1,0:T(8,128)}, u32[]{:S(2)}) copy-start(f32[8,512]{1,0:T(8,128)} %param.10) | copy-start | bytes 49156
  2.0 22.0 %copy-start = (bf16[4096,256]{1,0:T(8,128)(2,1)S(1)}, bf16[4096,256]{1,0:T(8,128)(2,1)}, u32[]{:S(2)}) copy-start(bf16[4096,256]{1,0:T(8,128)(2,1)} %param.8) | copy-start | bytes 6291460
  2.0 21.9 %all-to-all-start = ((bf16[8,128,512]{2,1,0:T(8,128)(2,1)}), bf16[8,128,512]{2,1,0:T(8,128)(2,1)S(1)}, u32[]{:S(2)}, u32[]{:S(2)}) async-start(bf16[8,128,512]{2,1,0:T(8,128)(2,1)} %broadcast_in_dim.84), calls=%async_computation | async-start | bytes 2097152 | tf_op jit(solution)/shard_map/all_to_all | solution.py:37
  26.6 50.1 %all-to-all-start.1 = ((bf16[320,8,256]{2,1,0:T(8,128)(2,1)}), bf16[320,8,256]{2,1,0:T(8,128)(2,1)}, u32[]{:S(2)}, u32[]{:S(2)}) async-start(bf16[320,8,256]{2,1,0:T(8,128)(2,1)} %copy.47), calls=%async_computation.1 | async-start | bytes 2621440 | tf_op jit(solution)/shard_map/all_to_all | solution.py:60
  76.7 33.5 %all-to-all-start.3 = ((bf16[192,8,256]{2,1,0:T(8,128)(2,1)}), bf16[192,8,256]{2,1,0:T(8,128)(2,1)}, u32[]{:S(2)}, u32[]{:S(2)}) async-start(bf16[192,8,256]{2,1,0:T(8,128)(2,1)} %copy.53), calls=%async_computation.3 | async-start | bytes 1572864 | tf_op jit(solution)/shard_map/all_to_all | solution.py:60
  86.7 0.8 copy-start.2
  91.9 27.5 %copy-start.11 = (bf16[8,32,32]{2,1,0:T(8,128)(2,1)S(1)}, bf16[8,32,32]{2,1,0:T(8,128)(2,1)}, u32[]{:S(2)}) copy-start(bf16[8,32,32]{2,1,0:T(8,128)(2,1)} %param.12) | copy-start | bytes 49156
  91.9 27.6 %copy-start.12 = (bf16[4,64,64]{2,1,0:T(8,128)(2,1)S(1)}, bf16[4,64,64]{2,1,0:T(8,128)(2,1)}, u32[]{:S(2)}) copy-start(bf16[4,64,64]{2,1,0:T(8,128)(2,1)} %param.13) | copy-start | bytes 98308
  110.2 59.2 %all-to-all-start.2 = ((bf16[512,5,256]{2,1,0:T(8,128)(2,1)}), bf16[512,5,256]{2,1,0:T(8,128)(2,1)}, u32[]{:S(2)}, u32[]{:S(2)}) async-start(bf16[512,5,256]{2,1,0:T(8,128)(2,1)} %copy.49), calls=%async_computation.2 | async-start | bytes 4194304 | tf_op jit(solution)/shard_map/all_to_all | solution.py:66
  118.7 0.5 copy-start.15
  119.2 0.6 copy-start.14
  120.2 4.5 %copy-start.3 = (bf16[8,1,64,512]{3,2,1,0:T(8,128)(2,1)S(1)}, bf16[8,1,64,512]{3,2,1,0:T(8,128)(2,1)}, u32[]{:S(2)}) copy-start(bf16[8,1,64,512]{3,2,1,0:T(8,128)(2,1)} %copy-done.2) | copy-start | bytes 1572868
  171.5 1.0 copy-start.7
  173.0 3.9 %copy-start.16 = (s32[8]{0:T(128)S(1)}, s32[8]{0:T(128)}, u32[]{:S(2)}) copy-start(s32[8]{0:T(128)} %get-tuple-element.18) | copy-start | bytes 100
  173.0 5.7 %copy-start.4 = (bf16[8,32,256]{2,1,0:T(8,128)(2,1)S(1)}, bf16[8,32,256]{2,1,0:T(8,128)(2,1)}, u32[]{:S(2)}) copy-start(bf16[8,32,256]{2,1,0:T(8,128)(2,1)} %broadcast_select_fusion.3) | copy-start | bytes 393220
  174.1 35.2 %collective-permute-start = (bf16[32,2560]{1,0:T(8,128)(2,1)}, bf16[32,2560]{1,0:T(8,128)(2,1)}, u32[]{:S(2)}, u32[]{:S(2)}) collective-permute-start(bf16[32,2560]{1,0:T(8,128)(2,1)} %get-tuple-element.16), channel_id=1, source_target_pairs={{0,1},{1,2},{2,3},{3,4},{4,5},{5,6},{6,7},{7,0},{8,9},{9,10},{10,1... | collective-permute-start | bytes 491528 | tf_op jit(solution)/shard_map/ppermute | solution.py:93
  177.8 2.2 copy-start.1
  181.6 13.6 %copy-start.8 = (bf16[32,2560]{1,0:T(8,128)(2,1)S(1)}, bf16[32,2560]{1,0:T(8,128)(2,1)}, u32[]{:S(2)}) copy-start(bf16[32,2560]{1,0:T(8,128)(2,1)} %get-tuple-element.10) | copy-start | bytes 491524
  181.6 17.9 %copy-start.9 = (bf16[32,2560]{1,0:T(8,128)(2,1)S(1)}, bf16[32,2560]{1,0:T(8,128)(2,1)}, u32[]{:S(2)}) copy-start(bf16[32,2560]{1,0:T(8,128)(2,1)} %get-tuple-element.11) | copy-start | bytes 491524
  181.6 51.7 %all-to-all-start.4 = ((bf16[512,3,256]{2,1,0:T(4,128)(2,1)}), bf16[512,3,256]{2,1,0:T(4,128)(2,1)S(1)}, u32[]{:S(2)}, u32[]{:S(2)}) async-start(bf16[512,3,256]{2,1,0:T(4,128)(2,1)} %copy.57), calls=%async_computation.4 | async-start | bytes 2097152 | tf_op jit(solution)/shard_map/all_to_all | solution.py:66
  195.3 46.8 %collective-permute-start.6 = (bf16[32,2560]{1,0:T(8,128)(2,1)S(1)}, bf16[32,2560]{1,0:T(8,128)(2,1)}, u32[]{:S(2)}, u32[]{:S(2)}) collective-permute-start(bf16[32,2560]{1,0:T(8,128)(2,1)S(1)} %copy-done.8), channel_id=1, source_target_pairs={{0,7},{1,0},{2,1},{3,2},{4,3},{5,4},{6,5},{7,6},{8,15},{9,8},{10,9... | collective-permute-start | bytes 491528 | tf_op jit(solution)/shard_map/ppermute | solution.py:93
  199.6 40.9 %collective-permute-start.5 = (bf16[32,2560]{1,0:T(8,128)(2,1)S(1)}, bf16[32,2560]{1,0:T(8,128)(2,1)}, u32[]{:S(2)}, u32[]{:S(2)}) collective-permute-start(bf16[32,2560]{1,0:T(8,128)(2,1)S(1)} %copy-done.9), channel_id=1, source_target_pairs={{0,6},{1,7},{2,0},{3,1},{4,2},{5,3},{6,4},{7,5},{8,14},{9,15},{10,... | collective-permute-start | bytes 491528 | tf_op jit(solution)/shard_map/ppermute | solution.py:93
  202.0 30.7 %collective-permute-start.4 = (bf16[32,2560]{1,0:T(8,128)(2,1)}, bf16[32,2560]{1,0:T(8,128)(2,1)S(1)}, u32[]{:S(2)}, u32[]{:S(2)}) collective-permute-start(bf16[32,2560]{1,0:T(8,128)(2,1)} %get-tuple-element.12), channel_id=1, source_target_pairs={{0,5},{1,6},{2,7},{3,0},{4,1},{5,2},{6,3},{7,4},{8,13},{9,14},{10,... | collective-permute-start | bytes 491528 | tf_op jit(solution)/shard_map/ppermute | solution.py:93
  205.3 26.7 %collective-permute-start.3 = (bf16[32,2560]{1,0:T(8,128)(2,1)}, bf16[32,2560]{1,0:T(8,128)(2,1)S(1)}, u32[]{:S(2)}, u32[]{:S(2)}) collective-permute-start(bf16[32,2560]{1,0:T(8,128)(2,1)} %get-tuple-element.13), channel_id=1, source_target_pairs={{0,4},{1,5},{2,6},{3,7},{4,0},{5,1},{6,2},{7,3},{8,12},{9,13},{10,... | collective-permute-start | bytes 491528 | tf_op jit(solution)/shard_map/ppermute | solution.py:93
  209.3 8.8 %collective-permute-start.1 = (bf16[32,2560]{1,0:T(8,128)(2,1)}, bf16[32,2560]{1,0:T(8,128)(2,1)S(1)}, u32[]{:S(2)}, u32[]{:S(2)}) collective-permute-start(bf16[32,2560]{1,0:T(8,128)(2,1)} %get-tuple-element.15), channel_id=1, source_target_pairs={{0,2},{1,3},{2,4},{3,5},{4,6},{5,7},{6,0},{7,1},{8,10},{9,11},{10,... | collective-permute-start | bytes 491528 | tf_op jit(solution)/shard_map/ppermute | solution.py:93
  218.1 13.1 %collective-permute-start.2 = (bf16[32,2560]{1,0:T(8,128)(2,1)}, bf16[32,2560]{1,0:T(8,128)(2,1)S(1)}, u32[]{:S(2)}, u32[]{:S(2)}) collective-permute-start(bf16[32,2560]{1,0:T(8,128)(2,1)} %get-tuple-element.14), channel_id=1, source_target_pairs={{0,3},{1,4},{2,5},{3,6},{4,7},{5,0},{6,1},{7,2},{8,11},{9,12},{10,... | collective-permute-start | bytes 491528 | tf_op jit(solution)/shard_map/ppermute | solution.py:93
  233.6 0.9 copy-start.6
  235.8 7.9 %copy-start.10 = (bf16[8,32,256]{2,1,0:T(8,128)(2,1)S(1)}, bf16[8,32,256]{2,1,0:T(8,128)(2,1)}, u32[]{:S(2)}) copy-start(bf16[8,32,256]{2,1,0:T(8,128)(2,1)} %gather_fusion.1) | copy-start | bytes 393220
  235.8 17.6 %all-to-all-start.5 = ((bf16[8,32,1536]{2,1,0:T(8,128)(2,1)}), bf16[8,32,1536]{2,1,0:T(8,128)(2,1)S(1)}, u32[]{:S(2)}, u32[]{:S(2)}) async-start(bf16[8,32,1536]{2,1,0:T(8,128)(2,1)} %bitcast.46), calls=%async_computation.5 | async-start | bytes 1572864 | tf_op jit(solution)/shard_map/all_to_all | solution.py:96
  243.7 9.7 %copy-start.5 = (bf16[256,256]{1,0:T(8,128)(2,1)S(1)}, bf16[256,256]{1,0:T(8,128)(2,1)}, u32[]{:S(2)}) copy-start(bf16[256,256]{1,0:T(8,128)(2,1)} %select_n.59) | copy-start | bytes 393220

commit v6 on v3

--- a/solution.py
+++ b/solution.py
@@ -4,7 +4,7 @@
 from jax.sharding import PartitionSpec as P
 
 BLOCK = 512
-CHUNKS = 2
+CHUNKS = 1
 
 
 def channel_weights(block_first, block_second, n_ch):

time: 233 us -> 206 us (0.88)
  the two profiles are of different devices: /device:TPU:24 before, /device:TPU:41 now
where the time goes in v6:
time: 206 us; the launch traced here: 205 us
  blocking collectives  91.1 us (44%)
  waiting for transfers between devices  85.2 us (41%)
  starting transfers between devices  12.9 us (6%)
  matrix products  6.89 us (3%)
  local copies, waits for them, and re-layouts  6.17 us (3%)
  other arithmetic  2.54 us (1%)
    all_to_all x1, blocking collectives, local(): lax.all_to_all(twisted, 'seq', split_axis=0, concat_axis=1, tiled=True)  70.4 us
    all_to_all x1, waiting for transfers between devices, local(): lax.all_to_all(mixed, 'seq', split_axis=0, concat_axis=1, tiled=True)  58.8 us
    all_to_all x1, waiting for transfers between devices, local(): lax.all_to_all(middle_t, 'ch', split_axis=0, concat_axis=0, tiled=True)  26.4 us
    all_to_all x1, blocking collectives, local(): both = lax.all_to_all(spread, 'ch', split_axis=0, concat_axis=0, tiled=True)  20.7 us
    all_to_all x1, starting transfers between devices, local(): lax.all_to_all(mixed, 'seq', split_axis=0, concat_axis=1, tiled=True)  9.17 us
  transfers between devices with their start and end apart: 2, of which 2 were waited for; matrix products, arithmetic and copies ran while one was open for 0% of the time, Pallas kernels for 0%

profile of v6, /device:TPU:41, one launch (start us, length us, event | category | flops | bytes accessed | tf_op | source)
XLA Modules:
  0.0 205.0 jit_solution(7616209718246362563)
XLA Ops:
  0.0 0.9 pad_maximum_fusion
  0.9 0.1 broadcast_in_dim.53
  1.0 0.0 copy-start
  1.0 0.0 copy-start.4
  1.0 20.7 %all_to_all.37 = bf16[8,128,512]{2,1,0:T(8,128)(2,1)S(1)} all-to-all(bf16[8,128,512]{2,1,0:T(8,128)(2,1)S(1)} %broadcast_in_dim.53), channel_id=1, replica_groups=mesh['seq'=64,'ch'=8] {'ch'}, dimensions={0} | all-to-all | bytes 2097152 | tf_op jit(solution)/shard_map/all_to_all | solution.py:37
  21.7 0.1 fusion.7
  21.8 0.0 copy-done
  21.8 0.0 copy-done.4
  21.9 1.5 multiply_convert_fusion
  23.3 1.2 copy.17
  24.5 70.4 %all_to_all.38 = bf16[512,8,256]{2,1,0:T(8,128)(2,1)S(1)} all-to-all(bf16[512,8,256]{2,1,0:T(8,128)(2,1)S(1)} %copy.17), channel_id=1, replica_groups=mesh['seq'=64,'ch'=8] {'seq'}, dimensions={0} | all-to-all | bytes 4194304 | tf_op jit(solution)/shard_map/all_to_all | solution.py:55
  94.9 1.3 fusion.4
  96.2 2.5 %copy.19 = bf16[512,8,256]{2,1,0:T(8,128)(2,1)} copy(bf16[512,8,256]{2,0,1:T(8,128)(2,1)S(1)} %fusion.4) | data formatting | bytes 4194304 | tf_op jit(solution)/shard_map/convert_element_type | solution.py:58
  98.7 0.0 copy-start.2
  98.7 9.2 %all-to-all-start.2 = ((bf16[512,8,256]{2,1,0:T(8,128)(2,1)}), bf16[512,8,256]{2,1,0:T(8,128)(2,1)S(1)}, u32[]{:S(2)}, u32[]{:S(2)}) async-start(bf16[512,8,256]{2,1,0:T(8,128)(2,1)} %copy.19), calls=%async_computation.2 | async-start | bytes 4194304 | tf_op jit(solution)/shard_map/all_to_all | solution.py:59
  107.9 0.0 copy-done.2
  108.0 0.1 broadcast_select_fusion
  108.1 0.4 select_n.23
  108.4 58.8 %all-to-all-done.2 = bf16[512,8,256]{2,1,0:T(8,128)(2,1)S(1)} async-done(((bf16[512,8,256]{2,1,0:T(8,128)(2,1)}), bf16[512,8,256]{2,1,0:T(8,128)(2,1)S(1)}, u32[]{:S(2)}, u32[]{:S(2)}) %all-to-all-start.2) | async-done | bytes 2097184 | tf_op jit(solution)/shard_map/all_to_all | solution.py:59
  167.2 0.5 convert_bitcast_fusion
  167.8 0.0 copy-start.1
  167.8 0.4 copy.20
  168.2 1.2 copy-done.1
  169.4 0.8 fusion
  170.2 2.1 %convolution_convert_fusion.1 = bf16[256,4096]{1,0:T(8,128)(2,1)} fusion(bf16[256,256]{1,0:T(8,128)(2,1)S(1)} %select_n.23, bf16[4096,256]{1,0:T(8,128)(2,1)S(1)} %fusion), kind=kOutput, calls=%fused_computation.1 | convolution fusion | flops 537919488 | bytes 4325376 | tf_op jit(solution)/shard_map/dot_general | solution.py:64
  172.3 0.0 copy-start.3
  172.3 3.7 %all-to-all-start.3 = ((bf16[8,32,4096]{2,1,0:T(8,128)(2,1)}), bf16[8,32,4096]{2,1,0:T(8,128)(2,1)S(1)}, u32[]{:S(2)}, u32[]{:S(2)}) async-start(bf16[8,32,4096]{2,1,0:T(8,128)(2,1)} %bitcast.47), calls=%async_computation.3 | async-start | bytes 4194304 | tf_op jit(solution)/shard_map/all_to_all | solution.py:68
  176.0 0.0 copy-done.3
  176.0 0.1 copy.21
  176.1 0.2 broadcast_select_fusion.1
  176.3 0.2 select_n.25
  176.5 26.4 %all-to-all-done.3 = bf16[8,32,4096]{2,1,0:T(8,128)(2,1)S(1)} async-done(((bf16[8,32,4096]{2,1,0:T(8,128)(2,1)}), bf16[8,32,4096]{2,1,0:T(8,128)(2,1)S(1)}, u32[]{:S(2)}, u32[]{:S(2)}) %all-to-all-start.3) | async-done | bytes 2097184 | tf_op jit(solution)/shard_map/all_to_all | solution.py:68
  203.0 2.1 %convolution_convert_fusion = bf16[4096,256]{1,0:T(8,128)(2,1)} fusion(bf16[256,4096]{1,0:T(8,128)(2,1)S(1)} %bitcast.45, bf16[256,256]{1,0:T(8,128)(2,1)S(1)} %select_n.25), kind=kOutput, calls=%fused_computation | convolution fusion | flops 537919488 | bytes 4325376 | tf_op jit(solution)/shard_map/dot_general | solution.py:70
  (3 shorter events, 0.0 us)
Async XLA Ops:
  1.0 20.9 %copy-start = (bf16[4096,256]{1,0:T(8,128)(2,1)S(1)}, bf16[4096,256]{1,0:T(8,128)(2,1)}, u32[]{:S(2)}) copy-start(bf16[4096,256]{1,0:T(8,128)(2,1)} %param.6) | copy-start | bytes 6291460
  1.0 20.9 %copy-start.4 = (f32[8,512]{1,0:T(8,128)S(1)}, f32[8,512]{1,0:T(8,128)}, u32[]{:S(2)}) copy-start(f32[8,512]{1,0:T(8,128)} %param.8) | copy-start | bytes 49156
  98.7 9.2 %copy-start.2 = (bf16[8,32,32]{2,1,0:T(8,128)(2,1)S(1)}, bf16[8,32,32]{2,1,0:T(8,128)(2,1)}, u32[]{:S(2)}) copy-start(bf16[8,32,32]{2,1,0:T(8,128)(2,1)} %param.10) | copy-start | bytes 49156
  98.7 68.5 %all-to-all-start.2 = ((bf16[512,8,256]{2,1,0:T(8,128)(2,1)}), bf16[512,8,256]{2,1,0:T(8,128)(2,1)S(1)}, u32[]{:S(2)}, u32[]{:S(2)}) async-start(bf16[512,8,256]{2,1,0:T(8,128)(2,1)} %copy.19), calls=%async_computation.2 | async-start | bytes 4194304 | tf_op jit(solution)/shard_map/all_to_all | solution.py:59
  167.8 1.6 copy-start.1
  172.3 3.7 %copy-start.3 = (bf16[4,64,64]{2,1,0:T(8,128)(2,1)S(1)}, bf16[4,64,64]{2,1,0:T(8,128)(2,1)}, u32[]{:S(2)}) copy-start(bf16[4,64,64]{2,1,0:T(8,128)(2,1)} %param.11) | copy-start | bytes 98308
  172.3 30.7 %all-to-all-start.3 = ((bf16[8,32,4096]{2,1,0:T(8,128)(2,1)}), bf16[8,32,4096]{2,1,0:T(8,128)(2,1)S(1)}, u32[]{:S(2)}, u32[]{:S(2)}) async-start(bf16[8,32,4096]{2,1,0:T(8,128)(2,1)} %bitcast.47), calls=%async_computation.3 | async-start | bytes 4194304 | tf_op jit(solution)/shard_map/all_to_all | solution.py:68

commit v7 on v6

--- a/solution.py
+++ b/solution.py
@@ -1,10 +1,11 @@
 import jax
 import jax.numpy as jnp
 from jax import lax
-from jax.sharding import PartitionSpec as P
+from jax.sharding import Mesh, PartitionSpec as P
 
 BLOCK = 512
 CHUNKS = 1
+SEQ = ("sq", "core")
 
 
 def channel_weights(block_first, block_second, n_ch):
@@ -32,12 +33,13 @@
         outer_rows = tok_rows // BLOCK
         token_grid = inputs.reshape(outer_rows, BLOCK, channels)
         rows = first_factor.shape[0]
-        pair = jnp.concatenate([first_factor, second_factor], axis=0)
-        spread = jnp.broadcast_to(pair[None], (n_ch,) + pair.shape)
-        both = lax.all_to_all(spread, "ch", split_axis=0, concat_axis=0, tiled=True)
-        both = both.reshape(n_ch, 2, rows, BLOCK)
-        full_first = both[:, 0].reshape(BLOCK, BLOCK)
-        full_second = both[:, 1].reshape(BLOCK, BLOCK)
+        core = lax.axis_index("core")
+        half = jnp.where(core == 0, first_factor, second_factor)
+        spread = jnp.broadcast_to(half[None], (n_ch,) + half.shape)
+        got = lax.all_to_all(spread, "ch", split_axis=0, concat_axis=0, tiled=True)
+        both = lax.all_gather(got.reshape(BLOCK, BLOCK), "core", axis=0)
+        full_first = both[0]
+        full_second = both[1]
         twiddle_t = jnp.transpose(twiddle)
         w1t, w2 = channel_weights(block_first, block_second, n_ch)
         contract = (((1,), (1,)), ((), ()))
@@ -52,11 +54,11 @@
                 preferred_element_type=jnp.float32,
             )
             twisted = (first * twiddle_t[lo:lo + width, :, None]).astype(jnp.bfloat16)
-            gathered = lax.all_to_all(twisted, "seq", split_axis=0, concat_axis=1, tiled=True)
+            gathered = lax.all_to_all(twisted, SEQ, split_axis=0, concat_axis=1, tiled=True)
             mixed = lax.dot_general(
                 full_second, gathered, contract, preferred_element_type=jnp.float32
             ).astype(jnp.bfloat16)
-            returned = lax.all_to_all(mixed, "seq", split_axis=0, concat_axis=1, tiled=True)
+            returned = lax.all_to_all(mixed, SEQ, split_axis=0, concat_axis=1, tiled=True)
             gated = (
                 token_grid[:, lo:lo + width].astype(jnp.float32) * returned.astype(jnp.float32)
             ).astype(jnp.bfloat16)
@@ -78,18 +80,20 @@
 
 
 def solution(mesh):
+    n_seq, n_ch = mesh.shape["seq"], mesh.shape["ch"]
+    split = Mesh(mesh.devices.reshape(n_seq // 2, 2, n_ch), SEQ + ("ch",))
     placed = (
-        P("seq", "ch"),
+        P(SEQ, "ch"),
         P("ch", None),
-        P("seq", None),
+        P(SEQ, None),
         P("ch", None),
         P("ch", None, None),
         P("ch", None, None),
     )
     return jax.shard_map(
-        make_local(mesh.shape["seq"], mesh.shape["ch"]),
-        mesh=mesh,
+        make_local(n_seq, n_ch),
+        mesh=split,
         in_specs=placed,
-        out_specs=P("seq", "ch"),
+        out_specs=P(SEQ, "ch"),
         check_vma=False,
     )

time: 206 us -> 230 us (1.12)
  waiting for transfers between devices: 85.2 us -> 104 us
  between operations: 0.18 us -> 13.5 us
  blocking collectives: 91.1 us -> 82 us
    all_gather x0 -> x1, waiting for transfers between devices: none -> 20.3 us  [local(): both = lax.all_gather(got.reshape(BLOCK, BLOCK), 'core', axis=0)]
    all_to_all x2, blocking collectives: 91.1 us -> 82 us  [the longest x1 67 us: local(): lax.all_to_all(twisted, SEQ, split_axis=0, concat_axis=1, tiled=True)]
  transfers between devices with their start and end apart: 2 -> 3, of which waited for: 2 -> 3; matrix products, arithmetic and copies ran while one was open for 0% -> 0% of each run, Pallas kernels for 0% -> 0%
where the time goes in v7:
time: 230 us; the launch traced here: 229 us
  waiting for transfers between devices  104 us (45%)
  blocking collectives  82 us (36%)
  between operations  13.5 us (6%)
  starting transfers between devices  13 us (6%)
  matrix products  7.91 us (3%)
  local copies, waits for them, and re-layouts  6.03 us (3%)
  other arithmetic  2.67 us (1%)
    all_to_all x1, blocking collectives, local(): lax.all_to_all(twisted, SEQ, split_axis=0, concat_axis=1, tiled=True)  67 us
    all_to_all x1, waiting for transfers between devices, local(): lax.all_to_all(mixed, SEQ, split_axis=0, concat_axis=1, tiled=True)  57.5 us
    all_to_all x1, waiting for transfers between devices, local(): lax.all_to_all(middle_t, 'ch', split_axis=0, concat_axis=0, tiled=True)  26.4 us
    all_gather x1, waiting for transfers between devices, local(): both = lax.all_gather(got.reshape(BLOCK, BLOCK), 'core', axis=0)  20.3 us
    all_to_all x1, blocking collectives, local(): got = lax.all_to_all(spread, 'ch', split_axis=0, concat_axis=0, tiled=True)  15 us
    all_to_all x1, starting transfers between devices, local(): lax.all_to_all(mixed, SEQ, split_axis=0, concat_axis=1, tiled=True)  9.24 us
  transfers between devices with their start and end apart: 3, of which 3 were waited for; matrix products, arithmetic and copies ran while one was open for 0% of the time, Pallas kernels for 0%

profile of v7, /device:TPU:41, one launch (start us, length us, event | category | flops | bytes accessed | tf_op | source)
XLA Modules:
  0.0 229.4 jit_solution(17220526420746609111)
XLA Ops:
  6.5 0.0 copy-start
  6.5 0.0 copy-start.5
  6.5 0.0 all-gather.2.cloned.1.call-start
  6.5 1.0 broadcast_select_fusion.2
  7.6 15.0 %all_to_all.37 = bf16[8,64,512]{2,1,0:T(8,128)(2,1)} all-to-all(bf16[8,64,512]{2,1,0:T(8,128)(2,1)S(1)} %broadcast_in_dim.53), channel_id=1, replica_groups=mesh['sq'=32,'core'=2,'ch'=8] {'ch'}, dimensions={0} | all-to-all | bytes 1048576 | tf_op jit(solution)/shard_map/all_to_all | solution.py:39
  22.6 0.0 all-gather.2.cloned.1.call-update
  22.6 20.3 %all-gather.2.cloned.1.call-done = bf16[2,512,512]{2,1,0:T(8,128)(2,1)} async-done(((bf16[1,512,512]{2,1,0:T(8,128)(2,1)}), bf16[2,512,512]{2,1,0:T(8,128)(2,1)}) %all-gather.2.cloned.1.call-update) | async-done | bytes 1048592 | tf_op jit(solution)/shard_map/all_gather | solution.py:40
  42.9 0.0 copy-done
  42.9 0.0 copy-done.5
  42.9 2.5 %multiply_convert_fusion = bf16[512,8,256]{2,0,1:T(8,128)(2,1)S(1)} fusion(bf16[8,512,256]{2,1,0:T(8,128)(2,1)S(1)} %bitcast.50, f32[512,8]{0,1:T(8,128)S(1)} %bitcast.52, bf16[2,512,512]{2,1,0:T(8,128)(2,1)} %all-gather.2.cloned.1.call-done), kind=kOutput, calls=%fused_computation.5 | convolution fusion | flops 1075838976 | bytes 4734976 | tf_op jit(solution)/shard_map/dot_general | solution.py:50
  45.4 1.2 copy.17
  46.6 0.0 copy-start.4
  46.6 67.0 %all_to_all.38 = bf16[512,8,256]{2,1,0:T(8,128)(2,1)S(1)} all-to-all(bf16[512,8,256]{2,1,0:T(8,128)(2,1)S(1)} %copy.17), channel_id=1, replica_groups=mesh['sq'=32,'core'=2,'ch'=8] {'sq','core'}, dimensions={0} | all-to-all | bytes 4194304 | tf_op jit(solution)/shard_map/all_to_all | solution.py:57
  113.7 0.0 copy-done.4
  113.7 1.3 fusion.4
  114.9 2.5 %copy.19 = bf16[512,8,256]{2,1,0:T(8,128)(2,1)} copy(bf16[512,8,256]{2,0,1:T(8,128)(2,1)S(1)} %fusion.4) | data formatting | bytes 4194304 | tf_op jit(solution)/shard_map/convert_element_type | solution.py:60
  117.4 0.0 copy-start.2
  117.4 9.2 %all-to-all-start.2 = ((bf16[512,8,256]{2,1,0:T(8,128)(2,1)}), bf16[512,8,256]{2,1,0:T(8,128)(2,1)S(1)}, u32[]{:S(2)}, u32[]{:S(2)}) async-start(bf16[512,8,256]{2,1,0:T(8,128)(2,1)} %copy.19), calls=%async_computation.2 | async-start | bytes 4194304 | tf_op jit(solution)/shard_map/all_to_all | solution.py:61
  126.7 0.0 copy-done.2
  126.7 0.1 broadcast_select_fusion
  126.9 0.4 select_n.31
  127.2 57.5 %all-to-all-done.2 = bf16[512,8,256]{2,1,0:T(8,128)(2,1)S(1)} async-done(((bf16[512,8,256]{2,1,0:T(8,128)(2,1)}), bf16[512,8,256]{2,1,0:T(8,128)(2,1)S(1)}, u32[]{:S(2)}, u32[]{:S(2)}) %all-to-all-start.2) | async-done | bytes 2097184 | tf_op jit(solution)/shard_map/all_to_all | solution.py:61
  184.8 0.5 convert_bitcast_fusion
  185.3 0.0 copy-start.1
  185.3 0.4 copy.20
  185.7 1.2 copy-done.1
  186.9 0.8 fusion
  187.7 2.1 convolution_convert_fusion.1
  189.8 0.0 copy-start.3
  189.8 3.7 %all-to-all-start.3 = ((bf16[8,32,4096]{2,1,0:T(8,128)(2,1)}), bf16[8,32,4096]{2,1,0:T(8,128)(2,1)S(1)}, u32[]{:S(2)}, u32[]{:S(2)}) async-start(bf16[8,32,4096]{2,1,0:T(8,128)(2,1)} %bitcast.47), calls=%async_computation.3 | async-start | bytes 4194304 | tf_op jit(solution)/shard_map/all_to_all | solution.py:70
  193.5 0.0 copy-done.3
  193.5 0.1 copy.21
  193.7 0.2 broadcast_select_fusion.1
  193.8 0.2 select_n.35
  194.1 26.4 %all-to-all-done.3 = bf16[8,32,4096]{2,1,0:T(8,128)(2,1)S(1)} async-done(((bf16[8,32,4096]{2,1,0:T(8,128)(2,1)}), bf16[8,32,4096]{2,1,0:T(8,128)(2,1)S(1)}, u32[]{:S(2)}, u32[]{:S(2)}) %all-to-all-start.3) | async-done | bytes 2097184 | tf_op jit(solution)/shard_map/all_to_all | solution.py:70
  220.5 2.1 convolution_convert_fusion
  (4 shorter events, 0.1 us)
Async XLA Ops:
  6.5 36.4 %copy-start = (bf16[4096,256]{1,0:T(8,128)(2,1)S(1)}, bf16[4096,256]{1,0:T(8,128)(2,1)}, u32[]{:S(2)}) copy-start(bf16[4096,256]{1,0:T(8,128)(2,1)} %param.6) | copy-start | bytes 6291460
  6.5 36.4 %copy-start.5 = (f32[8,512]{1,0:T(8,128)S(1)}, f32[8,512]{1,0:T(8,128)}, u32[]{:S(2)}) copy-start(f32[8,512]{1,0:T(8,128)} %param.8) | copy-start | bytes 49156
  6.5 36.4 %all-gather.2.cloned.1.call-start = ((), (), s32[]{:S(2)}) async-start(), calls=%async_computation.4 | async-start | bytes 1572864 | tf_op jit(solution)/shard_map/all_gather | solution.py:40
  46.6 67.0 %copy-start.4 = (bf16[2,512,512]{2,1,0:T(8,128)(2,1)S(1)}, bf16[2,512,512]{2,1,0:T(8,128)(2,1)}, u32[]{:S(2)}) copy-start(bf16[2,512,512]{2,1,0:T(8,128)(2,1)} %all-gather.2.cloned.1.call-done) | copy-start | bytes 3145732
  117.4 9.3 %copy-start.2 = (bf16[8,32,32]{2,1,0:T(8,128)(2,1)S(1)}, bf16[8,32,32]{2,1,0:T(8,128)(2,1)}, u32[]{:S(2)}) copy-start(bf16[8,32,32]{2,1,0:T(8,128)(2,1)} %param.10) | copy-start | bytes 49156
  117.4 67.3 %all-to-all-start.2 = ((bf16[512,8,256]{2,1,0:T(8,128)(2,1)}), bf16[512,8,256]{2,1,0:T(8,128)(2,1)S(1)}, u32[]{:S(2)}, u32[]{:S(2)}) async-start(bf16[512,8,256]{2,1,0:T(8,128)(2,1)} %copy.19), calls=%async_computation.2 | async-start | bytes 4194304 | tf_op jit(solution)/shard_map/all_to_all | solution.py:61
  185.3 1.6 copy-start.1
  189.8 3.7 %copy-start.3 = (bf16[4,64,64]{2,1,0:T(8,128)(2,1)S(1)}, bf16[4,64,64]{2,1,0:T(8,128)(2,1)}, u32[]{:S(2)}) copy-start(bf16[4,64,64]{2,1,0:T(8,128)(2,1)} %param.11) | copy-start | bytes 98308
  189.8 30.7 %all-to-all-start.3 = ((bf16[8,32,4096]{2,1,0:T(8,128)(2,1)}), bf16[8,32,4096]{2,1,0:T(8,128)(2,1)S(1)}, u32[]{:S(2)}, u32[]{:S(2)}) async-start(bf16[8,32,4096]{2,1,0:T(8,128)(2,1)} %bitcast.47), calls=%async_computation.3 | async-start | bytes 4194304 | tf_op jit(solution)/shard_map/all_to_all | solution.py:70
Sparse Core Ops, SparseCore 0:
  22.7 20.1 all-gather.1

commit v8 on v6

--- a/solution.py
+++ b/solution.py
@@ -1,6 +1,7 @@
 import jax
 import jax.numpy as jnp
 from jax import lax
+from jax.experimental import pallas as pl
 from jax.sharding import PartitionSpec as P
 
 BLOCK = 512
@@ -24,6 +25,32 @@
     w2 = jnp.where(eye_m, bs, jnp.zeros((), bs.dtype))
     w2 = w2.reshape(n_ch * n_m2 * a_l, n_m2 * n_p)
     return w1t, w2
+
+
+def gate_kernel(w_ref, x_ref, r_ref, o_ref):
+    srcs, _, subs, chans = r_ref.shape
+    back = r_ref[:, 0, :, :].astype(jnp.float32).reshape(srcs * subs, chans)
+    gated = (x_ref[0].astype(jnp.float32) * back).astype(jnp.bfloat16)
+    middle = lax.dot_general(
+        w_ref[...], gated, (((1,), (1,)), ((), ())), preferred_element_type=jnp.float32
+    )
+    o_ref[...] = middle.astype(o_ref.dtype)
+
+
+def gate_first(w1t, token_grid, returned):
+    outer, inner, chans = token_grid.shape
+    srcs, _, subs, _ = returned.shape
+    return pl.pallas_call(
+        gate_kernel,
+        out_shape=jax.ShapeDtypeStruct((chans, outer * inner), jnp.bfloat16),
+        grid=(outer,),
+        in_specs=[
+            pl.BlockSpec((chans, chans), lambda p: (0, 0)),
+            pl.BlockSpec((1, inner, chans), lambda p: (p, 0, 0)),
+            pl.BlockSpec((srcs, 1, subs, chans), lambda p: (0, p, 0, 0)),
+        ],
+        out_specs=pl.BlockSpec((chans, inner), lambda p: (0, p)),
+    )(w1t, token_grid, returned)
 
 
 def make_local(n_seq, n_ch):
@@ -56,14 +83,9 @@
             mixed = lax.dot_general(
                 full_second, gathered, contract, preferred_element_type=jnp.float32
             ).astype(jnp.bfloat16)
-            returned = lax.all_to_all(mixed, "seq", split_axis=0, concat_axis=1, tiled=True)
-            gated = (
-                token_grid[:, lo:lo + width].astype(jnp.float32) * returned.astype(jnp.float32)
-            ).astype(jnp.bfloat16)
-            gated = gated.reshape(outer_rows * width, channels)
-            middle_t = lax.dot_general(
-                w1t, gated, contract, preferred_element_type=jnp.float32
-            ).astype(jnp.bfloat16)
+            returned = lax.all_to_all(mixed, "seq", split_axis=0, concat_axis=0, tiled=True)
+            returned = returned.reshape(n_seq, outer_rows, width // n_seq, channels)
+            middle_t = gate_first(w1t, token_grid, returned)
             middle_t = middle_t.reshape(n_ch, channels // n_ch, outer_rows * width)
             recv = lax.all_to_all(middle_t, "ch", split_axis=0, concat_axis=0, tiled=True)
             recv = recv.reshape(channels, outer_rows * width)

time: 206 us -> 209 us (1.015)
  Pallas kernels: 0 us -> 7.09 us
    pallas_call x0 -> x1, Pallas kernels: none -> 7.09 us  [gate_first(): pl.pallas_call(gate_kernel, out_shape=jax.ShapeDtypeStruct((chans, outer...]
  transfers between devices with their start and end apart: 2 -> 2, of which waited for: 2 -> 2; matrix products, arithmetic and copies ran while one was open for 0% -> 1% of each run, Pallas kernels for 0% -> 0%
where the time goes in v8:
time: 209 us; the launch traced here: 208 us
  blocking collectives  91.1 us (44%)
  waiting for transfers between devices  84.6 us (40%)
  starting transfers between devices  12.9 us (6%)
  Pallas kernels  7.09 us (3%)
  local copies, waits for them, and re-layouts  6.57 us (3%)
  matrix products  4.82 us (2%)
    all_to_all x1, blocking collectives, local(): lax.all_to_all(twisted, 'seq', split_axis=0, concat_axis=1, tiled=True)  70.4 us
    all_to_all x1, waiting for transfers between devices, local(): lax.all_to_all(mixed, 'seq', split_axis=0, concat_axis=0, tiled=True)  58.1 us
    all_to_all x1, waiting for transfers between devices, local(): lax.all_to_all(middle_t, 'ch', split_axis=0, concat_axis=0, tiled=True)  26.4 us
    all_to_all x1, blocking collectives, local(): both = lax.all_to_all(spread, 'ch', split_axis=0, concat_axis=0, tiled=True)  20.7 us
    all_to_all x1, starting transfers between devices, local(): lax.all_to_all(mixed, 'seq', split_axis=0, concat_axis=0, tiled=True)  9.17 us
    pallas_call x1, Pallas kernels, gate_first(): pl.pallas_call(gate_kernel, out_shape=jax.ShapeDtypeStruct((chans, outer...  7.09 us
  transfers between devices with their start and end apart: 2, of which 2 were waited for; matrix products, arithmetic and copies ran while one was open for 1% of the time, Pallas kernels for 0%

profile of v8, /device:TPU:41, one launch (start us, length us, event | category | flops | bytes accessed | tf_op | source)
XLA Modules:
  0.0 208.4 jit_solution(2727597002108022103)
XLA Ops:
  0.0 0.9 pad_maximum_fusion
  0.9 0.1 broadcast_in_dim.53
  1.0 0.0 copy-start.1
  1.0 0.0 copy-start.4
  1.0 20.7 %all_to_all.33 = bf16[8,128,512]{2,1,0:T(8,128)(2,1)S(1)} all-to-all(bf16[8,128,512]{2,1,0:T(8,128)(2,1)S(1)} %broadcast_in_dim.53), channel_id=1, replica_groups=mesh['seq'=64,'ch'=8] {'ch'}, dimensions={0} | all-to-all | bytes 2097152 | tf_op jit(solution)/shard_map/all_to_all | solution.py:64
  21.7 0.1 fusion.6
  21.8 0.0 copy-done.1
  21.8 0.0 copy-done.4
  21.9 1.5 multiply_convert_fusion
  23.3 1.2 copy.17
  24.5 70.4 %all_to_all.34 = bf16[512,8,256]{2,1,0:T(8,128)(2,1)S(1)} all-to-all(bf16[512,8,256]{2,1,0:T(8,128)(2,1)S(1)} %copy.17), channel_id=1, replica_groups=mesh['seq'=64,'ch'=8] {'seq'}, dimensions={0} | all-to-all | bytes 4194304 | tf_op jit(solution)/shard_map/all_to_all | solution.py:82
  94.9 1.3 fusion.3
  96.2 2.5 %copy.19 = bf16[512,8,256]{2,1,0:T(8,128)(2,1)} copy(bf16[512,8,256]{2,0,1:T(8,128)(2,1)S(1)} %fusion.3) | data formatting | bytes 4194304 | tf_op jit(solution)/shard_map/convert_element_type | solution.py:85
  98.7 0.0 copy-start.2
  98.7 9.2 %all-to-all-start.2 = ((bf16[512,8,256]{2,1,0:T(8,128)(2,1)}), bf16[512,8,256]{2,1,0:T(8,128)(2,1)S(1)}, u32[]{:S(2)}, u32[]{:S(2)}) async-start(bf16[512,8,256]{2,1,0:T(8,128)(2,1)} %copy.19), calls=%async_computation.2 | async-start | bytes 4194304 | tf_op jit(solution)/shard_map/all_to_all | solution.py:86
  107.9 0.0 copy-done.2
  108.0 0.1 broadcast_select_fusion
  108.1 1.0 select_n.23.w_ref
  109.1 58.1 %all-to-all-done.2 = bf16[512,8,256]{2,1,0:T(8,128)(2,1)S(1)} async-done(((bf16[512,8,256]{2,1,0:T(8,128)(2,1)}), bf16[512,8,256]{2,1,0:T(8,128)(2,1)S(1)}, u32[]{:S(2)}, u32[]{:S(2)}) %all-to-all-start.2) | async-done | bytes 2097184 | tf_op jit(solution)/shard_map/all_to_all | solution.py:86
  167.2 0.0 copy-start
  167.2 1.3 copy-done
  168.6 7.1 %shard_map.64 = bf16[256,4096]{1,0:T(8,128)(2,1)} custom-call(bf16[256,256]{1,0:T(8,128)(2,1)} %select_n.23.w_ref, bf16[8,512,256]{2,1,0:T(8,128)(2,1)} %bitcast.40, bf16[64,8,8,256]{3,2,1,0:T(8,128)(2,1)} %bitcast.37), custom_call_target="tpu_custom_call" | custom-call | tf_op jit(solution)/shard_map/pallas_call | solution.py:43
  175.6 0.0 copy-start.3
  175.6 3.7 %all-to-all-start.3 = ((bf16[8,32,4096]{2,1,0:T(8,128)(2,1)}), bf16[8,32,4096]{2,1,0:T(8,128)(2,1)S(1)}, u32[]{:S(2)}, u32[]{:S(2)}) async-start(bf16[8,32,4096]{2,1,0:T(8,128)(2,1)} %bitcast.38), calls=%async_computation.3 | async-start | bytes 4194304 | tf_op jit(solution)/shard_map/all_to_all | solution.py:90
  179.4 0.0 copy-done.3
  179.4 0.1 copy.20
  179.5 0.2 broadcast_select_fusion.1
  179.7 0.2 select_n.25
  179.9 26.4 %all-to-all-done.3 = bf16[8,32,4096]{2,1,0:T(8,128)(2,1)S(1)} async-done(((bf16[8,32,4096]{2,1,0:T(8,128)(2,1)}), bf16[8,32,4096]{2,1,0:T(8,128)(2,1)S(1)}, u32[]{:S(2)}, u32[]{:S(2)}) %all-to-all-start.3) | async-done | bytes 2097184 | tf_op jit(solution)/shard_map/all_to_all | solution.py:90
  206.3 2.1 convolution_convert_fusion
  (3 shorter events, 0.0 us)
Async XLA Ops:
  1.0 20.9 %copy-start.1 = (bf16[4096,256]{1,0:T(8,128)(2,1)S(1)}, bf16[4096,256]{1,0:T(8,128)(2,1)}, u32[]{:S(2)}) copy-start(bf16[4096,256]{1,0:T(8,128)(2,1)} %param.6) | copy-start | bytes 6291460
  1.0 20.9 %copy-start.4 = (f32[8,512]{1,0:T(8,128)S(1)}, f32[8,512]{1,0:T(8,128)}, u32[]{:S(2)}) copy-start(f32[8,512]{1,0:T(8,128)} %param.8) | copy-start | bytes 49156
  98.7 9.2 %copy-start.2 = (bf16[8,32,32]{2,1,0:T(8,128)(2,1)S(1)}, bf16[8,32,32]{2,1,0:T(8,128)(2,1)}, u32[]{:S(2)}) copy-start(bf16[8,32,32]{2,1,0:T(8,128)(2,1)} %param.10) | copy-start | bytes 49156
  98.7 68.5 %all-to-all-start.2 = ((bf16[512,8,256]{2,1,0:T(8,128)(2,1)}), bf16[512,8,256]{2,1,0:T(8,128)(2,1)S(1)}, u32[]{:S(2)}, u32[]{:S(2)}) async-start(bf16[512,8,256]{2,1,0:T(8,128)(2,1)} %copy.19), calls=%async_computation.2 | async-start | bytes 4194304 | tf_op jit(solution)/shard_map/all_to_all | solution.py:86
  167.2 1.3 copy-start
  175.6 3.7 %copy-start.3 = (bf16[4,64,64]{2,1,0:T(8,128)(2,1)S(1)}, bf16[4,64,64]{2,1,0:T(8,128)(2,1)}, u32[]{:S(2)}) copy-start(bf16[4,64,64]{2,1,0:T(8,128)(2,1)} %param.11) | copy-start | bytes 98308
  175.6 30.7 %all-to-all-start.3 = ((bf16[8,32,4096]{2,1,0:T(8,128)(2,1)}), bf16[8,32,4096]{2,1,0:T(8,128)(2,1)S(1)}, u32[]{:S(2)}, u32[]{:S(2)}) async-start(bf16[8,32,4096]{2,1,0:T(8,128)(2,1)} %bitcast.38), calls=%async_computation.3 | async-start | bytes 4194304 | tf_op jit(solution)/shard_map/all_to_all | solution.py:90

commit v9 on v6

--- a/solution.py
+++ b/solution.py
@@ -1,6 +1,7 @@
 import jax
 import jax.numpy as jnp
 from jax import lax
+from jax.experimental import pallas as pl
 from jax.sharding import PartitionSpec as P
 
 BLOCK = 512
@@ -26,6 +27,39 @@
     return w1t, w2
 
 
+def first_kernel(f_ref, x_ref, tw_ref, o_ref):
+    tw = tw_ref[...]
+    for i in range(x_ref.shape[0]):
+        acc = jnp.dot(f_ref[...], x_ref[i], preferred_element_type=jnp.float32)
+        o_ref[:, i, :] = (acc * tw[:, i:i + 1]).astype(o_ref.dtype)
+
+
+def first_twisted(full_first, token_grid, twiddle_t):
+    outer, inner, chans = token_grid.shape
+    rows = full_first.shape[0]
+    return pl.pallas_call(
+        first_kernel,
+        out_shape=jax.ShapeDtypeStruct((rows, outer, chans), jnp.bfloat16),
+    )(full_first, token_grid, twiddle_t)
+
+
+def second_kernel(s_ref, g_ref, o_ref):
+    srcs, subs, inner, chans = g_ref.shape
+    for k in range(subs):
+        g = g_ref[:, k, :, :].astype(jnp.float32).reshape(srcs * inner, chans)
+        acc = jnp.dot(s_ref[...], g.astype(jnp.bfloat16), preferred_element_type=jnp.float32)
+        o_ref[:, k, :] = acc.astype(o_ref.dtype)
+
+
+def second_mixed(full_second, gathered):
+    srcs, subs, inner, chans = gathered.shape
+    rows = full_second.shape[0]
+    return pl.pallas_call(
+        second_kernel,
+        out_shape=jax.ShapeDtypeStruct((rows, subs, chans), jnp.bfloat16),
+    )(full_second, gathered)
+
+
 def make_local(n_seq, n_ch):
     def local(inputs, first_factor, twiddle, second_factor, block_first, block_second):
         tok_rows, channels = inputs.shape
@@ -45,17 +79,10 @@
         outs = []
         for q in range(CHUNKS):
             lo = q * width
-            first = lax.dot_general(
-                full_first[lo:lo + width],
-                token_grid,
-                contract,
-                preferred_element_type=jnp.float32,
-            )
-            twisted = (first * twiddle_t[lo:lo + width, :, None]).astype(jnp.bfloat16)
-            gathered = lax.all_to_all(twisted, "seq", split_axis=0, concat_axis=1, tiled=True)
-            mixed = lax.dot_general(
-                full_second, gathered, contract, preferred_element_type=jnp.float32
-            ).astype(jnp.bfloat16)
+            twisted = first_twisted(full_first[lo:lo + width], token_grid, twiddle_t)
+            gathered = lax.all_to_all(twisted, "seq", split_axis=0, concat_axis=0, tiled=True)
+            gathered = gathered.reshape(n_seq, width // n_seq, outer_rows, channels)
+            mixed = second_mixed(full_second, gathered)
             returned = lax.all_to_all(mixed, "seq", split_axis=0, concat_axis=1, tiled=True)
             gated = (
                 token_grid[:, lo:lo + width].astype(jnp.float32) * returned.astype(jnp.float32)

time: 206 us -> 213 us (1.034)
  blocking collectives: 91.1 us -> 74.5 us
  Pallas kernels: 0 us -> 13.4 us
  starting transfers between devices: 12.9 us -> 20.3 us
  waiting for transfers between devices: 85.2 us -> 92.2 us
  matrix products: 6.89 us -> 4.15 us
    all_to_all x2 -> x1, blocking collectives: 91.1 us -> 74.5 us  [local(): lax.all_to_all(twisted, 'seq', split_axis=0, concat_axis=0, tiled=True)]
    all_to_all x0 -> x1, waiting for transfers between devices: none -> 13.7 us  [local(): both = lax.all_to_all(spread, 'ch', split_axis=0, concat_axis=0, tiled=True)]
    pallas_call x0 -> x2, Pallas kernels: none -> 13.4 us  [the longest x1 6.75 us: second_mixed(): pl.pallas_call(second_kernel, out_shape=jax.ShapeDtypeStruct((rows, subs,...]
    all_to_all x1, waiting for transfers between devices: 58.8 us -> 51.5 us  [local(): lax.all_to_all(mixed, 'seq', split_axis=0, concat_axis=1, tiled=True)]
    all_to_all x0 -> x1, starting transfers between devices: none -> 5.83 us  [local(): both = lax.all_to_all(spread, 'ch', split_axis=0, concat_axis=0, tiled=True)]
    convert_element_type x2 -> x0, local copies, waits for them, and re-layouts: 3.7 us -> none  [the longest x1 2.51 us: local(): mixed = lax.dot_general(full_second, gathered, contract, preferred_elemen...]
    dot_general x2 -> x0, matrix products: 2.74 us -> none  [the longest x1 1.48 us: local(): lax.dot_general(full_first[lo:lo + width], token_grid, contract, preferre...]
  transfers between devices with their start and end apart: 2 -> 3, of which waited for: 2 -> 3; matrix products, arithmetic and copies ran while one was open for 0% -> 1% of each run, Pallas kernels for 0% -> 0%
where the time goes in v9:
time: 213 us; the launch traced here: 212 us
  waiting for transfers between devices  92.2 us (43%)
  blocking collectives  74.5 us (35%)
  starting transfers between devices  20.3 us (10%)
  Pallas kernels  13.4 us (6%)
  local copies, waits for them, and re-layouts  5.29 us (2%)
  matrix products  4.15 us (2%)
  other arithmetic  2.56 us (1%)
    all_to_all x1, blocking collectives, local(): lax.all_to_all(twisted, 'seq', split_axis=0, concat_axis=0, tiled=True)  74.5 us
    all_to_all x1, waiting for transfers between devices, local(): lax.all_to_all(mixed, 'seq', split_axis=0, concat_axis=1, tiled=True)  51.5 us
    all_to_all x1, waiting for transfers between devices, local(): lax.all_to_all(middle_t, 'ch', split_axis=0, concat_axis=0, tiled=True)  27 us
    all_to_all x1, waiting for transfers between devices, local(): both = lax.all_to_all(spread, 'ch', split_axis=0, concat_axis=0, tiled=True)  13.7 us
    all_to_all x1, starting transfers between devices, local(): lax.all_to_all(mixed, 'seq', split_axis=0, concat_axis=1, tiled=True)  8.79 us
    pallas_call x1, Pallas kernels, second_mixed(): pl.pallas_call(second_kernel, out_shape=jax.ShapeDtypeStruct((rows, subs,...  6.75 us
    pallas_call x1, Pallas kernels, first_twisted(): pl.pallas_call(first_kernel, out_shape=jax.ShapeDtypeStruct((rows, outer,...  6.6 us
    all_to_all x1, starting transfers between devices, local(): both = lax.all_to_all(spread, 'ch', split_axis=0, concat_axis=0, tiled=True)  5.83 us
  transfers between devices with their start and end apart: 3, of which 3 were waited for; matrix products, arithmetic and copies ran while one was open for 1% of the time, Pallas kernels for 0%

profile of v9, /device:TPU:41, one launch (start us, length us, event | category | flops | bytes accessed | tf_op | source)
XLA Modules:
  0.0 212.4 jit_solution(3370503871206170505)
XLA Ops:
  0.0 0.0 copy-start.3
  0.0 0.9 pad_maximum_fusion
  0.9 1.1 broadcast_in_dim.52
  2.0 5.8 %all-to-all-start = ((bf16[8,128,512]{2,1,0:T(8,128)(2,1)}), bf16[8,128,512]{2,1,0:T(8,128)(2,1)S(1)}, u32[]{:S(2)}, u32[]{:S(2)}) async-start(bf16[8,128,512]{2,1,0:T(8,128)(2,1)} %broadcast_in_dim.52), calls=%async_computation | async-start | bytes 2097152 | tf_op jit(solution)/shard_map/all_to_all | solution.py:71
  7.8 0.0 copy-done.3
  7.8 0.8 copy.12
  8.6 13.7 %all-to-all-done = bf16[8,128,512]{2,1,0:T(8,128)(2,1)S(1)} async-done(((bf16[8,128,512]{2,1,0:T(8,128)(2,1)}), bf16[8,128,512]{2,1,0:T(8,128)(2,1)S(1)}, u32[]{:S(2)}, u32[]{:S(2)}) %all-to-all-start) | async-done | bytes 1048608 | tf_op jit(solution)/shard_map/all_to_all | solution.py:71
  22.3 1.1 fusion.1
  23.5 6.6 %shard_map.64 = bf16[512,8,256]{2,1,0:T(8,128)(2,1)} custom-call(bf16[512,512]{1,0:T(8,128)(2,1)} %bitcast.38, bf16[8,512,256]{2,1,0:T(8,128)(2,1)} %bitcast.35, f32[512,8]{1,0:T(8,128)} %bitcast.39), custom_call_target="tpu_custom_call" | custom-call | tf_op jit(solution)/shard_map/pallas_call | solution.py:40
  30.1 74.5 %all_to_all.24 = bf16[512,8,256]{2,1,0:T(8,128)(2,1)} all-to-all(bf16[512,8,256]{2,1,0:T(8,128)(2,1)} %shard_map.64), channel_id=1, replica_groups=mesh['seq'=64,'ch'=8] {'seq'}, dimensions={0} | all-to-all | bytes 4194304 | tf_op jit(solution)/shard_map/all_to_all | solution.py:83
  104.5 6.8 %shard_map.65 = bf16[512,8,256]{2,1,0:T(8,128)(2,1)} custom-call(bf16[512,512]{1,0:T(8,128)(2,1)} %bitcast.37, bf16[64,8,8,256]{3,2,1,0:T(8,128)(2,1)} %bitcast.34), custom_call_target="tpu_custom_call" | custom-call | tf_op jit(solution)/shard_map/pallas_call | solution.py:57
  111.3 0.0 copy-start.1
  111.3 8.8 %all-to-all-start.2 = ((bf16[512,8,256]{2,1,0:T(8,128)(2,1)}), bf16[512,8,256]{2,1,0:T(8,128)(2,1)S(1)}, u32[]{:S(2)}, u32[]{:S(2)}) async-start(bf16[512,8,256]{2,1,0:T(8,128)(2,1)} %shard_map.65), calls=%async_computation.2 | async-start | bytes 4194304 | tf_op jit(solution)/shard_map/all_to_all | solution.py:86
  120.1 0.0 copy-done.1
  120.1 0.1 broadcast_select_fusion
  120.3 0.4 select_n.23
  120.6 51.5 %all-to-all-done.2 = bf16[512,8,256]{2,1,0:T(8,128)(2,1)S(1)} async-done(((bf16[512,8,256]{2,1,0:T(8,128)(2,1)}), bf16[512,8,256]{2,1,0:T(8,128)(2,1)S(1)}, u32[]{:S(2)}, u32[]{:S(2)}) %all-to-all-start.2) | async-done | bytes 2097184 | tf_op jit(solution)/shard_map/all_to_all | solution.py:86
  172.1 0.5 convert_bitcast_fusion
  172.6 0.0 copy-start
  172.7 0.4 copy.13
  173.0 1.2 copy-done
  174.2 0.8 fusion
  175.0 2.1 convolution_convert_fusion.1
  177.1 0.0 copy-start.2
  177.1 5.7 %all-to-all-start.3 = ((bf16[8,32,4096]{2,1,0:T(8,128)(2,1)}), bf16[8,32,4096]{2,1,0:T(8,128)(2,1)S(1)}, u32[]{:S(2)}, u32[]{:S(2)}) async-start(bf16[8,32,4096]{2,1,0:T(8,128)(2,1)} %bitcast.33), calls=%async_computation.3 | async-start | bytes 4194304 | tf_op jit(solution)/shard_map/all_to_all | solution.py:95
  182.8 0.0 copy-done.2
  182.8 0.1 copy.14
  183.0 0.2 broadcast_select_fusion.1
  183.2 0.2 select_n.25
  183.4 27.0 %all-to-all-done.3 = bf16[8,32,4096]{2,1,0:T(8,128)(2,1)S(1)} async-done(((bf16[8,32,4096]{2,1,0:T(8,128)(2,1)}), bf16[8,32,4096]{2,1,0:T(8,128)(2,1)S(1)}, u32[]{:S(2)}, u32[]{:S(2)}) %all-to-all-start.3) | async-done | bytes 2097184 | tf_op jit(solution)/shard_map/all_to_all | solution.py:95
  210.3 2.1 convolution_convert_fusion
  (3 shorter events, 0.0 us)
Async XLA Ops:
  0.0 7.8 %copy-start.3 = (f32[8,512]{1,0:T(8,128)S(1)}, f32[8,512]{1,0:T(8,128)}, u32[]{:S(2)}) copy-start(f32[8,512]{1,0:T(8,128)} %param.8) | copy-start | bytes 49156
  2.0 20.4 %all-to-all-start = ((bf16[8,128,512]{2,1,0:T(8,128)(2,1)}), bf16[8,128,512]{2,1,0:T(8,128)(2,1)S(1)}, u32[]{:S(2)}, u32[]{:S(2)}) async-start(bf16[8,128,512]{2,1,0:T(8,128)(2,1)} %broadcast_in_dim.52), calls=%async_computation | async-start | bytes 2097152 | tf_op jit(solution)/shard_map/all_to_all | solution.py:71
  111.3 8.8 %copy-start.1 = (bf16[8,32,32]{2,1,0:T(8,128)(2,1)S(1)}, bf16[8,32,32]{2,1,0:T(8,128)(2,1)}, u32[]{:S(2)}) copy-start(bf16[8,32,32]{2,1,0:T(8,128)(2,1)} %param.10) | copy-start | bytes 49156
  111.3 60.8 %all-to-all-start.2 = ((bf16[512,8,256]{2,1,0:T(8,128)(2,1)}), bf16[512,8,256]{2,1,0:T(8,128)(2,1)S(1)}, u32[]{:S(2)}, u32[]{:S(2)}) async-start(bf16[512,8,256]{2,1,0:T(8,128)(2,1)} %shard_map.65), calls=%async_computation.2 | async-start | bytes 4194304 | tf_op jit(solution)/shard_map/all_to_all | solution.py:86
  172.6 1.6 copy-start
  177.1 5.7 %copy-start.2 = (bf16[4,64,64]{2,1,0:T(8,128)(2,1)S(1)}, bf16[4,64,64]{2,1,0:T(8,128)(2,1)}, u32[]{:S(2)}) copy-start(bf16[4,64,64]{2,1,0:T(8,128)(2,1)} %param.11) | copy-start | bytes 98308
  177.1 33.2 %all-to-all-start.3 = ((bf16[8,32,4096]{2,1,0:T(8,128)(2,1)}), bf16[8,32,4096]{2,1,0:T(8,128)(2,1)S(1)}, u32[]{:S(2)}, u32[]{:S(2)}) async-start(bf16[8,32,4096]{2,1,0:T(8,128)(2,1)} %bitcast.33), calls=%async_computation.3 | async-start | bytes 4194304 | tf_op jit(solution)/shard_map/all_to_all | solution.py:95

commit v10 on v6

--- a/solution.py
+++ b/solution.py
@@ -39,6 +39,7 @@
         full_first = both[:, 0].reshape(BLOCK, BLOCK)
         full_second = both[:, 1].reshape(BLOCK, BLOCK)
         twiddle_t = jnp.transpose(twiddle)
+        token_f32 = lax.optimization_barrier(token_grid.astype(jnp.float32))
         w1t, w2 = channel_weights(block_first, block_second, n_ch)
         contract = (((1,), (1,)), ((), ()))
         width = BLOCK // CHUNKS
@@ -58,7 +59,7 @@
             ).astype(jnp.bfloat16)
             returned = lax.all_to_all(mixed, "seq", split_axis=0, concat_axis=1, tiled=True)
             gated = (
-                token_grid[:, lo:lo + width].astype(jnp.float32) * returned.astype(jnp.float32)
+                token_f32[:, lo:lo + width] * returned.astype(jnp.float32)
             ).astype(jnp.bfloat16)
             gated = gated.reshape(outer_rows * width, channels)
             middle_t = lax.dot_general(

time: 206 us -> 205 us (level)
  other arithmetic: 2.54 us -> 7.85 us
  waiting for transfers between devices: 85.2 us -> 81.3 us
    convert_element_type x2, other arithmetic: 1.35 us -> 6.65 us  [the longest x1 3.94 us: local(): token_f32 = lax.optimization_barrier(token_grid.astype(jnp.float32))]
    all_to_all x1, waiting for transfers between devices: 58.8 us -> 54.9 us  [local(): lax.all_to_all(mixed, 'seq', split_axis=0, concat_axis=1, tiled=True)]
  transfers between devices with their start and end apart: 2 -> 2, of which waited for: 2 -> 2; matrix products, arithmetic and copies ran while one was open for 0% -> 2% of each run, Pallas kernels for 0% -> 0%
where the time goes in v10:
time: 205 us
  blocking collectives  91.1 us (44%)
  waiting for transfers between devices  81.3 us (40%)
  starting transfers between devices  12.8 us (6%)
  other arithmetic  7.85 us (4%)
  matrix products  6.88 us (3%)
  local copies, waits for them, and re-layouts  4.59 us (2%)
    all_to_all x1, blocking collectives, local(): lax.all_to_all(twisted, 'seq', split_axis=0, concat_axis=1, tiled=True)  70.4 us
    all_to_all x1, waiting for transfers between devices, local(): lax.all_to_all(mixed, 'seq', split_axis=0, concat_axis=1, tiled=True)  54.9 us
    all_to_all x1, waiting for transfers between devices, local(): lax.all_to_all(middle_t, 'ch', split_axis=0, concat_axis=0, tiled=True)  26.4 us
    all_to_all x1, blocking collectives, local(): both = lax.all_to_all(spread, 'ch', split_axis=0, concat_axis=0, tiled=True)  20.7 us
    all_to_all x1, starting transfers between devices, local(): lax.all_to_all(mixed, 'seq', split_axis=0, concat_axis=1, tiled=True)  9.04 us
  transfers between devices with their start and end apart: 2, of which 2 were waited for; matrix products, arithmetic and copies ran while one was open for 2% of the time, Pallas kernels for 0%

profile of v10, /device:TPU:41, one launch (start us, length us, event | category | flops | bytes accessed | tf_op | source)
XLA Modules:
  0.0 204.7 jit_solution(14131549622757158093)
XLA Ops:
  0.0 0.9 pad_maximum_fusion
  0.9 0.1 broadcast_in_dim.53
  1.0 0.0 copy-start
  1.0 0.0 copy-start.3
  1.0 20.7 %all_to_all.37 = bf16[8,128,512]{2,1,0:T(8,128)(2,1)S(1)} all-to-all(bf16[8,128,512]{2,1,0:T(8,128)(2,1)S(1)} %broadcast_in_dim.53), channel_id=1, replica_groups=mesh['seq'=64,'ch'=8] {'ch'}, dimensions={0} | all-to-all | bytes 2097152 | tf_op jit(solution)/shard_map/all_to_all | solution.py:37
  21.7 0.1 fusion.7
  21.8 0.0 copy-done
  21.8 0.0 copy-done.3
  21.9 1.5 multiply_convert_fusion
  23.3 1.2 copy.17
  24.5 70.4 %all_to_all.38 = bf16[512,8,256]{2,1,0:T(8,128)(2,1)S(1)} all-to-all(bf16[512,8,256]{2,1,0:T(8,128)(2,1)S(1)} %copy.17), channel_id=1, replica_groups=mesh['seq'=64,'ch'=8] {'seq'}, dimensions={0} | all-to-all | bytes 4194304 | tf_op jit(solution)/shard_map/all_to_all | solution.py:56
  94.9 1.3 fusion.4
  96.2 2.5 %copy.19 = bf16[512,8,256]{2,1,0:T(8,128)(2,1)} copy(bf16[512,8,256]{2,0,1:T(8,128)(2,1)S(1)} %fusion.4) | data formatting | bytes 4194304 | tf_op jit(solution)/shard_map/convert_element_type | solution.py:59
  98.7 9.0 %all-to-all-start.2 = ((bf16[512,8,256]{2,1,0:T(8,128)(2,1)}), bf16[512,8,256]{2,1,0:T(8,128)(2,1)S(1)}, u32[]{:S(2)}, u32[]{:S(2)}) async-start(bf16[512,8,256]{2,1,0:T(8,128)(2,1)} %copy.19), calls=%async_computation.2 | async-start | bytes 4194304 | tf_op jit(solution)/shard_map/all_to_all | solution.py:60
  107.8 0.0 copy-start.1
  107.8 3.9 %convert_element_type.30 = f32[8,512,256]{2,1,0:T(8,128)} convert(bf16[8,512,256]{2,1,0:T(8,128)(2,1)} %bitcast.52) | non-fusion elementwise | flops 1048576 | bytes 6291456 | tf_op jit(solution)/shard_map/convert_element_type | solution.py:42
  111.7 0.0 copy-done.1
  111.8 0.1 broadcast_select_fusion
  111.9 0.4 select_n.29
  112.2 54.9 %all-to-all-done.2 = bf16[512,8,256]{2,1,0:T(8,128)(2,1)S(1)} async-done(((bf16[512,8,256]{2,1,0:T(8,128)(2,1)}), bf16[512,8,256]{2,1,0:T(8,128)(2,1)S(1)}, u32[]{:S(2)}, u32[]{:S(2)}) %all-to-all-start.2) | async-done | bytes 2097184 | tf_op jit(solution)/shard_map/all_to_all | solution.py:60
  167.1 2.7 %fusion = bf16[8,512,256]{2,1,0:T(8,128)(2,1)S(1)} fusion(f32[8,512,256]{2,1,0:T(8,128)} %convert_element_type.30, bf16[64,8,8,256]{3,2,1,0:T(8,128)(2,1)S(1)} %bitcast.49), kind=kLoop, calls=%fused_computation.4 | loop fusion | flops 3145728 | bytes 8388608 | tf_op jit(solution)/shard_map/convert_element_type | solution.py:63
  169.8 2.1 %convolution_convert_fusion.1 = bf16[256,4096]{1,0:T(8,128)(2,1)} fusion(bf16[256,256]{1,0:T(8,128)(2,1)S(1)} %select_n.29, bf16[4096,256]{1,0:T(8,128)(2,1)S(1)} %bitcast.50), kind=kOutput, calls=%fused_computation.1 | convolution fusion | flops 537919488 | bytes 4325376 | tf_op jit(solution)/shard_map/dot_general | solution.py:65
  171.9 0.0 copy-start.2
  171.9 3.7 %all-to-all-start.3 = ((bf16[8,32,4096]{2,1,0:T(8,128)(2,1)}), bf16[8,32,4096]{2,1,0:T(8,128)(2,1)S(1)}, u32[]{:S(2)}, u32[]{:S(2)}) async-start(bf16[8,32,4096]{2,1,0:T(8,128)(2,1)} %bitcast.48), calls=%async_computation.3 | async-start | bytes 4194304 | tf_op jit(solution)/shard_map/all_to_all | solution.py:69
  175.6 0.0 copy-done.2
  175.6 0.1 copy.21
  175.8 0.2 broadcast_select_fusion.1
  176.0 0.2 select_n.31
  176.2 26.4 %all-to-all-done.3 = bf16[8,32,4096]{2,1,0:T(8,128)(2,1)S(1)} async-done(((bf16[8,32,4096]{2,1,0:T(8,128)(2,1)}), bf16[8,32,4096]{2,1,0:T(8,128)(2,1)S(1)}, u32[]{:S(2)}, u32[]{:S(2)}) %all-to-all-start.3) | async-done | bytes 2097184 | tf_op jit(solution)/shard_map/all_to_all | solution.py:69
  202.6 2.1 %convolution_convert_fusion = bf16[4096,256]{1,0:T(8,128)(2,1)} fusion(bf16[256,4096]{1,0:T(8,128)(2,1)S(1)} %bitcast.47, bf16[256,256]{1,0:T(8,128)(2,1)S(1)} %select_n.31), kind=kOutput, calls=%fused_computation | convolution fusion | flops 537919488 | bytes 4325376 | tf_op jit(solution)/shard_map/dot_general | solution.py:71
  (3 shorter events, 0.0 us)
Async XLA Ops:
  1.0 20.9 %copy-start = (bf16[4096,256]{1,0:T(8,128)(2,1)S(1)}, bf16[4096,256]{1,0:T(8,128)(2,1)}, u32[]{:S(2)}) copy-start(bf16[4096,256]{1,0:T(8,128)(2,1)} %param.6) | copy-start | bytes 6291460
  1.0 20.9 %copy-start.3 = (f32[8,512]{1,0:T(8,128)S(1)}, f32[8,512]{1,0:T(8,128)}, u32[]{:S(2)}) copy-start(f32[8,512]{1,0:T(8,128)} %param.8) | copy-start | bytes 49156
  98.7 68.4 %all-to-all-start.2 = ((bf16[512,8,256]{2,1,0:T(8,128)(2,1)}), bf16[512,8,256]{2,1,0:T(8,128)(2,1)S(1)}, u32[]{:S(2)}, u32[]{:S(2)}) async-start(bf16[512,8,256]{2,1,0:T(8,128)(2,1)} %copy.19), calls=%async_computation.2 | async-start | bytes 4194304 | tf_op jit(solution)/shard_map/all_to_all | solution.py:60
  107.8 4.0 %copy-start.1 = (bf16[8,32,32]{2,1,0:T(8,128)(2,1)S(1)}, bf16[8,32,32]{2,1,0:T(8,128)(2,1)}, u32[]{:S(2)}) copy-start(bf16[8,32,32]{2,1,0:T(8,128)(2,1)} %param.10) | copy-start | bytes 49156
  171.9 3.7 %copy-start.2 = (bf16[4,64,64]{2,1,0:T(8,128)(2,1)S(1)}, bf16[4,64,64]{2,1,0:T(8,128)(2,1)}, u32[]{:S(2)}) copy-start(bf16[4,64,64]{2,1,0:T(8,128)(2,1)} %param.11) | copy-start | bytes 98308
  171.9 30.7 %all-to-all-start.3 = ((bf16[8,32,4096]{2,1,0:T(8,128)(2,1)}), bf16[8,32,4096]{2,1,0:T(8,128)(2,1)S(1)}, u32[]{:S(2)}, u32[]{:S(2)}) async-start(bf16[8,32,4096]{2,1,0:T(8,128)(2,1)} %bitcast.48), calls=%async_computation.3 | async-start | bytes 4194304 | tf_op jit(solution)/shard_map/all_to_all | solution.py:69

commit v11 on v6

--- a/solution.py
+++ b/solution.py
@@ -39,6 +39,7 @@
         full_first = both[:, 0].reshape(BLOCK, BLOCK)
         full_second = both[:, 1].reshape(BLOCK, BLOCK)
         twiddle_t = jnp.transpose(twiddle)
+        token_f32 = lax.optimization_barrier(token_grid)
         w1t, w2 = channel_weights(block_first, block_second, n_ch)
         contract = (((1,), (1,)), ((), ()))
         width = BLOCK // CHUNKS
@@ -58,7 +59,7 @@
             ).astype(jnp.bfloat16)
             returned = lax.all_to_all(mixed, "seq", split_axis=0, concat_axis=1, tiled=True)
             gated = (
-                token_grid[:, lo:lo + width].astype(jnp.float32) * returned.astype(jnp.float32)
+                token_f32[:, lo:lo + width].astype(jnp.float32) * returned.astype(jnp.float32)
             ).astype(jnp.bfloat16)
             gated = gated.reshape(outer_rows * width, channels)
             middle_t = lax.dot_general(

time: 206 us -> 205 us (level)
  no operation moved by 1% of the time
where the time goes in v11:
time: 205 us; the launch traced here: 204 us
  blocking collectives  91.1 us (44%)
  waiting for transfers between devices  85.2 us (42%)
  starting transfers between devices  12.9 us (6%)
  matrix products  6.88 us (3%)
  local copies, waits for them, and re-layouts  4.59 us (2%)
  other arithmetic  3.28 us (2%)
    all_to_all x1, blocking collectives, local(): lax.all_to_all(twisted, 'seq', split_axis=0, concat_axis=1, tiled=True)  70.4 us
    all_to_all x1, waiting for transfers between devices, local(): lax.all_to_all(mixed, 'seq', split_axis=0, concat_axis=1, tiled=True)  58.8 us
    all_to_all x1, waiting for transfers between devices, local(): lax.all_to_all(middle_t, 'ch', split_axis=0, concat_axis=0, tiled=True)  26.4 us
    all_to_all x1, blocking collectives, local(): both = lax.all_to_all(spread, 'ch', split_axis=0, concat_axis=0, tiled=True)  20.7 us
    all_to_all x1, starting transfers between devices, local(): lax.all_to_all(mixed, 'seq', split_axis=0, concat_axis=1, tiled=True)  9.17 us
  transfers between devices with their start and end apart: 2, of which 2 were waited for; matrix products, arithmetic and copies ran while one was open for 0% of the time, Pallas kernels for 0%

profile of v11, /device:TPU:41, one launch (start us, length us, event | category | flops | bytes accessed | tf_op | source)
XLA Modules:
  0.0 204.2 jit_solution(6038117477607222569)
XLA Ops:
  0.0 0.9 pad_maximum_fusion
  0.9 0.1 broadcast_in_dim.53
  1.0 0.0 copy-start
  1.0 0.0 copy-start.3
  1.0 20.7 %all_to_all.37 = bf16[8,128,512]{2,1,0:T(8,128)(2,1)S(1)} all-to-all(bf16[8,128,512]{2,1,0:T(8,128)(2,1)S(1)} %broadcast_in_dim.53), channel_id=1, replica_groups=mesh['seq'=64,'ch'=8] {'ch'}, dimensions={0} | all-to-all | bytes 2097152 | tf_op jit(solution)/shard_map/all_to_all | solution.py:37
  21.7 0.1 fusion.7
  21.8 0.0 copy-done
  21.8 0.0 copy-done.3
  21.9 1.5 multiply_convert_fusion
  23.3 1.2 copy.17
  24.5 70.4 %all_to_all.38 = bf16[512,8,256]{2,1,0:T(8,128)(2,1)S(1)} all-to-all(bf16[512,8,256]{2,1,0:T(8,128)(2,1)S(1)} %copy.17), channel_id=1, replica_groups=mesh['seq'=64,'ch'=8] {'seq'}, dimensions={0} | all-to-all | bytes 4194304 | tf_op jit(solution)/shard_map/all_to_all | solution.py:56
  94.9 1.3 fusion.4
  96.2 2.5 %copy.19 = bf16[512,8,256]{2,1,0:T(8,128)(2,1)} copy(bf16[512,8,256]{2,0,1:T(8,128)(2,1)S(1)} %fusion.4) | data formatting | bytes 4194304 | tf_op jit(solution)/shard_map/convert_element_type | solution.py:59
  98.7 0.0 copy-start.1
  98.7 9.2 %all-to-all-start.2 = ((bf16[512,8,256]{2,1,0:T(8,128)(2,1)}), bf16[512,8,256]{2,1,0:T(8,128)(2,1)S(1)}, u32[]{:S(2)}, u32[]{:S(2)}) async-start(bf16[512,8,256]{2,1,0:T(8,128)(2,1)} %copy.19), calls=%async_computation.2 | async-start | bytes 4194304 | tf_op jit(solution)/shard_map/all_to_all | solution.py:60
  107.9 0.0 copy-done.1
  108.0 0.1 broadcast_select_fusion
  108.1 0.4 select_n.29
  108.4 58.8 %all-to-all-done.2 = bf16[512,8,256]{2,1,0:T(8,128)(2,1)S(1)} async-done(((bf16[512,8,256]{2,1,0:T(8,128)(2,1)}), bf16[512,8,256]{2,1,0:T(8,128)(2,1)S(1)}, u32[]{:S(2)}, u32[]{:S(2)}) %all-to-all-start.2) | async-done | bytes 2097184 | tf_op jit(solution)/shard_map/all_to_all | solution.py:60
  167.2 2.1 %fusion = bf16[8,512,256]{2,1,0:T(8,128)(2,1)S(1)} fusion(bf16[8,512,256]{2,1,0:T(8,128)(2,1)} %bitcast.52, bf16[64,8,8,256]{3,2,1,0:T(8,128)(2,1)S(1)} %bitcast.48), kind=kLoop, calls=%fused_computation.4 | loop fusion | flops 4194304 | bytes 6291456 | tf_op jit(solution)/shard_map/convert_element_type | solution.py:63
  169.3 2.1 %convolution_convert_fusion.1 = bf16[256,4096]{1,0:T(8,128)(2,1)} fusion(bf16[256,256]{1,0:T(8,128)(2,1)S(1)} %select_n.29, bf16[4096,256]{1,0:T(8,128)(2,1)S(1)} %bitcast.49), kind=kOutput, calls=%fused_computation.1 | convolution fusion | flops 537919488 | bytes 4325376 | tf_op jit(solution)/shard_map/dot_general | solution.py:65
  171.4 0.0 copy-start.2
  171.4 3.7 %all-to-all-start.3 = ((bf16[8,32,4096]{2,1,0:T(8,128)(2,1)}), bf16[8,32,4096]{2,1,0:T(8,128)(2,1)S(1)}, u32[]{:S(2)}, u32[]{:S(2)}) async-start(bf16[8,32,4096]{2,1,0:T(8,128)(2,1)} %bitcast.50), calls=%async_computation.3 | async-start | bytes 4194304 | tf_op jit(solution)/shard_map/all_to_all | solution.py:69
  175.1 0.0 copy-done.2
  175.1 0.1 copy.21
  175.3 0.2 broadcast_select_fusion.1
  175.5 0.2 select_n.31
  175.7 26.4 %all-to-all-done.3 = bf16[8,32,4096]{2,1,0:T(8,128)(2,1)S(1)} async-done(((bf16[8,32,4096]{2,1,0:T(8,128)(2,1)}), bf16[8,32,4096]{2,1,0:T(8,128)(2,1)S(1)}, u32[]{:S(2)}, u32[]{:S(2)}) %all-to-all-start.3) | async-done | bytes 2097184 | tf_op jit(solution)/shard_map/all_to_all | solution.py:69
  202.1 2.1 %convolution_convert_fusion = bf16[4096,256]{1,0:T(8,128)(2,1)} fusion(bf16[256,4096]{1,0:T(8,128)(2,1)S(1)} %bitcast.47, bf16[256,256]{1,0:T(8,128)(2,1)S(1)} %select_n.31), kind=kOutput, calls=%fused_computation | convolution fusion | flops 537919488 | bytes 4325376 | tf_op jit(solution)/shard_map/dot_general | solution.py:71
  (3 shorter events, 0.0 us)
Async XLA Ops:
  1.0 20.9 %copy-start = (bf16[4096,256]{1,0:T(8,128)(2,1)S(1)}, bf16[4096,256]{1,0:T(8,128)(2,1)}, u32[]{:S(2)}) copy-start(bf16[4096,256]{1,0:T(8,128)(2,1)} %param.6) | copy-start | bytes 6291460
  1.0 20.9 %copy-start.3 = (f32[8,512]{1,0:T(8,128)S(1)}, f32[8,512]{1,0:T(8,128)}, u32[]{:S(2)}) copy-start(f32[8,512]{1,0:T(8,128)} %param.8) | copy-start | bytes 49156
  98.7 9.2 %copy-start.1 = (bf16[8,32,32]{2,1,0:T(8,128)(2,1)S(1)}, bf16[8,32,32]{2,1,0:T(8,128)(2,1)}, u32[]{:S(2)}) copy-start(bf16[8,32,32]{2,1,0:T(8,128)(2,1)} %param.10) | copy-start | bytes 49156
  98.7 68.5 %all-to-all-start.2 = ((bf16[512,8,256]{2,1,0:T(8,128)(2,1)}), bf16[512,8,256]{2,1,0:T(8,128)(2,1)S(1)}, u32[]{:S(2)}, u32[]{:S(2)}) async-start(bf16[512,8,256]{2,1,0:T(8,128)(2,1)} %copy.19), calls=%async_computation.2 | async-start | bytes 4194304 | tf_op jit(solution)/shard_map/all_to_all | solution.py:60
  171.4 3.7 %copy-start.2 = (bf16[4,64,64]{2,1,0:T(8,128)(2,1)S(1)}, bf16[4,64,64]{2,1,0:T(8,128)(2,1)}, u32[]{:S(2)}) copy-start(bf16[4,64,64]{2,1,0:T(8,128)(2,1)} %param.11) | copy-start | bytes 98308
  171.4 30.7 %all-to-all-start.3 = ((bf16[8,32,4096]{2,1,0:T(8,128)(2,1)}), bf16[8,32,4096]{2,1,0:T(8,128)(2,1)S(1)}, u32[]{:S(2)}, u32[]{:S(2)}) async-start(bf16[8,32,4096]{2,1,0:T(8,128)(2,1)} %bitcast.50), calls=%async_computation.3 | async-start | bytes 4194304 | tf_op jit(solution)/shard_map/all_to_all | solution.py:69

commit v12 on v11

--- a/solution.py
+++ b/solution.py
@@ -53,6 +53,7 @@
                 preferred_element_type=jnp.float32,
             )
             twisted = (first * twiddle_t[lo:lo + width, :, None]).astype(jnp.bfloat16)
+            twisted, w1t, w2 = lax.optimization_barrier((twisted, w1t, w2))
             gathered = lax.all_to_all(twisted, "seq", split_axis=0, concat_axis=1, tiled=True)
             mixed = lax.dot_general(
                 full_second, gathered, contract, preferred_element_type=jnp.float32

time: 205 us -> 203 us (level)
  waiting for transfers between devices: 85.2 us -> 62.2 us
  blocking collectives: 91.1 us -> 108 us
  local copies, waits for them, and re-layouts: 4.59 us -> 7.24 us
    all_to_all x1, waiting for transfers between devices: 26.4 us -> 10.1 us  [local(): both = lax.all_to_all(spread, 'ch', split_axis=0, concat_axis=0, tiled=True)]
    all_to_all x1, blocking collectives: 20.7 us -> 33.5 us  [local(): lax.all_to_all(middle_t, 'ch', split_axis=0, concat_axis=0, tiled=True)]
    all_to_all x1, waiting for transfers between devices: 58.8 us -> 52.2 us  [local(): lax.all_to_all(mixed, 'seq', split_axis=0, concat_axis=1, tiled=True)]
    all_to_all x1, blocking collectives: 70.4 us -> 74.3 us  [local(): lax.all_to_all(twisted, 'seq', split_axis=0, concat_axis=1, tiled=True)]
    all_to_all x1, starting transfers between devices: 3.74 us -> 5.83 us  [local(): both = lax.all_to_all(spread, 'ch', split_axis=0, concat_axis=0, tiled=True)]
  transfers between devices with their start and end apart: 2 -> 2, of which waited for: 2 -> 2; matrix products, arithmetic and copies ran while one was open for 0% -> 2% of each run, Pallas kernels for 0% -> 0%
where the time goes in v12:
time: 203 us
  blocking collectives  108 us (53%)
  waiting for transfers between devices  62.2 us (31%)
  starting transfers between devices  14.5 us (7%)
  local copies, waits for them, and re-layouts  7.24 us (4%)
  matrix products  5.56 us (3%)
  other arithmetic  5.05 us (2%)
    all_to_all x1, blocking collectives, local(): lax.all_to_all(twisted, 'seq', split_axis=0, concat_axis=1, tiled=True)  74.3 us
    all_to_all x1, waiting for transfers between devices, local(): lax.all_to_all(mixed, 'seq', split_axis=0, concat_axis=1, tiled=True)  52.2 us
    all_to_all x1, blocking collectives, local(): lax.all_to_all(middle_t, 'ch', split_axis=0, concat_axis=0, tiled=True)  33.5 us
    all_to_all x1, waiting for transfers between devices, local(): both = lax.all_to_all(spread, 'ch', split_axis=0, concat_axis=0, tiled=True)  10.1 us
    all_to_all x1, starting transfers between devices, local(): lax.all_to_all(mixed, 'seq', split_axis=0, concat_axis=1, tiled=True)  8.66 us
    all_to_all x1, starting transfers between devices, local(): both = lax.all_to_all(spread, 'ch', split_axis=0, concat_axis=0, tiled=True)  5.83 us
  transfers between devices with their start and end apart: 2, of which 2 were waited for; matrix products, arithmetic and copies ran while one was open for 2% of the time, Pallas kernels for 0%

profile of v12, /device:TPU:41, one launch (start us, length us, event | category | flops | bytes accessed | tf_op | source)
XLA Modules:
  0.0 202.5 jit_solution(12817067652406120706)
XLA Ops:
  0.0 0.0 copy-start.1
  0.0 0.0 copy-start.2
  0.0 0.9 pad_maximum_fusion
  0.9 1.1 broadcast_in_dim.49
  2.0 5.8 %all-to-all-start = ((bf16[8,128,512]{2,1,0:T(8,128)(2,1)}), bf16[8,128,512]{2,1,0:T(8,128)(2,1)S(1)}, u32[]{:S(2)}, u32[]{:S(2)}) async-start(bf16[8,128,512]{2,1,0:T(8,128)(2,1)} %broadcast_in_dim.49), calls=%async_computation | async-start | bytes 2097152 | tf_op jit(solution)/shard_map/all_to_all | solution.py:37
  7.8 0.0 copy-done.1
  7.8 0.6 copy.16
  8.5 0.0 copy-done.2
  8.5 0.0 copy-start
  8.5 0.0 copy-start.3
  8.5 0.1 copy.17
  8.6 0.2 broadcast_select_fusion.1
  8.8 0.2 select_n.19
  9.0 1.8 broadcast_select_fusion
  10.9 1.4 select_n.17
  12.3 10.1 %all-to-all-done = bf16[8,128,512]{2,1,0:T(8,128)(2,1)S(1)} async-done(((bf16[8,128,512]{2,1,0:T(8,128)(2,1)}), bf16[8,128,512]{2,1,0:T(8,128)(2,1)S(1)}, u32[]{:S(2)}, u32[]{:S(2)}) %all-to-all-start) | async-done | bytes 1048608 | tf_op jit(solution)/shard_map/all_to_all | solution.py:37
  22.4 0.1 fusion.7
  22.5 0.0 copy-done
  22.5 0.0 copy-done.3
  22.5 1.5 multiply_convert_fusion
  24.0 1.2 copy.19
  25.2 74.3 %all_to_all.37 = bf16[512,8,256]{2,1,0:T(8,128)(2,1)S(1)} all-to-all(bf16[512,8,256]{2,1,0:T(8,128)(2,1)S(1)} %copy.19), channel_id=1, replica_groups=mesh['seq'=64,'ch'=8] {'seq'}, dimensions={0} | all-to-all | bytes 4194304 | tf_op jit(solution)/shard_map/all_to_all | solution.py:57
  99.5 1.3 fusion.4
  100.7 2.5 %copy.21 = bf16[512,8,256]{2,1,0:T(8,128)(2,1)} copy(bf16[512,8,256]{2,0,1:T(8,128)(2,1)S(1)} %fusion.4) | data formatting | bytes 4194304 | tf_op jit(solution)/shard_map/convert_element_type | solution.py:60
  103.2 8.7 %all-to-all-start.2 = ((bf16[512,8,256]{2,1,0:T(8,128)(2,1)}), bf16[512,8,256]{2,1,0:T(8,128)(2,1)S(1)}, u32[]{:S(2)}, u32[]{:S(2)}) async-start(bf16[512,8,256]{2,1,0:T(8,128)(2,1)} %copy.21), calls=%async_computation.2 | async-start | bytes 4194304 | tf_op jit(solution)/shard_map/all_to_all | solution.py:61
  111.9 52.2 %all-to-all-done.2 = bf16[512,8,256]{2,1,0:T(8,128)(2,1)S(1)} async-done(((bf16[512,8,256]{2,1,0:T(8,128)(2,1)}), bf16[512,8,256]{2,1,0:T(8,128)(2,1)S(1)}, u32[]{:S(2)}, u32[]{:S(2)}) %all-to-all-start.2) | async-done | bytes 2097184 | tf_op jit(solution)/shard_map/all_to_all | solution.py:61
  164.1 2.1 %fusion = bf16[8,512,256]{2,1,0:T(8,128)(2,1)S(1)} fusion(bf16[8,512,256]{2,1,0:T(8,128)(2,1)} %bitcast.52, bf16[64,8,8,256]{3,2,1,0:T(8,128)(2,1)S(1)} %bitcast.48), kind=kLoop, calls=%fused_computation.4 | loop fusion | flops 4194304 | bytes 6291456 | tf_op jit(solution)/shard_map/convert_element_type | solution.py:64
  166.2 0.7 convolution_convert_fusion.1
  166.9 33.5 %all_to_all.38 = bf16[8,32,4096]{2,1,0:T(8,128)(2,1)S(1)} all-to-all(bf16[8,32,4096]{2,1,0:T(8,128)(2,1)S(1)} %bitcast.50), channel_id=1, replica_groups=mesh['seq'=64,'ch'=8] {'ch'}, dimensions={0} | all-to-all | bytes 4194304 | tf_op jit(solution)/shard_map/all_to_all | solution.py:70
  200.5 2.1 %convolution_convert_fusion = bf16[4096,256]{1,0:T(8,128)(2,1)} fusion(bf16[256,4096]{1,0:T(8,128)(2,1)S(1)} %bitcast.47, bf16[256,256]{1,0:T(8,128)(2,1)S(1)} %select_n.19), kind=kOutput, calls=%fused_computation | convolution fusion | flops 537919488 | bytes 4325376 | tf_op jit(solution)/shard_map/dot_general | solution.py:72
  (2 shorter events, 0.0 us)
Async XLA Ops:
  0.0 7.8 %copy-start.1 = (bf16[8,32,32]{2,1,0:T(8,128)(2,1)S(1)}, bf16[8,32,32]{2,1,0:T(8,128)(2,1)}, u32[]{:S(2)}) copy-start(bf16[8,32,32]{2,1,0:T(8,128)(2,1)} %param.10) | copy-start | bytes 49156
  0.0 8.5 %copy-start.2 = (bf16[4,64,64]{2,1,0:T(8,128)(2,1)S(1)}, bf16[4,64,64]{2,1,0:T(8,128)(2,1)}, u32[]{:S(2)}) copy-start(bf16[4,64,64]{2,1,0:T(8,128)(2,1)} %param.11) | copy-start | bytes 98308
  2.0 20.4 %all-to-all-start = ((bf16[8,128,512]{2,1,0:T(8,128)(2,1)}), bf16[8,128,512]{2,1,0:T(8,128)(2,1)S(1)}, u32[]{:S(2)}, u32[]{:S(2)}) async-start(bf16[8,128,512]{2,1,0:T(8,128)(2,1)} %broadcast_in_dim.49), calls=%async_computation | async-start | bytes 2097152 | tf_op jit(solution)/shard_map/all_to_all | solution.py:37
  8.5 14.0 %copy-start = (bf16[4096,256]{1,0:T(8,128)(2,1)S(1)}, bf16[4096,256]{1,0:T(8,128)(2,1)}, u32[]{:S(2)}) copy-start(bf16[4096,256]{1,0:T(8,128)(2,1)} %param.6) | copy-start | bytes 6291460
  8.5 14.0 %copy-start.3 = (f32[8,512]{1,0:T(8,128)S(1)}, f32[8,512]{1,0:T(8,128)}, u32[]{:S(2)}) copy-start(f32[8,512]{1,0:T(8,128)} %param.8) | copy-start | bytes 49156
  103.2 60.8 %all-to-all-start.2 = ((bf16[512,8,256]{2,1,0:T(8,128)(2,1)}), bf16[512,8,256]{2,1,0:T(8,128)(2,1)S(1)}, u32[]{:S(2)}, u32[]{:S(2)}) async-start(bf16[512,8,256]{2,1,0:T(8,128)(2,1)} %copy.21), calls=%async_computation.2 | async-start | bytes 4194304 | tf_op jit(solution)/shard_map/all_to_all | solution.py:61
